TPU v7x, 32 devices: a whole 2x2x4 slice. The times are simulated.
32 devices in a mesh: region: 8 (over y, x, core), dom: 4 (over z).
Axes of the slice: x: 2, y: 2, z: 4, core: 2. Of those that a mesh axis runs over, the one named last changes fastest.
Arguments:
- feats: bfloat16 [16384, 512], P(('region', 'dom')), may hold values from -6 to 6
- hub_feats: bfloat16 [64, 512], P('region'), may hold values from -6 to 6
- hub_ids: int32 [16384, 4], P(('region', 'dom')), may hold values from 0 to 63
- tile_src: int32 [512], P(('region', 'dom')), may hold values from 0 to 4
- tile_mask: int32 [512, 128, 128], P(('region', 'dom')), may hold values 0 or 1
- w_stack: bfloat16 [1024, 512], replicated, may hold values from -0.1875 to 0.1875
- cotangent: bfloat16 [16384, 512], P(('region', 'dom')), may hold values from -6 to 6
Outputs:
- activ: bfloat16 [16384, 512], P(('region', 'dom'))
- weight_grad: float32 [1024, 512], P('dom')
- hub_grad: float32 [64, 512], P('region')
Inputs may be any that keep to these rules, and one draw needn't show every extreme that they name: tile_src names a block of the part's window: 0 is the block taken from the previous part, 1 to 4 are the part's own blocks. `hub_ids`: hub ids index rows of hub_feats.
All inputs are finite; a program needn't handle non-finite values. No bound on the sum of `tile_mask` on one device may be relied on, other than what follows from the above.
Results may differ from a plain program's by a relative error of at most 0.0051.
Values may be sent and summed in bfloat16 or wider, within the bound.
No kernel may reach another device: no remote copies, remote signals or barrier semaphores. Data moves between devices by JAX's collectives and lax.ppermute only.
A program may use at most 64 MiB of HBM per device.

v0:
```python
import jax
import jax.numpy as jnp
from jax import lax
from jax.sharding import PartitionSpec as P


def shifted(value, axis, steps):
    count = lax.axis_size(axis)
    initial, last = (max(0, -steps), min(count, count - steps))
    return lax.ppermute(value, axis, [(source, source + steps) for source in range(initial, last)])


def on_device(feats, hub_feats, hub_ids, tile_src, tile_mask, w_stack, cotangent):
    rows, width = feats.shape
    tile = tile_mask.shape[1]
    nblk = rows // tile
    per_block = tile_src.shape[0] // nblk
    hub_count = hub_ids.shape[1]
    owned = hub_feats.shape[0]
    total_hubs = owned * lax.axis_size("region")
    prev = shifted(feats[rows - tile :], "dom", 1)
    window = jnp.concatenate([prev, feats], axis=0).reshape(nblk + 1, tile, width)
    picked = jnp.take(window, tile_src, axis=0)
    mask_b = tile_mask.astype(jnp.bfloat16)
    prod = jnp.einsum("tij,tjd->tid", mask_b, picked, preferred_element_type=jnp.float32)
    nsum = prod.reshape(nblk, per_block, tile, width).sum(axis=1).reshape(rows, width)
    cnt = tile_mask.reshape(nblk, per_block, tile, tile).sum(axis=(1, 3)).reshape(rows)
    deg = 1.0 + cnt.astype(jnp.float32) + jnp.float32(hub_count)
    hub_cols = lax.broadcasted_iota(jnp.int32, (rows, total_hubs), 1)
    counts = jnp.zeros((rows, total_hubs), jnp.float32)
    for slot in range(hub_count):
        counts = counts + (hub_ids[:, slot : slot + 1] == hub_cols).astype(jnp.float32)
    counts = counts.astype(jnp.bfloat16)
    block = counts
    hsum = jnp.dot(
        block,
        lax.all_gather(hub_feats, "region", axis=0, tiled=True),
        preferred_element_type=jnp.float32,
    )
    agg = ((feats.astype(jnp.float32) + nsum + hsum) / deg[:, None]).astype(jnp.bfloat16)
    inputs = jnp.concatenate([feats, agg], axis=1)
    z = jnp.dot(inputs, w_stack, preferred_element_type=jnp.float32)
    sig = jax.nn.sigmoid(z)
    activ = (z * sig).astype(jnp.bfloat16)
    dz = (cotangent.astype(jnp.float32) * sig * (1.0 + z * (1.0 - sig))).astype(jnp.bfloat16)
    partial_w = lax.psum_scatter(
        lax.dot_general(inputs, dz, (((0,), (0,)), ((), ())), preferred_element_type=jnp.float32),
        "dom",
        scatter_dimension=0,
        tiled=True,
    )
    weight_grad = lax.psum(partial_w, "region")
    dagg = lax.dot_general(
        dz, w_stack[width:], (((1,), (1,)), ((), ())), preferred_element_type=jnp.float32
    )
    sgrad = (dagg / deg[:, None]).astype(jnp.bfloat16)
    block = counts
    region_sum = lax.psum_scatter(
        lax.dot_general(block, sgrad, (((0,), (0,)), ((), ())), preferred_element_type=jnp.float32),
        "region",
        scatter_dimension=0,
        tiled=True,
    )
    hub_grad = lax.psum(region_sum, "dom")
    return (activ, weight_grad, hub_grad)


def solution(mesh):
    placed = (
        P(("region", "dom"), None),
        P("region", None),
        P(("region", "dom"), None),
        P(("region", "dom")),
        P(("region", "dom"), None, None),
        P(),
        P(("region", "dom"), None),
    )
    return jax.shard_map(
        on_device,
        mesh=mesh,
        in_specs=placed,
        out_specs=(P(("region", "dom"), None), P("dom", None), P("region", None)),
        check_vma=False,
    )
```

profile of v0, /device:TPU:0, one launch (start us, length us, event | category | flops | bytes accessed | tf_op | source)
XLA Modules:
  0.0 183.3 jit_solution(3585333480241991576)
XLA Ops:
  7.2 0.0 copy-start
  7.2 0.0 copy-start.2
  7.2 0.0 reduce-scatter.3.cloned.1.call-start
  7.2 1.0 slice.18
  8.2 5.0 %collective-permute-start = (bf16[128,512]{1,0:T(8,128)(2,1)S(1)}, bf16[128,512]{1,0:T(8,128)(2,1)S(1)}, u32[]{:S(2)}, u32[]{:S(2)}) collective-permute-start(bf16[128,512]{1,0:T(8,128)(2,1)S(1)} %slice.18), channel_id=1, source_target_pairs={{0,1},{1,2},{2,3},{4,5},{5,6},{6,7},{8,9},{9,10},{10,11},{12,13},{... | collective-permute-start | bytes 393224 | tf_op jit(solution)/shard_map/ppermute | solution.py:10
  13.2 1.6 reduce_sum.26
  14.8 0.9 fusion.19
  15.6 0.7 compare_select_fusion
  16.3 0.7 compare_and_fusion
  17.0 1.3 copy.23
  18.2 0.0 copy-done.2
  18.2 9.3 %all_gather.3 = bf16[64,512]{1,0:T(8,128)(2,1)S(1)} all-gather(bf16[8,512]{1,0:T(8,128)(2,1)S(1)} %copy-done.2), channel_id=1, replica_groups=mesh['region'=8,'dom'=4] {'region'}, dimensions={0}, use_global_device_ids=true | all-gather | bytes 73728 | tf_op jit(solution)/shard_map/all_gather | solution.py:37
  27.5 0.0 collective-permute-done
  27.5 0.0 copy-done
  27.6 0.0 copy-start.1
  27.6 2.0 %gather_fusion = bf16[16,128,512]{2,1,0:T(8,128)(2,1)} fusion(bf16[5,128,512]{2,1,0:T(8,128)(2,1)S(1)} %bitcast.23, s32[1024]{0:T(1024)S(1)} %pad_clamp_fusion), kind=kCustom, calls=%fused_computation | custom fusion | bytes 4194368 | tf_op jit(solution)/shard_map/jit(_take)/gather | solution.py:23
  29.6 0.0 copy-done.1
  29.6 2.6 %bitcast_reduce_fusion = f32[4,128,512]{1,2,0:T(8,128)S(1)} fusion(bf16[16,128,512]{2,1,0:T(8,128)(2,1)} %gather_fusion, pred[16]{0:T(512)(128)(4,1)S(1)} %compare_and_fusion, s32[16,128,128]{2,1,0:T(8,128)S(1)} %copy-done.1), kind=kOutput, calls=%fused_computation.1 | convolution fusion | flops 270532608 | bytes 4194320 | tf_op jit(solution)/shard_map/tij,tjd->tid/dot_general | solution.py:25
  32.2 0.0 copy-start.3
  32.2 0.0 copy-start.4
  32.2 1.0 fusion.6
  33.2 0.2 copy-done.3
  33.4 0.1 copy-done.4
  33.6 1.9 %multiply_convert_fusion = (bf16[512,512]{1,0:T(8,128)(2,1)S(1)}, bf16[512,512]{1,0:T(8,128)(2,1)}) fusion(bf16[512,512]{1,0:T(8,128)(2,1)S(1)} %copy-done.4, bf16[1024,512]{1,0:T(8,128)(2,1)S(1)} %copy-done.3, bf16[512,512]{0,1:T(8,128)(2,1)S(1)} %fusion.6, bf16[512,512]{0,1:T(8,128)(2,1)S(1)} %copy.23), kind=kOutput, calls=%fused_computation.13 | convolution fusion | flops 542113792 | bytes 3670016 | tf_op jit(solution)/shard_map/dot_general | solution.py:42
  35.5 2.1 %fusion.10 = f32[1024,512]{1,0:T(8,128)} fusion(bf16[512,512]{1,0:T(8,128)(2,1)S(1)} %get-tuple-element.3, bf16[512,512]{0,1:T(8,128)(2,1)S(1)} %fusion.6, bf16[512,512]{0,1:T(8,128)(2,1)S(1)} %copy.23), kind=kOutput, calls=%fused_computation.17 | convolution fusion | flops 538968064 | bytes 3670016 | tf_op jit(solution)/shard_map/dot_general | solution.py:47
  37.5 0.0 reduce-scatter.3.cloned.1.call-update
  37.6 0.0 reduce-scatter.5.cloned.1.call-start
  37.6 1.3 fusion.8
  39.0 0.0 reduce-scatter.5.cloned.1.call-update
  39.0 0.0 all-reduce.2.cloned.1.call-start
  39.0 41.6 %reduce-scatter.3.cloned.1.call-done = f32[256,512]{1,0:T(8,128)} async-done(((f32[1024,512]{1,0:T(8,128)}), f32[256,512]{1,0:T(8,128)}) %reduce-scatter.3.cloned.1.call-update) | async-done | bytes 524304 | tf_op jit(solution)/shard_map/reduce_scatter | solution.py:46
  80.6 0.0 all-reduce.2.cloned.1.call-update
  80.7 36.3 %reduce-scatter.5.cloned.1.call-done = f32[8,512]{1,0:T(8,128)} async-done(((f32[64,512]{1,0:T(8,128)}), f32[8,512]{1,0:T(8,128)}) %reduce-scatter.5.cloned.1.call-update) | async-done | bytes 16400 | tf_op jit(solution)/shard_map/reduce_scatter | solution.py:58
  117.0 19.9 %psum.15 = f32[8,512]{1,0:T(8,128)} all-reduce(f32[8,512]{1,0:T(8,128)} %reduce-scatter.5.cloned.1.call-done), channel_id=1, replica_groups=mesh['region'=8,'dom'=4] {'dom'}, use_global_device_ids=true, to_apply=%region_6.7 | all-reduce | flops 4096 | bytes 32768 | tf_op jit(solution)/shard_map/psum | solution.py:64
  136.9 38.0 %all-reduce.2.cloned.1.call-done = f32[256,512]{1,0:T(8,128)} async-done(((f32[256,512]{1,0:T(8,128)}), f32[256,512]{1,0:T(8,128)}) %all-reduce.2.cloned.1.call-update) | async-done | bytes 524304 | tf_op jit(solution)/shard_map/psum | solution.py:52
  174.9 1.9 %copy.30 = f32[256,512]{1,0:T(8,128)} copy(f32[256,512]{1,0:T(8,128)} %all-reduce.2.cloned.1.call-done) | data formatting | bytes 1048576
  (4 shorter events, 0.1 us)
Async XLA Ops:
  7.2 20.3 %copy-start = (bf16[512,512]{1,0:T(8,128)(2,1)S(1)}, bf16[512,512]{1,0:T(8,128)(2,1)}, u32[]{:S(2)}) copy-start(bf16[512,512]{1,0:T(8,128)(2,1)} %param.7) | copy-start | bytes 1572868
  7.2 11.0 %copy-start.2 = (bf16[8,512]{1,0:T(8,128)(2,1)S(1)}, bf16[8,512]{1,0:T(8,128)(2,1)}, u32[]{:S(2)}) copy-start(bf16[8,512]{1,0:T(8,128)(2,1)} %param.8) | copy-start | bytes 24580
  7.2 73.4 %reduce-scatter.3.cloned.1.call-start = ((), (), s32[]{:S(2)}) async-start(), calls=%async_computation.2 | async-start | bytes 2621440 | tf_op jit(solution)/shard_map/reduce_scatter | solution.py:46
  8.2 19.3 %collective-permute-start = (bf16[128,512]{1,0:T(8,128)(2,1)S(1)}, bf16[128,512]{1,0:T(8,128)(2,1)S(1)}, u32[]{:S(2)}, u32[]{:S(2)}) collective-permute-start(bf16[128,512]{1,0:T(8,128)(2,1)S(1)} %slice.18), channel_id=1, source_target_pairs={{0,1},{1,2},{2,3},{4,5},{5,6},{6,7},{8,9},{9,10},{10,11},{12,13},{... | collective-permute-start | bytes 393224 | tf_op jit(solution)/shard_map/ppermute | solution.py:10
  27.6 2.0 %copy-start.1 = (s32[16,128,128]{2,1,0:T(8,128)S(1)}, s32[16,128,128]{2,1,0:T(8,128)}, u32[]{:S(2)}) copy-start(s32[16,128,128]{2,1,0:T(8,128)} %param.11) | copy-start | bytes 3145732
  32.2 1.2 copy-start.3
  32.2 1.3 copy-start.4
  37.6 79.4 %reduce-scatter.5.cloned.1.call-start = ((), (), s32[]{:S(2)}) async-start(), calls=%async_computation.4 | async-start | bytes 147456 | tf_op jit(solution)/shard_map/reduce_scatter | solution.py:58
  39.0 135.9 %all-reduce.2.cloned.1.call-start = ((), (), s32[]{:S(2)}) async-start(), calls=%async_computation.3 | async-start | bytes 1048576 | tf_op jit(solution)/shard_map/psum | solution.py:52
Sparse Core Ops, SparseCore 0:
  37.7 42.8 reduce-scatter.2
  84.2 32.7 reduce-scatter.4
  120.1 54.7 all-reduce.1
where the time goes:
time: 184 us; the launch traced here: 183 us
  waiting for transfers between devices  116 us (63%)
  blocking collectives  29.2 us (16%)
  between operations  13.9 us (8%)
  matrix products  8.9 us (5%)
  local copies, waits for them, and re-layouts  7.35 us (4%)
  starting transfers between devices  5.08 us (3%)
  other arithmetic  2.97 us (2%)
    reduce_scatter x1, waiting for transfers between devices, on_device(): lax.psum_scatter(lax.dot_general(inputs, dz, (((0,), (0,)), ((), ())), pr...  41.6 us
    psum x1, waiting for transfers between devices, on_device(): weight_grad = lax.psum(partial_w, 'region')  38 us
    reduce_scatter x1, waiting for transfers between devices, on_device(): lax.psum_scatter(lax.dot_general(block, sgrad, (((0,), (0,)), ((), ())),...  36.3 us
    psum x1, blocking collectives, on_device(): hub_grad = lax.psum(region_sum, 'dom')  19.9 us
    all_gather x1, blocking collectives, on_device(): lax.all_gather(hub_feats, 'region', axis=0, tiled=True)  9.26 us
    ppermute x1, starting transfers between devices, shifted(): lax.ppermute(value, axis, [(source, source + steps) for source in range(i...  4.96 us
  transfers between devices with their start and end apart: 4, of which 3 were waited for; matrix products, arithmetic and copies ran while one was open for 3% of the time, Pallas kernels for 0%

commit v1 on v0

--- a/solution.py
+++ b/solution.py
@@ -10,6 +10,58 @@
     return lax.ppermute(value, axis, [(source, source + steps) for source in range(initial, last)])
 
 
+def log2(n):
+    bits = n.bit_length() - 1
+    assert (1 << bits) == n
+    return bits
+
+
+def swap(value, axis, bit):
+    count = lax.axis_size(axis)
+    return lax.ppermute(value, axis, [(i, i ^ (1 << bit)) for i in range(count)])
+
+
+def scatter_sum(value, axis, at, order):
+    count = lax.axis_size(axis)
+    levels = log2(count)
+    me = lax.axis_index(axis)
+    shape = value.shape
+    value = value.reshape(shape[:at] + (2,) * levels + shape[at + 1 :])
+    held = [levels - 1 - k for k in range(levels)]
+    for bit in order:
+        dim = at + held.index(bit)
+        mine = (me >> bit) & 1
+        keep = lax.dynamic_index_in_dim(value, mine, axis=dim, keepdims=False)
+        send = lax.dynamic_index_in_dim(value, 1 - mine, axis=dim, keepdims=False)
+        value = keep + swap(send, axis, bit)
+        held.remove(bit)
+    return value
+
+
+def gather_ordered(value, axis, order):
+    count = lax.axis_size(axis)
+    levels = log2(count)
+    me = lax.axis_index(axis)
+    rest = value.shape
+    held = []
+    for bit in order:
+        other = swap(value, axis, bit)
+        mine = ((me >> bit) & 1) == 0
+        low = jnp.where(mine, value, other)
+        high = jnp.where(mine, other, value)
+        value = jnp.stack([low, high], axis=0)
+        held.insert(0, bit)
+    natural = [held.index(levels - 1 - k) for k in range(levels)]
+    value = jnp.transpose(value, natural + list(range(levels, levels + len(rest))))
+    return value.reshape((count,) + rest)
+
+
+def sum_all(value, axis):
+    for bit in range(log2(lax.axis_size(axis))):
+        value = value + swap(value, axis, bit)
+    return value
+
+
 def on_device(feats, hub_feats, hub_ids, tile_src, tile_mask, w_stack, cotangent):
     rows, width = feats.shape
     tile = tile_mask.shape[1]
@@ -17,8 +69,13 @@
     per_block = tile_src.shape[0] // nblk
     hub_count = hub_ids.shape[1]
     owned = hub_feats.shape[0]
-    total_hubs = owned * lax.axis_size("region")
+    regions = lax.axis_size("region")
+    doms = lax.axis_size("dom")
+    total_hubs = owned * regions
+    up = list(range(log2(regions)))
+    down = up[::-1]
     prev = shifted(feats[rows - tile :], "dom", 1)
+    hub_table = gather_ordered(hub_feats, "region", down).reshape(total_hubs, width)
     window = jnp.concatenate([prev, feats], axis=0).reshape(nblk + 1, tile, width)
     picked = jnp.take(window, tile_src, axis=0)
     mask_b = tile_mask.astype(jnp.bfloat16)
@@ -31,37 +88,26 @@
     for slot in range(hub_count):
         counts = counts + (hub_ids[:, slot : slot + 1] == hub_cols).astype(jnp.float32)
     counts = counts.astype(jnp.bfloat16)
-    block = counts
-    hsum = jnp.dot(
-        block,
-        lax.all_gather(hub_feats, "region", axis=0, tiled=True),
-        preferred_element_type=jnp.float32,
-    )
+    hsum = jnp.dot(counts, hub_table, preferred_element_type=jnp.float32)
     agg = ((feats.astype(jnp.float32) + nsum + hsum) / deg[:, None]).astype(jnp.bfloat16)
     inputs = jnp.concatenate([feats, agg], axis=1)
     z = jnp.dot(inputs, w_stack, preferred_element_type=jnp.float32)
     sig = jax.nn.sigmoid(z)
     activ = (z * sig).astype(jnp.bfloat16)
     dz = (cotangent.astype(jnp.float32) * sig * (1.0 + z * (1.0 - sig))).astype(jnp.bfloat16)
-    partial_w = lax.psum_scatter(
-        lax.dot_general(inputs, dz, (((0,), (0,)), ((), ())), preferred_element_type=jnp.float32),
-        "dom",
-        scatter_dimension=0,
-        tiled=True,
-    )
-    weight_grad = lax.psum(partial_w, "region")
+    partial_w = lax.dot_general(inputs, dz, (((0,), (0,)), ((), ())), preferred_element_type=jnp.float32)
+    span = partial_w.shape[0] // (doms * regions)
+    partial_w = partial_w.reshape(doms, regions, span, width)
+    region_w = scatter_sum(partial_w, "region", 1, up)
+    piece_w = scatter_sum(region_w, "dom", 0, list(range(log2(doms))))
+    weight_grad = gather_ordered(piece_w, "region", down).reshape(regions * span, width)
     dagg = lax.dot_general(
         dz, w_stack[width:], (((1,), (1,)), ((), ())), preferred_element_type=jnp.float32
     )
     sgrad = (dagg / deg[:, None]).astype(jnp.bfloat16)
-    block = counts
-    region_sum = lax.psum_scatter(
-        lax.dot_general(block, sgrad, (((0,), (0,)), ((), ())), preferred_element_type=jnp.float32),
-        "region",
-        scatter_dimension=0,
-        tiled=True,
-    )
-    hub_grad = lax.psum(region_sum, "dom")
+    partial_h = lax.dot_general(counts, sgrad, (((0,), (0,)), ((), ())), preferred_element_type=jnp.float32)
+    partial_h = partial_h.reshape(regions, owned, width)
+    hub_grad = sum_all(scatter_sum(partial_h, "region", 0, up), "dom")
     return (activ, weight_grad, hub_grad)
 
 

time: 184 us -> 83.2 us (0.45)
  waiting for transfers between devices: 116 us -> 38.8 us
  blocking collectives: 29.2 us -> 0 us
  starting transfers between devices: 5.08 us -> 23.5 us
  between operations: 13.9 us -> 0.97 us
  other arithmetic: 2.97 us -> 6.88 us
  matrix products: 8.9 us -> 6.86 us
    reduce_scatter x2 -> x0, waiting for transfers between devices: 77.9 us -> none  [the longest x1 41.6 us: on_device(): lax.psum_scatter(lax.dot_general(inputs, dz, (((0,), (0,)), ((), ())), pr...]
    ppermute x0 -> x16, waiting for transfers between devices: none -> 38.8 us  [swap(): return lax.ppermute(value, axis, [(i, i ^ 1 << bit) for i in range(count)])]
    psum x1 -> x0, waiting for transfers between devices: 38 us -> none  [on_device(): weight_grad = lax.psum(partial_w, 'region')]
    ppermute x0 -> x16, starting transfers between devices: none -> 20 us  [swap(): return lax.ppermute(value, axis, [(i, i ^ 1 << bit) for i in range(count)])]
    psum x1 -> x0, blocking collectives: 19.9 us -> none  [on_device(): hub_grad = lax.psum(region_sum, 'dom')]
    all_gather x1 -> x0, blocking collectives: 9.26 us -> none  [on_device(): lax.all_gather(hub_feats, 'region', axis=0, tiled=True)]
    add x0 -> x10, other arithmetic: none -> 2.21 us  [the longest x8 1.6 us: scatter_sum(): value = keep + swap(send, axis, bit)]
    unnamed x12 -> x15, local copies, waits for them, and re-layouts: 3.5 us -> 1.64 us
  transfers between devices with their start and end apart: 4 -> 17, of which waited for: 3 -> 11; matrix products, arithmetic and copies ran while one was open for 3% -> 10% of each run, Pallas kernels for 0% -> 0%
where the time goes in v1:
time: 83.2 us; the launch traced here: 82.8 us
  waiting for transfers between devices  38.8 us (47%)
  starting transfers between devices  23.5 us (28%)
  other arithmetic  6.88 us (8%)
  matrix products  6.86 us (8%)
  local copies, waits for them, and re-layouts  5.76 us (7%)
  between operations  0.97 us (1%)
    ppermute x16, waiting for transfers between devices, swap(): return lax.ppermute(value, axis, [(i, i ^ 1 << bit) for i in range(count)])  38.8 us
    ppermute x16, starting transfers between devices, swap(): return lax.ppermute(value, axis, [(i, i ^ 1 << bit) for i in range(count)])  20 us
    ppermute x1, starting transfers between devices, shifted(): lax.ppermute(value, axis, [(source, source + steps) for source in range(i...  3.49 us
    dot_general x1, matrix products, on_device(): jnp.einsum('tij,tjd->tid', mask_b, picked, preferred_element_type=jnp.flo...  2.61 us
    gather x1, local copies, waits for them, and re-layouts, on_device(): picked = jnp.take(window, tile_src, axis=0)  2.02 us
    dot_general x1, matrix products, on_device(): z = jnp.dot(inputs, w_stack, preferred_element_type=jnp.float32)  1.9 us
    another operation x12, other arithmetic, gather_ordered(): value = jnp.stack([low, high], axis=0)  1.7 us
  transfers between devices with their start and end apart: 17, of which 11 were waited for; matrix products, arithmetic and copies ran while one was open for 10% of the time, Pallas kernels for 0%

profile of v1, /device:TPU:0, one launch (start us, length us, event | category | flops | bytes accessed | tf_op | source)
XLA Modules:
  0.0 82.8 jit_solution(18148758109445703200)
XLA Ops:
  0.6 0.0 copy-start
  0.6 3.1 %collective-permute-start.1 = (bf16[8,512]{1,0:T(8,128)(2,1)}, bf16[8,512]{1,0:T(8,128)(2,1)S(1)}, u32[]{:S(2)}, u32[]{:S(2)}) collective-permute-start(bf16[8,512]{1,0:T(8,128)(2,1)} %param.8), channel_id=1, source_target_pairs={{0,16},{4,20},{8,24},{12,28},{16,0},{20,4},{24,8},{28,12},{1,17},{... | collective-permute-start | bytes 24584 | tf_op jit(solution)/shard_map/ppermute | solution.py:21
  3.7 0.9 %slice.18 = bf16[128,512]{1,0:T(8,128)(2,1)S(1)} slice(bf16[512,512]{1,0:T(8,128)(2,1)} %param.7), slice={[384:512], [0:512]} | slice | bytes 262144 | tf_op jit(solution)/shard_map/slice | solution.py:77
  4.6 3.5 %collective-permute-start = (bf16[128,512]{1,0:T(8,128)(2,1)S(1)}, bf16[128,512]{1,0:T(8,128)(2,1)S(1)}, u32[]{:S(2)}, u32[]{:S(2)}) collective-permute-start(bf16[128,512]{1,0:T(8,128)(2,1)S(1)} %slice.18), channel_id=1, source_target_pairs={{0,1},{1,2},{2,3},{4,5},{5,6},{6,7},{8,9},{9,10},{10,11},{12,13},{... | collective-permute-start | bytes 393224 | tf_op jit(solution)/shard_map/ppermute | solution.py:10
  8.1 0.9 %fusion.19 = (s32[512,1]{0,1:T(1,128)S(1)}, s32[512,1]{0,1:T(1,128)S(1)}, s32[512,1]{0,1:T(1,128)S(1)}, s32[512,1]{0,1:T(1,128)S(1)}) fusion(s32[512,4]{0,1:T(4,128)} %param.9), kind=kLoop, calls=%fused_computation.71 | loop fusion | bytes 16384 | tf_op jit(solution)/shard_map/slice | solution.py:89
  9.0 1.6 %reduce_sum.26 = s32[16,128]{1,0:T(8,128)S(1)} reduce(s32[16,128,128]{2,1,0:T(8,128)} %param.11, s32[]{:T(128)} %constant.79.clone.1), dimensions={2}, to_apply=%region_1.2 | reduce | flops 260096 | bytes 1056772 | tf_op jit(solution)/shard_map/reduce_sum | solution.py:84
  10.6 0.7 compare_select_fusion
  11.2 0.0 collective-permute-done.1
  11.2 0.7 select_bitcast_fusion.11
  12.0 1.5 %collective-permute-start.2 = (bf16[2,8,512]{2,1,0:T(8,128)(2,1)S(1)}, bf16[2,8,512]{2,1,0:T(8,128)(2,1)S(1)}, u32[]{:S(2)}, u32[]{:S(2)}) collective-permute-start(bf16[2,8,512]{2,1,0:T(8,128)(2,1)S(1)} %pad_maximum_fusion.9), channel_id=1, source_target_pairs={{0,8},{4,12},{8,0},{12,4},{16,24},{20,28},{24,16},{28,20},{1,9},{5... | collective-permute-start | bytes 49160 | tf_op jit(solution)/shard_map/ppermute | solution.py:21
  13.4 0.7 compare_and_fusion
  14.1 1.6 %collective-permute-done.2 = bf16[2,8,512]{2,1,0:T(8,128)(2,1)S(1)} collective-permute-done((bf16[2,8,512]{2,1,0:T(8,128)(2,1)S(1)}, bf16[2,8,512]{2,1,0:T(8,128)(2,1)S(1)}, u32[]{:S(2)}, u32[]{:S(2)}) %collective-permute-start.2) | collective-permute-done | bytes 16416 | tf_op jit(solution)/shard_map/ppermute | solution.py:21
  15.7 0.1 collective-permute-start.3
  15.8 1.3 %copy.39 = bf16[512,512]{0,1:T(8,128)(2,1)S(1)} copy(bf16[512,512]{1,0:T(8,128)(2,1)} %param.7) | data formatting | bytes 1048576 | tf_op args[0]
  17.1 0.0 collective-permute-done.3
  17.1 0.0 collective-permute-done
  17.1 0.0 copy-done
  17.2 0.0 copy-start.1
  17.2 2.0 %gather_fusion = bf16[16,128,512]{2,1,0:T(8,128)(2,1)} fusion(bf16[5,128,512]{2,1,0:T(8,128)(2,1)S(1)} %bitcast.97, s32[1024]{0:T(1024)S(1)} %pad_clamp_fusion), kind=kCustom, calls=%fused_computation | custom fusion | bytes 4194368 | tf_op jit(solution)/shard_map/jit(_take)/gather | solution.py:80
  19.2 2.6 %bitcast_reduce_fusion = f32[4,128,512]{1,2,0:T(8,128)S(1)} fusion(bf16[16,128,512]{2,1,0:T(8,128)(2,1)} %gather_fusion, pred[16]{0:T(512)(128)(4,1)S(1)} %compare_and_fusion, s32[16,128,128]{2,1,0:T(8,128)S(1)} %copy-done.1), kind=kOutput, calls=%fused_computation.1 | convolution fusion | flops 270532608 | bytes 4194320 | tf_op jit(solution)/shard_map/tij,tjd->tid/dot_general | solution.py:82
  21.8 0.0 copy-start.4
  21.9 0.0 copy-start.6
  21.9 1.0 %fusion.6 = bf16[512,512]{0,1:T(8,128)(2,1)S(1)} fusion(bf16[64,512]{1,0:T(8,128)(2,1)S(1)} %bitcast.106, bf16[512,512]{0,1:T(8,128)(2,1)S(1)} %copy.39, f32[512]{0:T(512)S(1)} %add_bitcast_fusion, s32[512]{0:T(512)S(1)} %bitcast.112, s32[512]{0:T(512)S(1)} %bitcast.114, s32[512]{0:T(512)S(1)} %bitcast.110, s32[512]{0:T(512)S(1)} %bitcast.108, ...), kind=kOutput, calls=%fused_computation.8 | convolution fusion | flops 35258368 | bytes 2172928 | tf_op jit(solution)/shard_map/dot_general | solution.py:91
  22.9 0.2 copy-done.4
  23.1 0.1 copy-done.6
  23.2 1.9 %multiply_convert_fusion = (bf16[512,512]{1,0:T(8,128)(2,1)S(1)}, bf16[512,512]{1,0:T(8,128)(2,1)}) fusion(bf16[512,512]{1,0:T(8,128)(2,1)S(1)} %copy-done.6, bf16[1024,512]{1,0:T(8,128)(2,1)S(1)} %copy-done.4, bf16[512,512]{0,1:T(8,128)(2,1)S(1)} %fusion.6, bf16[512,512]{0,1:T(8,128)(2,1)S(1)} %copy.39), kind=kOutput, calls=%fused_computation.15 | convolution fusion | flops 542113792 | bytes 3670016 | tf_op jit(solution)/shard_map/dot_general | solution.py:94
  25.1 0.7 fusion.10
  25.8 0.1 dynamic-slice_bitcast_fusion
  25.9 0.6 collective-permute-start.4
  26.5 2.4 %collective-permute-done.4 = f32[4,2,2,32,512]{4,3,2,1,0:T(8,128)} collective-permute-done((f32[4,2,2,32,512]{4,3,2,1,0:T(8,128)S(1)}, f32[4,2,2,32,512]{4,3,2,1,0:T(8,128)}, u32[]{:S(2)}, u32[]{:S(2)}) %collective-permute-start.4) | collective-permute-done | bytes 1048608 | tf_op jit(solution)/shard_map/ppermute | solution.py:21
  28.9 1.4 %bitcast_add_fusion.1 = f32[4,2,2,32,512]{4,3,2,1,0:T(8,128)S(1)} fusion(f32[4,2,2,32,512]{4,3,2,1,0:T(8,128)} %collective-permute-done.4, f32[4,2,2,2,32,512]{5,4,3,2,1,0:T(8,128)S(1)} %bitcast.99, s32[]{:T(128)S(6)} %select_n.139), kind=kLoop, calls=%fused_computation.13 | loop fusion | flops 262144 | bytes 3145732 | tf_op jit(solution)/shard_map/add | solution.py:36
  30.3 0.1 constant_dynamic-slice_fusion.1
  30.4 0.0 copy-start.3
  30.4 0.0 copy-start.5
  30.5 1.6 %collective-permute-start.5 = (f32[4,2,32,512]{3,2,0,1:T(8,128)S(1)}, f32[4,2,32,512]{3,2,0,1:T(8,128)S(1)}, u32[]{:S(2)}, u32[]{:S(2)}) collective-permute-start(f32[4,2,32,512]{3,2,0,1:T(8,128)S(1)} %bitcast.103), channel_id=1, source_target_pairs={{0,8},{4,12},{8,0},{12,4},{16,24},{20,28},{24,16},{28,20},{1,9},{5... | collective-permute-start | bytes 1572872 | tf_op jit(solution)/shard_map/ppermute | solution.py:21
  32.1 12.7 %collective-permute-done.5 = f32[4,2,32,512]{3,2,0,1:T(8,128)S(1)} collective-permute-done((f32[4,2,32,512]{3,2,0,1:T(8,128)S(1)}, f32[4,2,32,512]{3,2,0,1:T(8,128)S(1)}, u32[]{:S(2)}, u32[]{:S(2)}) %collective-permute-start.5) | collective-permute-done | bytes 524320 | tf_op jit(solution)/shard_map/ppermute | solution.py:21
  44.8 0.1 bitcast_add_fusion.2
  44.9 0.6 collective-permute-start.6
  45.5 7.2 %collective-permute-done.6 = f32[4,32,512]{2,1,0:T(8,128)S(1)} collective-permute-done((f32[4,32,512]{2,1,0:T(8,128)S(1)}, f32[4,32,512]{2,1,0:T(8,128)S(1)}, u32[]{:S(2)}, u32[]{:S(2)}) %collective-permute-start.6) | collective-permute-done | bytes 262176 | tf_op jit(solution)/shard_map/ppermute | solution.py:21
  52.8 1.6 %collective-permute-start.7 = (f32[2,32,512]{2,1,0:T(8,128)S(1)}, f32[2,32,512]{2,1,0:T(8,128)S(1)}, u32[]{:S(2)}, u32[]{:S(2)}) collective-permute-start(f32[2,32,512]{2,1,0:T(8,128)S(1)} %dynamic-slice_bitcast_fusion.2), channel_id=1, source_target_pairs={{0,1},{1,0},{2,3},{3,2},{4,5},{5,4},{6,7},{7,6},{8,9},{9,8},{10,11... | collective-permute-start | bytes 393224 | tf_op jit(solution)/shard_map/ppermute | solution.py:21
  54.4 0.0 copy-done.3
  54.4 0.7 fusion.8
  55.1 0.1 collective-permute-start.12
  55.2 2.6 %collective-permute-done.7 = f32[2,32,512]{2,1,0:T(8,128)S(1)} collective-permute-done((f32[2,32,512]{2,1,0:T(8,128)S(1)}, f32[2,32,512]{2,1,0:T(8,128)S(1)}, u32[]{:S(2)}, u32[]{:S(2)}) %collective-permute-start.7) | collective-permute-done | bytes 131104 | tf_op jit(solution)/shard_map/ppermute | solution.py:21
  57.8 2.6 %collective-permute-start.8 = (f32[32,512]{1,0:T(8,128)S(1)}, f32[32,512]{1,0:T(8,128)S(1)}, u32[]{:S(2)}, u32[]{:S(2)}) collective-permute-start(f32[32,512]{1,0:T(8,128)S(1)} %dynamic-slice_bitcast_fusion.4), channel_id=1, source_target_pairs={{0,2},{1,3},{2,0},{3,1},{4,6},{5,7},{6,4},{7,5},{8,10},{9,11},{10,... | collective-permute-start | bytes 196616 | tf_op jit(solution)/shard_map/ppermute | solution.py:21
  60.5 0.0 collective-permute-done.12
  60.5 2.6 %collective-permute-done.8 = f32[32,512]{1,0:T(8,128)S(1)} collective-permute-done((f32[32,512]{1,0:T(8,128)S(1)}, f32[32,512]{1,0:T(8,128)S(1)}, u32[]{:S(2)}, u32[]{:S(2)}) %collective-permute-start.8) | collective-permute-done | bytes 65568 | tf_op jit(solution)/shard_map/ppermute | solution.py:21
  63.1 0.6 collective-permute-start.9
  63.6 1.5 %collective-permute-start.13 = (f32[2,8,512]{2,1,0:T(8,128)S(1)}, f32[2,8,512]{2,1,0:T(8,128)S(1)}, u32[]{:S(2)}, u32[]{:S(2)}) collective-permute-start(f32[2,8,512]{2,1,0:T(8,128)S(1)} %dynamic-slice_bitcast_fusion.5), channel_id=1, source_target_pairs={{0,8},{4,12},{8,0},{12,4},{16,24},{20,28},{24,16},{28,20},{1,9},{5... | collective-permute-start | bytes 98312 | tf_op jit(solution)/shard_map/ppermute | solution.py:21
  65.1 2.4 %collective-permute-done.9 = f32[32,512]{1,0:T(8,128)S(1)} collective-permute-done((f32[32,512]{1,0:T(8,128)S(1)}, f32[32,512]{1,0:T(8,128)S(1)}, u32[]{:S(2)}, u32[]{:S(2)}) %collective-permute-start.9) | collective-permute-done | bytes 65568 | tf_op jit(solution)/shard_map/ppermute | solution.py:21
  67.6 1.4 %collective-permute-start.10 = (f32[2,32,512]{2,1,0:T(8,128)S(1)}, f32[2,32,512]{2,1,0:T(8,128)S(1)}, u32[]{:S(2)}, u32[]{:S(2)}) collective-permute-start(f32[2,32,512]{2,1,0:T(8,128)S(1)} %pad_maximum_fusion.6), channel_id=1, source_target_pairs={{0,8},{4,12},{8,0},{12,4},{16,24},{20,28},{24,16},{28,20},{1,9},{5... | collective-permute-start | bytes 393224 | tf_op jit(solution)/shard_map/ppermute | solution.py:21
  69.0 0.0 collective-permute-done.13
  69.0 0.6 collective-permute-start.14
  69.7 3.0 %collective-permute-done.10 = f32[2,32,512]{2,1,0:T(8,128)S(1)} collective-permute-done((f32[2,32,512]{2,1,0:T(8,128)S(1)}, f32[2,32,512]{2,1,0:T(8,128)S(1)}, u32[]{:S(2)}, u32[]{:S(2)}) %collective-permute-start.10) | collective-permute-done | bytes 131104 | tf_op jit(solution)/shard_map/ppermute | solution.py:21
  72.7 0.1 collective-permute-start.11
  72.8 0.1 collective-permute-done.14
  72.8 1.6 %collective-permute-start.15 = (f32[8,512]{1,0:T(8,128)S(1)}, f32[8,512]{1,0:T(8,128)S(1)}, u32[]{:S(2)}, u32[]{:S(2)}) collective-permute-start(f32[8,512]{1,0:T(8,128)S(1)} %bitcast_add_fusion.8), channel_id=1, source_target_pairs={{0,1},{1,0},{2,3},{3,2},{4,5},{5,4},{6,7},{7,6},{8,9},{9,8},{10,11... | collective-permute-start | bytes 49160 | tf_op jit(solution)/shard_map/ppermute | solution.py:21
  74.5 2.2 %collective-permute-done.15 = f32[8,512]{1,0:T(8,128)S(1)} collective-permute-done((f32[8,512]{1,0:T(8,128)S(1)}, f32[8,512]{1,0:T(8,128)S(1)}, u32[]{:S(2)}, u32[]{:S(2)}) %collective-permute-start.15) | collective-permute-done | bytes 16416 | tf_op jit(solution)/shard_map/ppermute | solution.py:21
  76.6 2.6 %collective-permute-start.16 = (f32[8,512]{1,0:T(8,128)S(1)}, f32[8,512]{1,0:T(8,128)S(1)}, u32[]{:S(2)}, u32[]{:S(2)}) collective-permute-start(f32[8,512]{1,0:T(8,128)S(1)} %add.150), channel_id=1, source_target_pairs={{0,2},{1,3},{2,0},{3,1},{4,6},{5,7},{6,4},{7,5},{8,10},{9,11},{10,... | collective-permute-start | bytes 49160 | tf_op jit(solution)/shard_map/ppermute | solution.py:21
  79.2 2.1 %collective-permute-done.16 = f32[8,512]{1,0:T(8,128)S(1)} collective-permute-done((f32[8,512]{1,0:T(8,128)S(1)}, f32[8,512]{1,0:T(8,128)S(1)}, u32[]{:S(2)}, u32[]{:S(2)}) %collective-permute-start.16) | collective-permute-done | bytes 16416 | tf_op jit(solution)/shard_map/ppermute | solution.py:21
  81.3 0.6 add.151
  81.9 0.0 collective-permute-done.11
  81.9 0.1 select_bitcast_fusion.1
  81.9 0.8 %pad_maximum_fusion.4 = f32[2,2,2,32,512]{4,3,0,1,2:T(8,128)} fusion(f32[1,2,2,32,512]{4,3,0,1,2:T(8,128)S(1)} %get-tuple-element.8, f32[1,2,2,32,512]{4,3,0,1,2:T(8,128)S(1)} %get-tuple-element.7), kind=kLoop, calls=%fused_computation.22 | loop fusion | flops 131072 | bytes 1048576 | tf_op jit(solution)/shard_map/stack | solution.py:52
  (31 shorter events, 0.4 us)
Async XLA Ops:
  0.6 16.5 %copy-start = (bf16[512,512]{1,0:T(8,128)(2,1)S(1)}, bf16[512,512]{1,0:T(8,128)(2,1)}, u32[]{:S(2)}) copy-start(bf16[512,512]{1,0:T(8,128)(2,1)} %param.7) | copy-start | bytes 1572868
  0.6 10.6 %collective-permute-start.1 = (bf16[8,512]{1,0:T(8,128)(2,1)}, bf16[8,512]{1,0:T(8,128)(2,1)S(1)}, u32[]{:S(2)}, u32[]{:S(2)}) collective-permute-start(bf16[8,512]{1,0:T(8,128)(2,1)} %param.8), channel_id=1, source_target_pairs={{0,16},{4,20},{8,24},{12,28},{16,0},{20,4},{24,8},{28,12},{1,17},{... | collective-permute-start | bytes 24584 | tf_op jit(solution)/shard_map/ppermute | solution.py:21
  4.6 12.5 %collective-permute-start = (bf16[128,512]{1,0:T(8,128)(2,1)S(1)}, bf16[128,512]{1,0:T(8,128)(2,1)S(1)}, u32[]{:S(2)}, u32[]{:S(2)}) collective-permute-start(bf16[128,512]{1,0:T(8,128)(2,1)S(1)} %slice.18), channel_id=1, source_target_pairs={{0,1},{1,2},{2,3},{4,5},{5,6},{6,7},{8,9},{9,10},{10,11},{12,13},{... | collective-permute-start | bytes 393224 | tf_op jit(solution)/shard_map/ppermute | solution.py:10
  12.0 3.7 %collective-permute-start.2 = (bf16[2,8,512]{2,1,0:T(8,128)(2,1)S(1)}, bf16[2,8,512]{2,1,0:T(8,128)(2,1)S(1)}, u32[]{:S(2)}, u32[]{:S(2)}) collective-permute-start(bf16[2,8,512]{2,1,0:T(8,128)(2,1)S(1)} %pad_maximum_fusion.9), channel_id=1, source_target_pairs={{0,8},{4,12},{8,0},{12,4},{16,24},{20,28},{24,16},{28,20},{1,9},{5... | collective-permute-start | bytes 49160 | tf_op jit(solution)/shard_map/ppermute | solution.py:21
  15.7 1.4 %collective-permute-start.3 = (bf16[2,2,8,512]{3,2,0,1:T(8,128)(2,1)S(1)}, bf16[2,2,8,512]{3,2,0,1:T(8,128)(2,1)S(1)}, u32[]{:S(2)}, u32[]{:S(2)}) collective-permute-start(bf16[2,2,8,512]{3,2,0,1:T(8,128)(2,1)S(1)} %pad_maximum_fusion.8), channel_id=1, source_target_pairs={{0,4},{4,0},{8,12},{12,8},{16,20},{20,16},{24,28},{28,24},{1,5},{5... | collective-permute-start | bytes 98312 | tf_op jit(solution)/shard_map/ppermute | solution.py:21
  17.2 2.0 %copy-start.1 = (s32[16,128,128]{2,1,0:T(8,128)S(1)}, s32[16,128,128]{2,1,0:T(8,128)}, u32[]{:S(2)}) copy-start(s32[16,128,128]{2,1,0:T(8,128)} %param.11) | copy-start | bytes 3145732
  21.8 1.2 %copy-start.4 = (bf16[1024,512]{1,0:T(8,128)(2,1)S(1)}, bf16[1024,512]{1,0:T(8,128)(2,1)}, u32[]{:S(2)}) copy-start(bf16[1024,512]{1,0:T(8,128)(2,1)} %param.12) | copy-start | bytes 3145732
  21.9 1.3 %copy-start.6 = (bf16[512,512]{1,0:T(8,128)(2,1)S(1)}, bf16[512,512]{1,0:T(8,128)(2,1)}, u32[]{:S(2)}) copy-start(bf16[512,512]{1,0:T(8,128)(2,1)} %param.13) | copy-start | bytes 1572868
  25.1 0.8 copy-start.2
  25.9 3.0 %collective-permute-start.4 = (f32[4,2,2,32,512]{4,3,2,1,0:T(8,128)S(1)}, f32[4,2,2,32,512]{4,3,2,1,0:T(8,128)}, u32[]{:S(2)}, u32[]{:S(2)}) collective-permute-start(f32[4,2,2,32,512]{4,3,2,1,0:T(8,128)S(1)} %dynamic-slice_bitcast_fusion), channel_id=1, source_target_pairs={{0,4},{4,0},{8,12},{12,8},{16,20},{20,16},{24,28},{28,24},{1,5},{5... | collective-permute-start | bytes 3145736 | tf_op jit(solution)/shard_map/ppermute | solution.py:21
  30.4 24.0 %copy-start.3 = (bf16[512,512]{1,0:T(8,128)(2,1)S(1)}, bf16[512,512]{1,0:T(8,128)(2,1)}, u32[]{:S(2)}) copy-start(bf16[512,512]{1,0:T(8,128)(2,1)} %copy-done.2) | copy-start | bytes 1572868
  30.4 24.0 %copy-start.5 = (bf16[1024,512]{1,0:T(8,128)(2,1)S(1)}, bf16[1024,512]{1,0:T(8,128)(2,1)}, u32[]{:S(2)}) copy-start(bf16[1024,512]{1,0:T(8,128)(2,1)} %param.12) | copy-start | bytes 3145732
  30.5 14.3 %collective-permute-start.5 = (f32[4,2,32,512]{3,2,0,1:T(8,128)S(1)}, f32[4,2,32,512]{3,2,0,1:T(8,128)S(1)}, u32[]{:S(2)}, u32[]{:S(2)}) collective-permute-start(f32[4,2,32,512]{3,2,0,1:T(8,128)S(1)} %bitcast.103), channel_id=1, source_target_pairs={{0,8},{4,12},{8,0},{12,4},{16,24},{20,28},{24,16},{28,20},{1,9},{5... | collective-permute-start | bytes 1572872 | tf_op jit(solution)/shard_map/ppermute | solution.py:21
  44.9 7.8 %collective-permute-start.6 = (f32[4,32,512]{2,1,0:T(8,128)S(1)}, f32[4,32,512]{2,1,0:T(8,128)S(1)}, u32[]{:S(2)}, u32[]{:S(2)}) collective-permute-start(f32[4,32,512]{2,1,0:T(8,128)S(1)} %dynamic-slice_bitcast_fusion.1), channel_id=1, source_target_pairs={{0,16},{4,20},{8,24},{12,28},{16,0},{20,4},{24,8},{28,12},{1,17},{... | collective-permute-start | bytes 786440 | tf_op jit(solution)/shard_map/ppermute | solution.py:21
  52.8 5.0 %collective-permute-start.7 = (f32[2,32,512]{2,1,0:T(8,128)S(1)}, f32[2,32,512]{2,1,0:T(8,128)S(1)}, u32[]{:S(2)}, u32[]{:S(2)}) collective-permute-start(f32[2,32,512]{2,1,0:T(8,128)S(1)} %dynamic-slice_bitcast_fusion.2), channel_id=1, source_target_pairs={{0,1},{1,0},{2,3},{3,2},{4,5},{5,4},{6,7},{7,6},{8,9},{9,8},{10,11... | collective-permute-start | bytes 393224 | tf_op jit(solution)/shard_map/ppermute | solution.py:21
  55.1 5.4 %collective-permute-start.12 = (f32[2,2,8,512]{3,2,1,0:T(8,128)S(1)}, f32[2,2,8,512]{3,2,1,0:T(8,128)S(1)}, u32[]{:S(2)}, u32[]{:S(2)}) collective-permute-start(f32[2,2,8,512]{3,2,1,0:T(8,128)S(1)} %dynamic-slice_bitcast_fusion.3), channel_id=1, source_target_pairs={{0,4},{4,0},{8,12},{12,8},{16,20},{20,16},{24,28},{28,24},{1,5},{5... | collective-permute-start | bytes 196616 | tf_op jit(solution)/shard_map/ppermute | solution.py:21
  57.8 5.2 %collective-permute-start.8 = (f32[32,512]{1,0:T(8,128)S(1)}, f32[32,512]{1,0:T(8,128)S(1)}, u32[]{:S(2)}, u32[]{:S(2)}) collective-permute-start(f32[32,512]{1,0:T(8,128)S(1)} %dynamic-slice_bitcast_fusion.4), channel_id=1, source_target_pairs={{0,2},{1,3},{2,0},{3,1},{4,6},{5,7},{6,4},{7,5},{8,10},{9,11},{10,... | collective-permute-start | bytes 196616 | tf_op jit(solution)/shard_map/ppermute | solution.py:21
  63.1 4.5 %collective-permute-start.9 = (f32[32,512]{1,0:T(8,128)S(1)}, f32[32,512]{1,0:T(8,128)S(1)}, u32[]{:S(2)}, u32[]{:S(2)}) collective-permute-start(f32[32,512]{1,0:T(8,128)S(1)} %bitcast_add_fusion.6), channel_id=1, source_target_pairs={{0,16},{4,20},{8,24},{12,28},{16,0},{20,4},{24,8},{28,12},{1,17},{... | collective-permute-start | bytes 196616 | tf_op jit(solution)/shard_map/ppermute | solution.py:21
  63.6 5.4 %collective-permute-start.13 = (f32[2,8,512]{2,1,0:T(8,128)S(1)}, f32[2,8,512]{2,1,0:T(8,128)S(1)}, u32[]{:S(2)}, u32[]{:S(2)}) collective-permute-start(f32[2,8,512]{2,1,0:T(8,128)S(1)} %dynamic-slice_bitcast_fusion.5), channel_id=1, source_target_pairs={{0,8},{4,12},{8,0},{12,4},{16,24},{20,28},{24,16},{28,20},{1,9},{5... | collective-permute-start | bytes 98312 | tf_op jit(solution)/shard_map/ppermute | solution.py:21
  67.6 5.0 %collective-permute-start.10 = (f32[2,32,512]{2,1,0:T(8,128)S(1)}, f32[2,32,512]{2,1,0:T(8,128)S(1)}, u32[]{:S(2)}, u32[]{:S(2)}) collective-permute-start(f32[2,32,512]{2,1,0:T(8,128)S(1)} %pad_maximum_fusion.6), channel_id=1, source_target_pairs={{0,8},{4,12},{8,0},{12,4},{16,24},{20,28},{24,16},{28,20},{1,9},{5... | collective-permute-start | bytes 393224 | tf_op jit(solution)/shard_map/ppermute | solution.py:21
  69.0 3.8 %collective-permute-start.14 = (f32[8,512]{1,0:T(8,128)S(1)}, f32[8,512]{1,0:T(8,128)S(1)}, u32[]{:S(2)}, u32[]{:S(2)}) collective-permute-start(f32[8,512]{1,0:T(8,128)S(1)} %dynamic-slice_bitcast_fusion.6), channel_id=1, source_target_pairs={{0,16},{4,20},{8,24},{12,28},{16,0},{20,4},{24,8},{28,12},{1,17},{... | collective-permute-start | bytes 49160 | tf_op jit(solution)/shard_map/ppermute | solution.py:21
  72.7 9.2 %collective-permute-start.11 = (f32[2,2,32,512]{3,2,0,1:T(8,128)S(1)}, f32[2,2,32,512]{3,2,0,1:T(8,128)S(1)}, u32[]{:S(2)}, u32[]{:S(2)}) collective-permute-start(f32[2,2,32,512]{3,2,0,1:T(8,128)S(1)} %pad_maximum_fusion.5), channel_id=1, source_target_pairs={{0,4},{4,0},{8,12},{12,8},{16,20},{20,16},{24,28},{28,24},{1,5},{5... | collective-permute-start | bytes 786440 | tf_op jit(solution)/shard_map/ppermute | solution.py:21
  72.8 3.8 %collective-permute-start.15 = (f32[8,512]{1,0:T(8,128)S(1)}, f32[8,512]{1,0:T(8,128)S(1)}, u32[]{:S(2)}, u32[]{:S(2)}) collective-permute-start(f32[8,512]{1,0:T(8,128)S(1)} %bitcast_add_fusion.8), channel_id=1, source_target_pairs={{0,1},{1,0},{2,3},{3,2},{4,5},{5,4},{6,7},{7,6},{8,9},{9,8},{10,11... | collective-permute-start | bytes 49160 | tf_op jit(solution)/shard_map/ppermute | solution.py:21
  76.6 4.6 %collective-permute-start.16 = (f32[8,512]{1,0:T(8,128)S(1)}, f32[8,512]{1,0:T(8,128)S(1)}, u32[]{:S(2)}, u32[]{:S(2)}) collective-permute-start(f32[8,512]{1,0:T(8,128)S(1)} %add.150), channel_id=1, source_target_pairs={{0,2},{1,3},{2,0},{3,1},{4,6},{5,7},{6,4},{7,5},{8,10},{9,11},{10,... | collective-permute-start | bytes 49160 | tf_op jit(solution)/shard_map/ppermute | solution.py:21

commit v2 on v1

--- a/solution.py
+++ b/solution.py
@@ -21,21 +21,40 @@
     return lax.ppermute(value, axis, [(i, i ^ (1 << bit)) for i in range(count)])
 
 
-def scatter_sum(value, axis, at, order):
+def scatter_sum(value, axis, at, order, other=None):
     count = lax.axis_size(axis)
     levels = log2(count)
     me = lax.axis_index(axis)
+    other = order if other is None else other
+    first = (me & 1) == 0
     shape = value.shape
     value = value.reshape(shape[:at] + (2,) * levels + shape[at + 1 :])
-    held = [levels - 1 - k for k in range(levels)]
-    for bit in order:
-        dim = at + held.index(bit)
-        mine = (me >> bit) & 1
-        keep = lax.dynamic_index_in_dim(value, mine, axis=dim, keepdims=False)
-        send = lax.dynamic_index_in_dim(value, 1 - mine, axis=dim, keepdims=False)
-        value = keep + swap(send, axis, bit)
-        held.remove(bit)
+    held = [[levels - 1 - k for k in range(levels)] for _ in range(2)]
+    for bit, bit_b in zip(order, other):
+        parts = []
+        for group, b in enumerate((bit, bit_b)):
+            dim = at + held[group].index(b)
+            mine = (me >> b) & 1
+            keep = lax.dynamic_index_in_dim(value, mine, axis=dim, keepdims=False)
+            send = lax.dynamic_index_in_dim(value, 1 - mine, axis=dim, keepdims=False)
+            parts.append((keep, send))
+            held[group].remove(b)
+        if bit == bit_b:
+            keep, send = parts[0]
+            value = keep + swap(send, axis, bit)
+        else:
+            keep = jnp.where(first, parts[0][0], parts[1][0])
+            send = jnp.where(first, parts[0][1], parts[1][1])
+            pairs = [(i, i ^ (1 << (bit if i & 1 == 0 else bit_b))) for i in range(count)]
+            value = keep + lax.ppermute(send, axis, pairs)
+    assert held[0] == held[1] or levels == 0
     return value
+
+
+def gather_small(value, axis):
+    count = lax.axis_size(axis)
+    spread = jnp.broadcast_to(value[None], (count,) + value.shape)
+    return lax.all_to_all(spread, axis, 0, 0)
 
 
 def gather_ordered(value, axis, order):
@@ -75,7 +94,7 @@
     up = list(range(log2(regions)))
     down = up[::-1]
     prev = shifted(feats[rows - tile :], "dom", 1)
-    hub_table = gather_ordered(hub_feats, "region", down).reshape(total_hubs, width)
+    hub_table = gather_small(hub_feats, "region").reshape(total_hubs, width)
     window = jnp.concatenate([prev, feats], axis=0).reshape(nblk + 1, tile, width)
     picked = jnp.take(window, tile_src, axis=0)
     mask_b = tile_mask.astype(jnp.bfloat16)
@@ -98,7 +117,7 @@
     partial_w = lax.dot_general(inputs, dz, (((0,), (0,)), ((), ())), preferred_element_type=jnp.float32)
     span = partial_w.shape[0] // (doms * regions)
     partial_w = partial_w.reshape(doms, regions, span, width)
-    region_w = scatter_sum(partial_w, "region", 1, up)
+    region_w = scatter_sum(partial_w, "region", 1, up, up[:1] + up[1:][::-1])
     piece_w = scatter_sum(region_w, "dom", 0, list(range(log2(doms))))
     weight_grad = gather_ordered(piece_w, "region", down).reshape(regions * span, width)
     dagg = lax.dot_general(
@@ -107,7 +126,8 @@
     sgrad = (dagg / deg[:, None]).astype(jnp.bfloat16)
     partial_h = lax.dot_general(counts, sgrad, (((0,), (0,)), ((), ())), preferred_element_type=jnp.float32)
     partial_h = partial_h.reshape(regions, owned, width)
-    hub_grad = sum_all(scatter_sum(partial_h, "region", 0, up), "dom")
+    region_h = lax.all_to_all(partial_h, "region", 0, 0).sum(axis=0)
+    hub_grad = gather_small(region_h, "dom").sum(axis=0)
     return (activ, weight_grad, hub_grad)
 
 

time: 83.2 us -> 89.4 us (1.075)
  blocking collectives: 0 us -> 9.57 us
  waiting for transfers between devices: 38.8 us -> 30.9 us
  starting transfers between devices: 23.5 us -> 25.7 us
  matrix products: 6.86 us -> 8.98 us
  local copies, waits for them, and re-layouts: 5.76 us -> 7.64 us
  other arithmetic: 6.88 us -> 5.14 us
    ppermute x16 -> x6, waiting for transfers between devices: 38.8 us -> 13.6 us  [swap(): return lax.ppermute(value, axis, [(i, i ^ 1 << bit) for i in range(count)])]
    ppermute x0 -> x2, waiting for transfers between devices: none -> 11.5 us  [scatter_sum(): value = keep + lax.ppermute(send, axis, pairs)]
    ppermute x16 -> x6, starting transfers between devices: 20 us -> 8.82 us  [swap(): return lax.ppermute(value, axis, [(i, i ^ 1 << bit) for i in range(count)])]
    all_to_all x0 -> x1, blocking collectives: none -> 9.57 us  [on_device(): region_h = lax.all_to_all(partial_h, 'region', 0, 0).sum(axis=0)]
    all_to_all x0 -> x2, starting transfers between devices: none -> 9.2 us  [gather_small(): return lax.all_to_all(spread, axis, 0, 0)]
    all_to_all x0 -> x2, waiting for transfers between devices: none -> 5.75 us  [gather_small(): return lax.all_to_all(spread, axis, 0, 0)]
    ppermute x0 -> x2, starting transfers between devices: none -> 4.17 us  [scatter_sum(): value = keep + lax.ppermute(send, axis, pairs)]
    broadcast_in_dim x0 -> x2, local copies, waits for them, and re-layouts: none -> 2.02 us  [gather_small(): spread = jnp.broadcast_to(value[None], (count,) + value.shape)]
  transfers between devices with their start and end apart: 17 -> 11, of which waited for: 11 -> 8; matrix products, arithmetic and copies ran while one was open for 10% -> 15% of each run, Pallas kernels for 0% -> 0%
where the time goes in v2:
time: 89.4 us; the launch traced here: 88.8 us
  waiting for transfers between devices  30.9 us (35%)
  starting transfers between devices  25.7 us (29%)
  blocking collectives  9.57 us (11%)
  matrix products  8.98 us (10%)
  local copies, waits for them, and re-layouts  7.64 us (9%)
  other arithmetic  5.14 us (6%)
  between operations  0.9 us (1%)
    ppermute x6, waiting for transfers between devices, swap(): return lax.ppermute(value, axis, [(i, i ^ 1 << bit) for i in range(count)])  13.6 us
    ppermute x2, waiting for transfers between devices, scatter_sum(): value = keep + lax.ppermute(send, axis, pairs)  11.5 us
    all_to_all x1, blocking collectives, on_device(): region_h = lax.all_to_all(partial_h, 'region', 0, 0).sum(axis=0)  9.57 us
    all_to_all x2, starting transfers between devices, gather_small(): return lax.all_to_all(spread, axis, 0, 0)  9.2 us
    ppermute x6, starting transfers between devices, swap(): return lax.ppermute(value, axis, [(i, i ^ 1 << bit) for i in range(count)])  8.82 us
    all_to_all x2, waiting for transfers between devices, gather_small(): return lax.all_to_all(spread, axis, 0, 0)  5.75 us
    ppermute x2, starting transfers between devices, scatter_sum(): value = keep + lax.ppermute(send, axis, pairs)  4.17 us
    dot_general x1, matrix products, on_device(): jnp.einsum('tij,tjd->tid', mask_b, picked, preferred_element_type=jnp.flo...  3.59 us
  transfers between devices with their start and end apart: 11, of which 8 were waited for; matrix products, arithmetic and copies ran while one was open for 15% of the time, Pallas kernels for 0%

profile of v2, /device:TPU:0, one launch (start us, length us, event | category | flops | bytes accessed | tf_op | source)
XLA Modules:
  0.0 88.8 jit_solution(6378350188593338451)
XLA Ops:
  0.6 0.0 copy-start
  0.6 1.4 %broadcast_in_dim.29 = bf16[8,8,512]{2,1,0:T(8,128)(2,1)} broadcast(bf16[8,512]{1,0:T(8,128)(2,1)} %param.8), dimensions={1,2} | broadcast | bytes 73728 | tf_op jit(solution)/shard_map/broadcast_in_dim | solution.py:56
  2.0 5.2 %all-to-all-start = ((bf16[8,8,512]{2,1,0:T(8,128)(2,1)}), bf16[8,8,512]{2,1,0:T(8,128)(2,1)S(1)}, u32[]{:S(2)}, u32[]{:S(2)}) async-start(bf16[8,8,512]{2,1,0:T(8,128)(2,1)} %broadcast_in_dim.29), calls=%async_computation | async-start | bytes 131072 | tf_op jit(solution)/shard_map/all_to_all | solution.py:57
  7.2 0.9 %slice.18 = bf16[128,512]{1,0:T(8,128)(2,1)S(1)} slice(bf16[512,512]{1,0:T(8,128)(2,1)} %param.7), slice={[384:512], [0:512]} | slice | bytes 262144 | tf_op jit(solution)/shard_map/slice | solution.py:96
  8.1 3.5 %collective-permute-start = (bf16[128,512]{1,0:T(8,128)(2,1)S(1)}, bf16[128,512]{1,0:T(8,128)(2,1)S(1)}, u32[]{:S(2)}, u32[]{:S(2)}) collective-permute-start(bf16[128,512]{1,0:T(8,128)(2,1)S(1)} %slice.18), channel_id=1, source_target_pairs={{0,1},{1,2},{2,3},{4,5},{5,6},{6,7},{8,9},{9,10},{10,11},{12,13},{... | collective-permute-start | bytes 393224 | tf_op jit(solution)/shard_map/ppermute | solution.py:10
  11.6 0.7 compare_and_fusion
  12.3 1.6 %reduce_sum.44 = s32[16,128]{1,0:T(8,128)S(1)} reduce(s32[16,128,128]{2,1,0:T(8,128)} %param.11, s32[]{:T(128)} %constant.71.clone.1), dimensions={2}, to_apply=%region_1.2 | reduce | flops 260096 | bytes 1056772 | tf_op jit(solution)/shard_map/reduce_sum | solution.py:103
  13.9 0.9 fusion.24
  14.8 0.7 compare_select_fusion
  15.4 1.3 %copy.46 = bf16[512,512]{0,1:T(8,128)(2,1)S(1)} copy(bf16[512,512]{1,0:T(8,128)(2,1)} %param.7) | data formatting | bytes 1048576 | tf_op args[0]
  16.7 0.0 collective-permute-done
  16.7 0.0 copy-done
  16.8 0.0 copy-start.1
  16.8 2.0 %gather_fusion = bf16[16,128,512]{2,1,0:T(8,128)(2,1)} fusion(bf16[5,128,512]{2,1,0:T(8,128)(2,1)S(1)} %bitcast.87, s32[1024]{0:T(1024)S(1)} %pad_clamp_fusion), kind=kCustom, calls=%fused_computation | custom fusion | bytes 4194368 | tf_op jit(solution)/shard_map/jit(_take)/gather | solution.py:99
  18.8 0.0 copy-done.1
  18.8 3.6 %bitcast_reduce_fusion = f32[4,128,512]{1,2,0:T(8,128)} fusion(bf16[16,128,512]{2,1,0:T(8,128)(2,1)} %gather_fusion, pred[16]{0:T(512)(128)(4,1)S(1)} %compare_and_fusion, s32[16,128,128]{2,1,0:T(8,128)S(1)} %copy-done.1), kind=kOutput, calls=%fused_computation.1 | convolution fusion | flops 270532608 | bytes 4194320 | tf_op jit(solution)/shard_map/tij,tjd->tid/dot_general | solution.py:101
  22.4 0.0 all-to-all-done
  22.4 0.0 copy-start.4
  22.4 0.0 copy-start.6
  22.4 2.1 %fusion.6 = bf16[512,512]{0,1:T(8,128)(2,1)S(1)} fusion(bf16[512,512]{0,1:T(8,128)(2,1)S(1)} %copy.46, f32[512]{0:T(512)S(1)} %add_bitcast_fusion, s32[512]{0:T(512)S(1)} %bitcast.98, s32[512]{0:T(512)S(1)} %bitcast.100, s32[512]{0:T(512)S(1)} %bitcast.96, s32[512]{0:T(512)S(1)} %bitcast.94, bf16[8,8,512]{2,1,0:T(8,128)(2,1)S(1)} %all-to-all-done, ...), kind=kOutput, calls=%fused_computation.8 | convolution fusion | flops 35258368 | bytes 2172928 | tf_op jit(solution)/shard_map/dot_general | solution.py:110
  24.5 0.0 copy-done.4
  24.5 0.0 copy-done.6
  24.5 1.9 %multiply_convert_fusion = (bf16[512,512]{1,0:T(8,128)(2,1)S(1)}, bf16[512,512]{1,0:T(8,128)(2,1)}) fusion(bf16[512,512]{1,0:T(8,128)(2,1)S(1)} %copy-done.6, bf16[1024,512]{1,0:T(8,128)(2,1)S(1)} %copy-done.4, bf16[512,512]{0,1:T(8,128)(2,1)S(1)} %fusion.6, bf16[512,512]{0,1:T(8,128)(2,1)S(1)} %copy.46), kind=kOutput, calls=%fused_computation.16 | convolution fusion | flops 542113792 | bytes 3670016 | tf_op jit(solution)/shard_map/dot_general | solution.py:113
  26.4 0.0 copy-start.2
  26.4 0.7 fusion.11
  27.1 0.1 copy-done.2
  27.2 0.2 constant_dynamic-slice_fusion.3
  27.5 0.1 copy.67
  27.6 0.3 collective-permute-start.1
  27.9 2.4 %collective-permute-done.1 = f32[4,2,2,32,512]{4,3,1,0,2:T(8,128)S(1)} collective-permute-done((f32[4,2,2,32,512]{4,3,1,0,2:T(8,128)S(1)}, f32[4,2,2,32,512]{4,3,1,0,2:T(8,128)S(1)}, u32[]{:S(2)}, u32[]{:S(2)}) %collective-permute-start.1) | collective-permute-done | bytes 1048608 | tf_op jit(solution)/shard_map/ppermute | solution.py:21
  30.3 0.2 bitcast_add_fusion.1
  30.6 0.1 constant_dynamic-slice_fusion.1
  30.7 0.1 bitcast_select_fusion
  30.8 2.1 %collective-permute-start.2 = (f32[4,2,32,512]{3,2,1,0:T(8,128)S(1)}, f32[4,2,32,512]{3,2,1,0:T(8,128)S(1)}, u32[]{:S(2)}, u32[]{:S(2)}) collective-permute-start(f32[4,2,32,512]{3,2,1,0:T(8,128)S(1)} %bitcast_select_fusion), channel_id=1, source_target_pairs={{0,8},{4,20},{8,0},{12,28},{16,24},{20,4},{24,16},{28,12},{1,9},{5... | collective-permute-start | bytes 1572872 | tf_op jit(solution)/shard_map/ppermute | solution.py:49
  32.8 7.2 %collective-permute-done.2 = f32[4,2,32,512]{3,2,1,0:T(8,128)S(1)} collective-permute-done((f32[4,2,32,512]{3,2,1,0:T(8,128)S(1)}, f32[4,2,32,512]{3,2,1,0:T(8,128)S(1)}, u32[]{:S(2)}, u32[]{:S(2)}) %collective-permute-start.2) | collective-permute-done | bytes 524320 | tf_op jit(solution)/shard_map/ppermute | solution.py:49
  40.0 0.1 fusion.13
  40.2 0.0 copy-start.3
  40.2 0.0 copy-start.5
  40.2 2.1 %collective-permute-start.3 = (f32[4,32,512]{2,1,0:T(8,128)S(1)}, f32[4,32,512]{2,1,0:T(8,128)S(1)}, u32[]{:S(2)}, u32[]{:S(2)}) collective-permute-start(f32[4,32,512]{2,1,0:T(8,128)S(1)} %select_bitcast_fusion.2), channel_id=1, source_target_pairs={{0,16},{4,12},{8,24},{12,4},{16,0},{20,28},{24,8},{28,20},{1,17},{... | collective-permute-start | bytes 786440 | tf_op jit(solution)/shard_map/ppermute | solution.py:49
  42.3 4.4 %collective-permute-done.3 = f32[4,32,512]{2,1,0:T(8,128)S(1)} collective-permute-done((f32[4,32,512]{2,1,0:T(8,128)S(1)}, f32[4,32,512]{2,1,0:T(8,128)S(1)}, u32[]{:S(2)}, u32[]{:S(2)}) %collective-permute-start.3) | collective-permute-done | bytes 262176 | tf_op jit(solution)/shard_map/ppermute | solution.py:49
  46.7 0.1 fusion.19
  46.8 1.6 %collective-permute-start.4 = (f32[2,32,512]{2,1,0:T(8,128)S(1)}, f32[2,32,512]{2,1,0:T(8,128)S(1)}, u32[]{:S(2)}, u32[]{:S(2)}) collective-permute-start(f32[2,32,512]{2,1,0:T(8,128)S(1)} %dynamic-slice_bitcast_fusion), channel_id=1, source_target_pairs={{0,1},{1,0},{2,3},{3,2},{4,5},{5,4},{6,7},{7,6},{8,9},{9,8},{10,11... | collective-permute-start | bytes 393224 | tf_op jit(solution)/shard_map/ppermute | solution.py:21
  48.4 3.4 %collective-permute-done.4 = f32[2,32,512]{2,1,0:T(8,128)S(1)} collective-permute-done((f32[2,32,512]{2,1,0:T(8,128)S(1)}, f32[2,32,512]{2,1,0:T(8,128)S(1)}, u32[]{:S(2)}, u32[]{:S(2)}) %collective-permute-start.4) | collective-permute-done | bytes 131104 | tf_op jit(solution)/shard_map/ppermute | solution.py:21
  51.8 2.7 %collective-permute-start.5 = (f32[32,512]{1,0:T(8,128)S(1)}, f32[32,512]{1,0:T(8,128)S(1)}, u32[]{:S(2)}, u32[]{:S(2)}) collective-permute-start(f32[32,512]{1,0:T(8,128)S(1)} %dynamic-slice_bitcast_fusion.1), channel_id=1, source_target_pairs={{0,2},{1,3},{2,0},{3,1},{4,6},{5,7},{6,4},{7,5},{8,10},{9,11},{10,... | collective-permute-start | bytes 196616 | tf_op jit(solution)/shard_map/ppermute | solution.py:21
  54.5 2.6 %collective-permute-done.5 = f32[32,512]{1,0:T(8,128)S(1)} collective-permute-done((f32[32,512]{1,0:T(8,128)S(1)}, f32[32,512]{1,0:T(8,128)S(1)}, u32[]{:S(2)}, u32[]{:S(2)}) %collective-permute-start.5) | collective-permute-done | bytes 65568 | tf_op jit(solution)/shard_map/ppermute | solution.py:21
  57.1 2.1 %collective-permute-start.6 = (f32[32,512]{1,0:T(8,128)S(1)}, f32[32,512]{1,0:T(8,128)S(1)}, u32[]{:S(2)}, u32[]{:S(2)}) collective-permute-start(f32[32,512]{1,0:T(8,128)S(1)} %bitcast_add_fusion.3), channel_id=1, source_target_pairs={{0,16},{4,20},{8,24},{12,28},{16,0},{20,4},{24,8},{28,12},{1,17},{... | collective-permute-start | bytes 196616 | tf_op jit(solution)/shard_map/ppermute | solution.py:21
  59.2 2.2 %collective-permute-done.6 = f32[32,512]{1,0:T(8,128)S(1)} collective-permute-done((f32[32,512]{1,0:T(8,128)S(1)}, f32[32,512]{1,0:T(8,128)S(1)}, u32[]{:S(2)}, u32[]{:S(2)}) %collective-permute-start.6) | collective-permute-done | bytes 65568 | tf_op jit(solution)/shard_map/ppermute | solution.py:21
  61.4 2.1 %collective-permute-start.7 = (f32[2,32,512]{2,1,0:T(8,128)S(1)}, f32[2,32,512]{2,1,0:T(8,128)S(1)}, u32[]{:S(2)}, u32[]{:S(2)}) collective-permute-start(f32[2,32,512]{2,1,0:T(8,128)S(1)} %pad_maximum_fusion.6), channel_id=1, source_target_pairs={{0,8},{4,12},{8,0},{12,4},{16,24},{20,28},{24,16},{28,20},{1,9},{5... | collective-permute-start | bytes 393224 | tf_op jit(solution)/shard_map/ppermute | solution.py:21
  63.5 2.9 %collective-permute-done.7 = f32[2,32,512]{2,1,0:T(8,128)S(1)} collective-permute-done((f32[2,32,512]{2,1,0:T(8,128)S(1)}, f32[2,32,512]{2,1,0:T(8,128)S(1)}, u32[]{:S(2)}, u32[]{:S(2)}) %collective-permute-start.7) | collective-permute-done | bytes 131104 | tf_op jit(solution)/shard_map/ppermute | solution.py:21
  66.5 0.1 collective-permute-start.8
  66.6 0.0 copy-done.3
  66.6 0.0 copy-done.5
  66.6 0.7 fusion.9
  67.3 9.6 %all_to_all.15 = f32[8,8,512]{2,1,0:T(8,128)S(1)} all-to-all(f32[8,8,512]{2,1,0:T(8,128)S(1)} %fusion.9), channel_id=1, replica_groups=mesh['region'=8,'dom'=4] {'region'}, dimensions={0} | all-to-all | bytes 262144 | tf_op jit(solution)/shard_map/all_to_all | solution.py:129
  76.9 0.6 broadcast_in_dim.30
  77.5 4.0 %all-to-all-start.2 = ((f32[4,8,512]{2,1,0:T(8,128)}), f32[4,8,512]{2,1,0:T(8,128)S(1)}, u32[]{:S(2)}, u32[]{:S(2)}) async-start(f32[4,8,512]{2,1,0:T(8,128)} %broadcast_in_dim.30), calls=%async_computation.2 | async-start | bytes 131072 | tf_op jit(solution)/shard_map/all_to_all | solution.py:57
  81.5 5.7 %all-to-all-done.2 = f32[4,8,512]{2,1,0:T(8,128)S(1)} async-done(((f32[4,8,512]{2,1,0:T(8,128)}), f32[4,8,512]{2,1,0:T(8,128)S(1)}, u32[]{:S(2)}, u32[]{:S(2)}) %all-to-all-start.2) | async-done | bytes 65568 | tf_op jit(solution)/shard_map/all_to_all | solution.py:57
  87.3 0.6 reduce_sum.48
  87.9 0.0 collective-permute-done.8
  87.9 0.8 pad_maximum_fusion.4
  (15 shorter events, 0.3 us)
Async XLA Ops:
  0.6 16.1 %copy-start = (bf16[512,512]{1,0:T(8,128)(2,1)S(1)}, bf16[512,512]{1,0:T(8,128)(2,1)}, u32[]{:S(2)}) copy-start(bf16[512,512]{1,0:T(8,128)(2,1)} %param.7) | copy-start | bytes 1572868
  2.0 20.4 %all-to-all-start = ((bf16[8,8,512]{2,1,0:T(8,128)(2,1)}), bf16[8,8,512]{2,1,0:T(8,128)(2,1)S(1)}, u32[]{:S(2)}, u32[]{:S(2)}) async-start(bf16[8,8,512]{2,1,0:T(8,128)(2,1)} %broadcast_in_dim.29), calls=%async_computation | async-start | bytes 131072 | tf_op jit(solution)/shard_map/all_to_all | solution.py:57
  8.1 8.6 %collective-permute-start = (bf16[128,512]{1,0:T(8,128)(2,1)S(1)}, bf16[128,512]{1,0:T(8,128)(2,1)S(1)}, u32[]{:S(2)}, u32[]{:S(2)}) collective-permute-start(bf16[128,512]{1,0:T(8,128)(2,1)S(1)} %slice.18), channel_id=1, source_target_pairs={{0,1},{1,2},{2,3},{4,5},{5,6},{6,7},{8,9},{9,10},{10,11},{12,13},{... | collective-permute-start | bytes 393224 | tf_op jit(solution)/shard_map/ppermute | solution.py:10
  16.8 2.0 %copy-start.1 = (s32[16,128,128]{2,1,0:T(8,128)S(1)}, s32[16,128,128]{2,1,0:T(8,128)}, u32[]{:S(2)}) copy-start(s32[16,128,128]{2,1,0:T(8,128)} %param.11) | copy-start | bytes 3145732
  22.4 2.1 %copy-start.4 = (bf16[1024,512]{1,0:T(8,128)(2,1)S(1)}, bf16[1024,512]{1,0:T(8,128)(2,1)}, u32[]{:S(2)}) copy-start(bf16[1024,512]{1,0:T(8,128)(2,1)} %param.12) | copy-start | bytes 3145732
  22.4 2.1 %copy-start.6 = (bf16[512,512]{1,0:T(8,128)(2,1)S(1)}, bf16[512,512]{1,0:T(8,128)(2,1)}, u32[]{:S(2)}) copy-start(bf16[512,512]{1,0:T(8,128)(2,1)} %param.13) | copy-start | bytes 1572868
  26.4 0.8 copy-start.2
  27.6 2.7 %collective-permute-start.1 = (f32[4,2,2,32,512]{4,3,1,0,2:T(8,128)S(1)}, f32[4,2,2,32,512]{4,3,1,0,2:T(8,128)S(1)}, u32[]{:S(2)}, u32[]{:S(2)}) collective-permute-start(f32[4,2,2,32,512]{4,3,1,0,2:T(8,128)S(1)} %bitcast.91), channel_id=1, source_target_pairs={{0,4},{4,0},{8,12},{12,8},{16,20},{20,16},{24,28},{28,24},{1,5},{5... | collective-permute-start | bytes 3145736 | tf_op jit(solution)/shard_map/ppermute | solution.py:21
  30.8 9.3 %collective-permute-start.2 = (f32[4,2,32,512]{3,2,1,0:T(8,128)S(1)}, f32[4,2,32,512]{3,2,1,0:T(8,128)S(1)}, u32[]{:S(2)}, u32[]{:S(2)}) collective-permute-start(f32[4,2,32,512]{3,2,1,0:T(8,128)S(1)} %bitcast_select_fusion), channel_id=1, source_target_pairs={{0,8},{4,20},{8,0},{12,28},{16,24},{20,4},{24,16},{28,12},{1,9},{5... | collective-permute-start | bytes 1572872 | tf_op jit(solution)/shard_map/ppermute | solution.py:49
  40.2 26.5 %copy-start.3 = (bf16[512,512]{1,0:T(8,128)(2,1)S(1)}, bf16[512,512]{1,0:T(8,128)(2,1)}, u32[]{:S(2)}) copy-start(bf16[512,512]{1,0:T(8,128)(2,1)} %copy-done.2) | copy-start | bytes 1572868
  40.2 26.5 %copy-start.5 = (bf16[1024,512]{1,0:T(8,128)(2,1)S(1)}, bf16[1024,512]{1,0:T(8,128)(2,1)}, u32[]{:S(2)}) copy-start(bf16[1024,512]{1,0:T(8,128)(2,1)} %param.12) | copy-start | bytes 3145732
  40.2 6.4 %collective-permute-start.3 = (f32[4,32,512]{2,1,0:T(8,128)S(1)}, f32[4,32,512]{2,1,0:T(8,128)S(1)}, u32[]{:S(2)}, u32[]{:S(2)}) collective-permute-start(f32[4,32,512]{2,1,0:T(8,128)S(1)} %select_bitcast_fusion.2), channel_id=1, source_target_pairs={{0,16},{4,12},{8,24},{12,4},{16,0},{20,28},{24,8},{28,20},{1,17},{... | collective-permute-start | bytes 786440 | tf_op jit(solution)/shard_map/ppermute | solution.py:49
  46.8 5.0 %collective-permute-start.4 = (f32[2,32,512]{2,1,0:T(8,128)S(1)}, f32[2,32,512]{2,1,0:T(8,128)S(1)}, u32[]{:S(2)}, u32[]{:S(2)}) collective-permute-start(f32[2,32,512]{2,1,0:T(8,128)S(1)} %dynamic-slice_bitcast_fusion), channel_id=1, source_target_pairs={{0,1},{1,0},{2,3},{3,2},{4,5},{5,4},{6,7},{7,6},{8,9},{9,8},{10,11... | collective-permute-start | bytes 393224 | tf_op jit(solution)/shard_map/ppermute | solution.py:21
  51.8 5.2 %collective-permute-start.5 = (f32[32,512]{1,0:T(8,128)S(1)}, f32[32,512]{1,0:T(8,128)S(1)}, u32[]{:S(2)}, u32[]{:S(2)}) collective-permute-start(f32[32,512]{1,0:T(8,128)S(1)} %dynamic-slice_bitcast_fusion.1), channel_id=1, source_target_pairs={{0,2},{1,3},{2,0},{3,1},{4,6},{5,7},{6,4},{7,5},{8,10},{9,11},{10,... | collective-permute-start | bytes 196616 | tf_op jit(solution)/shard_map/ppermute | solution.py:21
  57.1 4.3 %collective-permute-start.6 = (f32[32,512]{1,0:T(8,128)S(1)}, f32[32,512]{1,0:T(8,128)S(1)}, u32[]{:S(2)}, u32[]{:S(2)}) collective-permute-start(f32[32,512]{1,0:T(8,128)S(1)} %bitcast_add_fusion.3), channel_id=1, source_target_pairs={{0,16},{4,20},{8,24},{12,28},{16,0},{20,4},{24,8},{28,12},{1,17},{... | collective-permute-start | bytes 196616 | tf_op jit(solution)/shard_map/ppermute | solution.py:21
  61.4 5.0 %collective-permute-start.7 = (f32[2,32,512]{2,1,0:T(8,128)S(1)}, f32[2,32,512]{2,1,0:T(8,128)S(1)}, u32[]{:S(2)}, u32[]{:S(2)}) collective-permute-start(f32[2,32,512]{2,1,0:T(8,128)S(1)} %pad_maximum_fusion.6), channel_id=1, source_target_pairs={{0,8},{4,12},{8,0},{12,4},{16,24},{20,28},{24,16},{28,20},{1,9},{5... | collective-permute-start | bytes 393224 | tf_op jit(solution)/shard_map/ppermute | solution.py:21
  66.5 21.4 %collective-permute-start.8 = (f32[2,2,32,512]{3,2,0,1:T(8,128)S(1)}, f32[2,2,32,512]{3,2,0,1:T(8,128)S(1)}, u32[]{:S(2)}, u32[]{:S(2)}) collective-permute-start(f32[2,2,32,512]{3,2,0,1:T(8,128)S(1)} %pad_maximum_fusion.5), channel_id=1, source_target_pairs={{0,4},{4,0},{8,12},{12,8},{16,20},{20,16},{24,28},{28,24},{1,5},{5... | collective-permute-start | bytes 786440 | tf_op jit(solution)/shard_map/ppermute | solution.py:21
  77.5 9.7 %all-to-all-start.2 = ((f32[4,8,512]{2,1,0:T(8,128)}), f32[4,8,512]{2,1,0:T(8,128)S(1)}, u32[]{:S(2)}, u32[]{:S(2)}) async-start(f32[4,8,512]{2,1,0:T(8,128)} %broadcast_in_dim.30), calls=%async_computation.2 | async-start | bytes 131072 | tf_op jit(solution)/shard_map/all_to_all | solution.py:57

commit v3 on v2

--- a/solution.py
+++ b/solution.py
@@ -51,12 +51,6 @@
     return value
 
 
-def gather_small(value, axis):
-    count = lax.axis_size(axis)
-    spread = jnp.broadcast_to(value[None], (count,) + value.shape)
-    return lax.all_to_all(spread, axis, 0, 0)
-
-
 def gather_ordered(value, axis, order):
     count = lax.axis_size(axis)
     levels = log2(count)
@@ -94,12 +88,14 @@
     up = list(range(log2(regions)))
     down = up[::-1]
     prev = shifted(feats[rows - tile :], "dom", 1)
-    hub_table = gather_small(hub_feats, "region").reshape(total_hubs, width)
-    window = jnp.concatenate([prev, feats], axis=0).reshape(nblk + 1, tile, width)
-    picked = jnp.take(window, tile_src, axis=0)
-    mask_b = tile_mask.astype(jnp.bfloat16)
-    prod = jnp.einsum("tij,tjd->tid", mask_b, picked, preferred_element_type=jnp.float32)
-    nsum = prod.reshape(nblk, per_block, tile, width).sum(axis=1).reshape(rows, width)
+    hub_table = gather_ordered(hub_feats, "region", down).reshape(total_hubs, width)
+    window = jnp.concatenate([prev, feats], axis=0)
+    src = tile_src.reshape(nblk, per_block)
+    chosen = src[:, :, None] == lax.broadcasted_iota(jnp.int32, (nblk, per_block, nblk + 1), 2)
+    masks = tile_mask.reshape(nblk, per_block, tile, 1, tile)
+    links = jnp.where(chosen[:, :, None, :, None], masks, 0).sum(axis=1)
+    links = links.reshape(rows, (nblk + 1) * tile)
+    nsum = jnp.dot(links.astype(jnp.bfloat16), window, preferred_element_type=jnp.float32)
     cnt = tile_mask.reshape(nblk, per_block, tile, tile).sum(axis=(1, 3)).reshape(rows)
     deg = 1.0 + cnt.astype(jnp.float32) + jnp.float32(hub_count)
     hub_cols = lax.broadcasted_iota(jnp.int32, (rows, total_hubs), 1)
@@ -126,8 +122,7 @@
     sgrad = (dagg / deg[:, None]).astype(jnp.bfloat16)
     partial_h = lax.dot_general(counts, sgrad, (((0,), (0,)), ((), ())), preferred_element_type=jnp.float32)
     partial_h = partial_h.reshape(regions, owned, width)
-    region_h = lax.all_to_all(partial_h, "region", 0, 0).sum(axis=0)
-    hub_grad = gather_small(region_h, "dom").sum(axis=0)
+    hub_grad = sum_all(scatter_sum(partial_h, "region", 0, up), "dom")
     return (activ, weight_grad, hub_grad)
 
 

time: 89.4 us -> 71.1 us (0.80)
  blocking collectives: 9.57 us -> 0 us
  matrix products: 8.98 us -> 4.89 us
  local copies, waits for them, and re-layouts: 7.64 us -> 4.08 us
  starting transfers between devices: 25.7 us -> 23.6 us
  waiting for transfers between devices: 30.9 us -> 32.6 us
    all_to_all x1 -> x0, blocking collectives: 9.57 us -> none  [on_device(): region_h = lax.all_to_all(partial_h, 'region', 0, 0).sum(axis=0)]
    all_to_all x2 -> x0, starting transfers between devices: 9.2 us -> none  [gather_small(): return lax.all_to_all(spread, axis, 0, 0)]
    ppermute x6 -> x14, starting transfers between devices: 8.82 us -> 17.9 us  [swap(): return lax.ppermute(value, axis, [(i, i ^ 1 << bit) for i in range(count)])]
    all_to_all x2 -> x0, waiting for transfers between devices: 5.75 us -> none  [gather_small(): return lax.all_to_all(spread, axis, 0, 0)]
    ppermute x6 -> x14, waiting for transfers between devices: 13.6 us -> 19 us  [swap(): return lax.ppermute(value, axis, [(i, i ^ 1 << bit) for i in range(count)])]
    dot_general x1, matrix products: 3.59 us -> 0.66 us  [on_device(): jnp.dot(links.astype(jnp.bfloat16), window, preferred_element_type=jnp.fl...]
    ppermute x2, starting transfers between devices: 4.17 us -> 2.13 us  [scatter_sum(): value = keep + lax.ppermute(send, axis, pairs)]
    ppermute x2, waiting for transfers between devices: 11.5 us -> 13.5 us  [scatter_sum(): value = keep + lax.ppermute(send, axis, pairs)]
  transfers between devices with their start and end apart: 11 -> 17, of which waited for: 8 -> 11; matrix products, arithmetic and copies ran while one was open for 15% -> 11% of each run, Pallas kernels for 0% -> 0%
where the time goes in v3:
time: 71.1 us; the launch traced here: 70.9 us
  waiting for transfers between devices  32.6 us (46%)
  starting transfers between devices  23.6 us (33%)
  matrix products  4.89 us (7%)
  other arithmetic  4.73 us (7%)
  local copies, waits for them, and re-layouts  4.08 us (6%)
  between operations  1.05 us (1%)
    ppermute x14, waiting for transfers between devices, swap(): return lax.ppermute(value, axis, [(i, i ^ 1 << bit) for i in range(count)])  19 us
    ppermute x14, starting transfers between devices, swap(): return lax.ppermute(value, axis, [(i, i ^ 1 << bit) for i in range(count)])  17.9 us
    ppermute x2, waiting for transfers between devices, scatter_sum(): value = keep + lax.ppermute(send, axis, pairs)  13.5 us
    ppermute x1, starting transfers between devices, shifted(): lax.ppermute(value, axis, [(source, source + steps) for source in range(i...  3.49 us
    ppermute x2, starting transfers between devices, scatter_sum(): value = keep + lax.ppermute(send, axis, pairs)  2.13 us
    reduce_sum x1, other arithmetic, on_device(): links = jnp.where(chosen[:, :, None, :, None], masks, 0).sum(axis=1)  1.92 us
    dot_general x1, matrix products, on_device(): z = jnp.dot(inputs, w_stack, preferred_element_type=jnp.float32)  1.91 us
  transfers between devices with their start and end apart: 17, of which 11 were waited for; matrix products, arithmetic and copies ran while one was open for 11% of the time, Pallas kernels for 0%

profile of v3, /device:TPU:0, one launch (start us, length us, event | category | flops | bytes accessed | tf_op | source)
XLA Modules:
  0.0 70.9 jit_solution(7260383100373239108)
XLA Ops:
  0.7 0.0 copy-start
  0.7 3.1 %collective-permute-start.1 = (bf16[8,512]{1,0:T(8,128)(2,1)}, bf16[8,512]{1,0:T(8,128)(2,1)S(1)}, u32[]{:S(2)}, u32[]{:S(2)}) collective-permute-start(bf16[8,512]{1,0:T(8,128)(2,1)} %param.8), channel_id=1, source_target_pairs={{0,16},{4,20},{8,24},{12,28},{16,0},{20,4},{24,8},{28,12},{1,17},{... | collective-permute-start | bytes 24584 | tf_op jit(solution)/shard_map/ppermute | solution.py:21
  3.7 0.9 %slice.18 = bf16[128,512]{1,0:T(8,128)(2,1)S(1)} slice(bf16[512,512]{1,0:T(8,128)(2,1)} %param.7), slice={[384:512], [0:512]} | slice | bytes 262144 | tf_op jit(solution)/shard_map/slice | solution.py:90
  4.6 3.5 %collective-permute-start = (bf16[128,512]{1,0:T(8,128)(2,1)S(1)}, bf16[128,512]{1,0:T(8,128)(2,1)S(1)}, u32[]{:S(2)}, u32[]{:S(2)}) collective-permute-start(bf16[128,512]{1,0:T(8,128)(2,1)S(1)} %slice.18), channel_id=1, source_target_pairs={{0,1},{1,2},{2,3},{4,5},{5,6},{6,7},{8,9},{9,10},{10,11},{12,13},{... | collective-permute-start | bytes 393224 | tf_op jit(solution)/shard_map/ppermute | solution.py:10
  8.1 0.7 %eq.69 = s32[4,4]{1,0:T(4,128)S(1)} reshape(s32[16]{0:T(128)} %param.10) | data formatting | bytes 128 | tf_op jit(solution)/shard_map/eq | solution.py:94
  8.9 0.1 iota_compare_fusion.4
  9.0 1.9 %select_reduce_fusion = s32[4,128,5,128]{3,1,2,0:T(8,128)S(1)} fusion(s32[4,4,128,128]{3,2,1,0:T(8,128)} %bitcast.112, pred[4,4,5]{2,1,0:T(4,128)(4,1)S(1)} %iota_compare_fusion.4), kind=kLoop, calls=%fused_computation | loop fusion | flops 2293760 | bytes 2359376 | tf_op jit(solution)/shard_map/reduce_sum | solution.py:96
  10.9 0.0 collective-permute-done.1
  10.9 1.6 %collective-permute-start.2 = (bf16[2,8,512]{2,1,0:T(8,128)(2,1)S(1)}, bf16[2,8,512]{2,1,0:T(8,128)(2,1)S(1)}, u32[]{:S(2)}, u32[]{:S(2)}) collective-permute-start(bf16[2,8,512]{2,1,0:T(8,128)(2,1)S(1)} %pad_maximum_fusion.8), channel_id=1, source_target_pairs={{0,8},{4,12},{8,0},{12,4},{16,24},{20,28},{24,16},{28,20},{1,9},{5... | collective-permute-start | bytes 49160 | tf_op jit(solution)/shard_map/ppermute | solution.py:21
  12.5 0.3 reduce_sum.26
  12.9 1.8 %collective-permute-done.2 = bf16[2,8,512]{2,1,0:T(8,128)(2,1)S(1)} collective-permute-done((bf16[2,8,512]{2,1,0:T(8,128)(2,1)S(1)}, bf16[2,8,512]{2,1,0:T(8,128)(2,1)S(1)}, u32[]{:S(2)}, u32[]{:S(2)}) %collective-permute-start.2) | collective-permute-done | bytes 16416 | tf_op jit(solution)/shard_map/ppermute | solution.py:21
  14.8 0.1 collective-permute-start.3
  14.9 0.2 copy.34
  15.1 0.1 convert_element_type.48
  15.2 0.9 %copy.31 = bf16[4,128,5,128]{1,0,3,2:T(4,128)(2,1)S(1)} copy(bf16[4,128,5,128]{3,1,2,0:T(8,128)(2,1)S(1)} %convert_element_type.48) | data formatting | bytes 1310720 | tf_op jit(solution)/shard_map/convert_element_type | solution.py:98
  16.2 0.0 collective-permute-done.3
  16.2 0.9 %fusion.18 = f32[512,512]{0,1:T(8,128)S(1)} fusion(bf16[64,512]{1,0:T(8,128)(2,1)S(1)} %bitcast.118, s32[512]{0:T(512)S(1)} %bitcast.126, s32[512]{0:T(512)S(1)} %bitcast.128, s32[512]{0:T(512)S(1)} %bitcast.124, s32[512]{0:T(512)S(1)} %bitcast.122), kind=kOutput, calls=%fused_computation.44 | convolution fusion | flops 33947648 | bytes 1122304 | tf_op jit(solution)/shard_map/dot_general | solution.py:106
  17.2 0.0 collective-permute-done
  17.2 0.0 copy-start.6
  17.2 0.0 copy-start.8
  17.2 0.7 fusion.2
  17.9 0.5 copy-done.6
  18.4 0.1 copy-done.8
  18.5 1.9 %multiply_convert_fusion = (bf16[512,512]{1,0:T(8,128)(2,1)S(1)}, bf16[512,512]{1,0:T(8,128)(2,1)}) fusion(bf16[512,512]{1,0:T(8,128)(2,1)S(1)} %copy-done.8, bf16[1024,512]{1,0:T(8,128)(2,1)S(1)} %copy-done.6, bf16[512,512]{0,1:T(8,128)(2,1)S(1)} %fusion.2, bf16[512,512]{0,1:T(8,128)(2,1)S(1)} %copy.34), kind=kOutput, calls=%fused_computation.11 | convolution fusion | flops 542113792 | bytes 3670016 | tf_op jit(solution)/shard_map/dot_general | solution.py:109
  20.4 0.7 fusion.5
  21.1 0.1 copy-done.2
  21.2 0.2 constant_dynamic-slice_fusion.3
  21.5 0.1 copy.57
  21.6 0.5 collective-permute-start.4
  22.1 2.3 %collective-permute-done.4 = f32[4,2,2,32,512]{4,3,1,0,2:T(8,128)S(1)} collective-permute-done((f32[4,2,2,32,512]{4,3,1,0,2:T(8,128)S(1)}, f32[4,2,2,32,512]{4,3,1,0,2:T(8,128)S(1)}, u32[]{:S(2)}, u32[]{:S(2)}) %collective-permute-start.4) | collective-permute-done | bytes 1048608 | tf_op jit(solution)/shard_map/ppermute | solution.py:21
  24.4 0.2 bitcast_add_fusion
  24.7 0.1 constant_dynamic-slice_fusion.1
  24.8 0.1 bitcast_select_fusion
  24.9 1.6 %collective-permute-start.5 = (f32[4,2,32,512]{3,2,1,0:T(8,128)S(1)}, f32[4,2,32,512]{3,2,1,0:T(8,128)S(1)}, u32[]{:S(2)}, u32[]{:S(2)}) collective-permute-start(f32[4,2,32,512]{3,2,1,0:T(8,128)S(1)} %bitcast_select_fusion), channel_id=1, source_target_pairs={{0,8},{4,20},{8,0},{12,28},{16,24},{20,4},{24,16},{28,12},{1,9},{5... | collective-permute-start | bytes 1572872 | tf_op jit(solution)/shard_map/ppermute | solution.py:49
  26.4 7.7 %collective-permute-done.5 = f32[4,2,32,512]{3,2,1,0:T(8,128)S(1)} collective-permute-done((f32[4,2,32,512]{3,2,1,0:T(8,128)S(1)}, f32[4,2,32,512]{3,2,1,0:T(8,128)S(1)}, u32[]{:S(2)}, u32[]{:S(2)}) %collective-permute-start.5) | collective-permute-done | bytes 524320 | tf_op jit(solution)/shard_map/ppermute | solution.py:49
  34.1 0.1 fusion.12
  34.3 0.0 copy-start.7
  34.3 0.6 collective-permute-start.6
  34.9 5.9 %collective-permute-done.6 = f32[4,32,512]{2,1,0:T(8,128)S(1)} collective-permute-done((f32[4,32,512]{2,1,0:T(8,128)S(1)}, f32[4,32,512]{2,1,0:T(8,128)S(1)}, u32[]{:S(2)}, u32[]{:S(2)}) %collective-permute-start.6) | collective-permute-done | bytes 262176 | tf_op jit(solution)/shard_map/ppermute | solution.py:49
  40.8 0.1 fusion.17
  40.8 1.6 %collective-permute-start.7 = (f32[2,32,512]{2,1,0:T(8,128)S(1)}, f32[2,32,512]{2,1,0:T(8,128)S(1)}, u32[]{:S(2)}, u32[]{:S(2)}) collective-permute-start(f32[2,32,512]{2,1,0:T(8,128)S(1)} %dynamic-slice_bitcast_fusion), channel_id=1, source_target_pairs={{0,1},{1,0},{2,3},{3,2},{4,5},{5,4},{6,7},{7,6},{8,9},{9,8},{10,11... | collective-permute-start | bytes 393224 | tf_op jit(solution)/shard_map/ppermute | solution.py:21
  42.5 0.7 fusion.4
  43.2 0.1 collective-permute-start.12
  43.3 2.6 %collective-permute-done.7 = f32[2,32,512]{2,1,0:T(8,128)S(1)} collective-permute-done((f32[2,32,512]{2,1,0:T(8,128)S(1)}, f32[2,32,512]{2,1,0:T(8,128)S(1)}, u32[]{:S(2)}, u32[]{:S(2)}) %collective-permute-start.7) | collective-permute-done | bytes 131104 | tf_op jit(solution)/shard_map/ppermute | solution.py:21
  45.9 2.7 %collective-permute-start.8 = (f32[32,512]{1,0:T(8,128)S(1)}, f32[32,512]{1,0:T(8,128)S(1)}, u32[]{:S(2)}, u32[]{:S(2)}) collective-permute-start(f32[32,512]{1,0:T(8,128)S(1)} %dynamic-slice_bitcast_fusion.2), channel_id=1, source_target_pairs={{0,2},{1,3},{2,0},{3,1},{4,6},{5,7},{6,4},{7,5},{8,10},{9,11},{10,... | collective-permute-start | bytes 196616 | tf_op jit(solution)/shard_map/ppermute | solution.py:21
  48.6 0.0 collective-permute-done.12
  48.6 2.6 %collective-permute-done.8 = f32[32,512]{1,0:T(8,128)S(1)} collective-permute-done((f32[32,512]{1,0:T(8,128)S(1)}, f32[32,512]{1,0:T(8,128)S(1)}, u32[]{:S(2)}, u32[]{:S(2)}) %collective-permute-start.8) | collective-permute-done | bytes 65568 | tf_op jit(solution)/shard_map/ppermute | solution.py:21
  51.2 0.6 collective-permute-start.9
  51.7 1.5 %collective-permute-start.13 = (f32[2,8,512]{2,1,0:T(8,128)S(1)}, f32[2,8,512]{2,1,0:T(8,128)S(1)}, u32[]{:S(2)}, u32[]{:S(2)}) collective-permute-start(f32[2,8,512]{2,1,0:T(8,128)S(1)} %dynamic-slice_bitcast_fusion.3), channel_id=1, source_target_pairs={{0,8},{4,12},{8,0},{12,4},{16,24},{20,28},{24,16},{28,20},{1,9},{5... | collective-permute-start | bytes 98312 | tf_op jit(solution)/shard_map/ppermute | solution.py:21
  53.2 2.4 %collective-permute-done.9 = f32[32,512]{1,0:T(8,128)S(1)} collective-permute-done((f32[32,512]{1,0:T(8,128)S(1)}, f32[32,512]{1,0:T(8,128)S(1)}, u32[]{:S(2)}, u32[]{:S(2)}) %collective-permute-start.9) | collective-permute-done | bytes 65568 | tf_op jit(solution)/shard_map/ppermute | solution.py:21
  55.7 1.4 %collective-permute-start.10 = (f32[2,32,512]{2,1,0:T(8,128)S(1)}, f32[2,32,512]{2,1,0:T(8,128)S(1)}, u32[]{:S(2)}, u32[]{:S(2)}) collective-permute-start(f32[2,32,512]{2,1,0:T(8,128)S(1)} %pad_maximum_fusion.5), channel_id=1, source_target_pairs={{0,8},{4,12},{8,0},{12,4},{16,24},{20,28},{24,16},{28,20},{1,9},{5... | collective-permute-start | bytes 393224 | tf_op jit(solution)/shard_map/ppermute | solution.py:21
  57.1 0.0 collective-permute-done.13
  57.1 0.6 collective-permute-start.14
  57.8 3.0 %collective-permute-done.10 = f32[2,32,512]{2,1,0:T(8,128)S(1)} collective-permute-done((f32[2,32,512]{2,1,0:T(8,128)S(1)}, f32[2,32,512]{2,1,0:T(8,128)S(1)}, u32[]{:S(2)}, u32[]{:S(2)}) %collective-permute-start.10) | collective-permute-done | bytes 131104 | tf_op jit(solution)/shard_map/ppermute | solution.py:21
  60.8 0.1 collective-permute-start.11
  60.9 0.1 collective-permute-done.14
  60.9 1.6 %collective-permute-start.15 = (f32[8,512]{1,0:T(8,128)S(1)}, f32[8,512]{1,0:T(8,128)S(1)}, u32[]{:S(2)}, u32[]{:S(2)}) collective-permute-start(f32[8,512]{1,0:T(8,128)S(1)} %bitcast_add_fusion.5), channel_id=1, source_target_pairs={{0,1},{1,0},{2,3},{3,2},{4,5},{5,4},{6,7},{7,6},{8,9},{9,8},{10,11... | collective-permute-start | bytes 49160 | tf_op jit(solution)/shard_map/ppermute | solution.py:21
  62.5 2.2 %collective-permute-done.15 = f32[8,512]{1,0:T(8,128)S(1)} collective-permute-done((f32[8,512]{1,0:T(8,128)S(1)}, f32[8,512]{1,0:T(8,128)S(1)}, u32[]{:S(2)}, u32[]{:S(2)}) %collective-permute-start.15) | collective-permute-done | bytes 16416 | tf_op jit(solution)/shard_map/ppermute | solution.py:21
  64.7 2.6 %collective-permute-start.16 = (f32[8,512]{1,0:T(8,128)S(1)}, f32[8,512]{1,0:T(8,128)S(1)}, u32[]{:S(2)}, u32[]{:S(2)}) collective-permute-start(f32[8,512]{1,0:T(8,128)S(1)} %add.150), channel_id=1, source_target_pairs={{0,2},{1,3},{2,0},{3,1},{4,6},{5,7},{6,4},{7,5},{8,10},{9,11},{10,... | collective-permute-start | bytes 49160 | tf_op jit(solution)/shard_map/ppermute | solution.py:21
  67.3 2.1 %collective-permute-done.16 = f32[8,512]{1,0:T(8,128)S(1)} collective-permute-done((f32[8,512]{1,0:T(8,128)S(1)}, f32[8,512]{1,0:T(8,128)S(1)}, u32[]{:S(2)}, u32[]{:S(2)}) %collective-permute-start.16) | collective-permute-done | bytes 16416 | tf_op jit(solution)/shard_map/ppermute | solution.py:21
  69.4 0.6 add.151
  70.0 0.0 collective-permute-done.11
  70.0 0.1 select_bitcast_fusion.1
  70.0 0.8 %pad_maximum_fusion.3 = f32[2,2,2,32,512]{4,3,0,1,2:T(8,128)} fusion(f32[1,2,2,32,512]{4,3,0,1,2:T(8,128)S(1)} %get-tuple-element.10, f32[1,2,2,32,512]{4,3,0,1,2:T(8,128)S(1)} %get-tuple-element.9), kind=kLoop, calls=%fused_computation.21 | loop fusion | flops 131072 | bytes 1048576 | tf_op jit(solution)/shard_map/stack | solution.py:65
  (36 shorter events, 0.3 us)
Async XLA Ops:
  0.6 10.3 %copy-start.5 = (bf16[8,512]{1,0:T(8,128)(2,1)S(1)}, bf16[8,512]{1,0:T(8,128)(2,1)}, u32[]{:S(2)}) copy-start(bf16[8,512]{1,0:T(8,128)(2,1)} %param.8) | copy-start | bytes 24580
  0.6 14.2 %copy-start.1 = (bf16[512,512]{1,0:T(8,128)(2,1)S(1)}, bf16[512,512]{1,0:T(8,128)(2,1)}, u32[]{:S(2)}) copy-start(bf16[512,512]{1,0:T(8,128)(2,1)} %param.7) | copy-start | bytes 1572868
  0.7 11.9 %copy-start = (s32[16,128,128]{2,1,0:T(8,128)S(1)}, s32[16,128,128]{2,1,0:T(8,128)}, u32[]{:S(2)}) copy-start(s32[16,128,128]{2,1,0:T(8,128)} %param.11) | copy-start | bytes 3145732
  0.7 11.8 %copy-start.4 = (s32[512,4]{0,1:T(4,128)S(1)}, s32[512,4]{0,1:T(4,128)}, u32[]{:S(2)}) copy-start(s32[512,4]{0,1:T(4,128)} %param.9) | copy-start | bytes 24580
  0.7 10.2 %collective-permute-start.1 = (bf16[8,512]{1,0:T(8,128)(2,1)}, bf16[8,512]{1,0:T(8,128)(2,1)S(1)}, u32[]{:S(2)}, u32[]{:S(2)}) collective-permute-start(bf16[8,512]{1,0:T(8,128)(2,1)} %param.8), channel_id=1, source_target_pairs={{0,16},{4,20},{8,24},{12,28},{16,0},{20,4},{24,8},{28,12},{1,17},{... | collective-permute-start | bytes 24584 | tf_op jit(solution)/shard_map/ppermute | solution.py:21
  4.6 12.5 %collective-permute-start = (bf16[128,512]{1,0:T(8,128)(2,1)S(1)}, bf16[128,512]{1,0:T(8,128)(2,1)S(1)}, u32[]{:S(2)}, u32[]{:S(2)}) collective-permute-start(bf16[128,512]{1,0:T(8,128)(2,1)S(1)} %slice.18), channel_id=1, source_target_pairs={{0,1},{1,2},{2,3},{4,5},{5,6},{6,7},{8,9},{9,10},{10,11},{12,13},{... | collective-permute-start | bytes 393224 | tf_op jit(solution)/shard_map/ppermute | solution.py:10
  10.9 3.8 %collective-permute-start.2 = (bf16[2,8,512]{2,1,0:T(8,128)(2,1)S(1)}, bf16[2,8,512]{2,1,0:T(8,128)(2,1)S(1)}, u32[]{:S(2)}, u32[]{:S(2)}) collective-permute-start(bf16[2,8,512]{2,1,0:T(8,128)(2,1)S(1)} %pad_maximum_fusion.8), channel_id=1, source_target_pairs={{0,8},{4,12},{8,0},{12,4},{16,24},{20,28},{24,16},{28,20},{1,9},{5... | collective-permute-start | bytes 49160 | tf_op jit(solution)/shard_map/ppermute | solution.py:21
  14.8 1.4 %collective-permute-start.3 = (bf16[2,2,8,512]{3,2,0,1:T(8,128)(2,1)S(1)}, bf16[2,2,8,512]{3,2,0,1:T(8,128)(2,1)S(1)}, u32[]{:S(2)}, u32[]{:S(2)}) collective-permute-start(bf16[2,2,8,512]{3,2,0,1:T(8,128)(2,1)S(1)} %pad_maximum_fusion.7), channel_id=1, source_target_pairs={{0,4},{4,0},{8,12},{12,8},{16,20},{20,16},{24,28},{28,24},{1,5},{5... | collective-permute-start | bytes 98312 | tf_op jit(solution)/shard_map/ppermute | solution.py:21
  17.2 1.2 %copy-start.6 = (bf16[1024,512]{1,0:T(8,128)(2,1)S(1)}, bf16[1024,512]{1,0:T(8,128)(2,1)}, u32[]{:S(2)}) copy-start(bf16[1024,512]{1,0:T(8,128)(2,1)} %param.12) | copy-start | bytes 3145732
  17.2 1.3 %copy-start.8 = (bf16[512,512]{1,0:T(8,128)(2,1)S(1)}, bf16[512,512]{1,0:T(8,128)(2,1)}, u32[]{:S(2)}) copy-start(bf16[512,512]{1,0:T(8,128)(2,1)} %param.13) | copy-start | bytes 1572868
  20.4 0.8 %copy-start.2 = (bf16[512,512]{1,0:T(8,128)(2,1)}, bf16[512,512]{1,0:T(8,128)(2,1)S(1)}, u32[]{:S(2)}) copy-start(bf16[512,512]{1,0:T(8,128)(2,1)S(1)} %get-tuple-element.7) | copy-start | bytes 1572868
  21.6 2.8 %collective-permute-start.4 = (f32[4,2,2,32,512]{4,3,1,0,2:T(8,128)S(1)}, f32[4,2,2,32,512]{4,3,1,0,2:T(8,128)S(1)}, u32[]{:S(2)}, u32[]{:S(2)}) collective-permute-start(f32[4,2,2,32,512]{4,3,1,0,2:T(8,128)S(1)} %bitcast.115), channel_id=1, source_target_pairs={{0,4},{4,0},{8,12},{12,8},{16,20},{20,16},{24,28},{28,24},{1,5},{5... | collective-permute-start | bytes 3145736 | tf_op jit(solution)/shard_map/ppermute | solution.py:21
  24.9 9.2 %collective-permute-start.5 = (f32[4,2,32,512]{3,2,1,0:T(8,128)S(1)}, f32[4,2,32,512]{3,2,1,0:T(8,128)S(1)}, u32[]{:S(2)}, u32[]{:S(2)}) collective-permute-start(f32[4,2,32,512]{3,2,1,0:T(8,128)S(1)} %bitcast_select_fusion), channel_id=1, source_target_pairs={{0,8},{4,20},{8,0},{12,28},{16,24},{20,4},{24,16},{28,12},{1,9},{5... | collective-permute-start | bytes 1572872 | tf_op jit(solution)/shard_map/ppermute | solution.py:49
  34.1 8.4 %copy-start.3 = (bf16[512,512]{1,0:T(8,128)(2,1)S(1)}, bf16[512,512]{1,0:T(8,128)(2,1)}, u32[]{:S(2)}) copy-start(bf16[512,512]{1,0:T(8,128)(2,1)} %copy-done.2) | copy-start | bytes 1572868
  34.3 8.2 %copy-start.7 = (bf16[1024,512]{1,0:T(8,128)(2,1)S(1)}, bf16[1024,512]{1,0:T(8,128)(2,1)}, u32[]{:S(2)}) copy-start(bf16[1024,512]{1,0:T(8,128)(2,1)} %param.12) | copy-start | bytes 3145732
  34.3 6.4 %collective-permute-start.6 = (f32[4,32,512]{2,1,0:T(8,128)S(1)}, f32[4,32,512]{2,1,0:T(8,128)S(1)}, u32[]{:S(2)}, u32[]{:S(2)}) collective-permute-start(f32[4,32,512]{2,1,0:T(8,128)S(1)} %select_bitcast_fusion.2), channel_id=1, source_target_pairs={{0,16},{4,12},{8,24},{12,4},{16,0},{20,28},{24,8},{28,20},{1,17},{... | collective-permute-start | bytes 786440 | tf_op jit(solution)/shard_map/ppermute | solution.py:49
  40.8 5.0 %collective-permute-start.7 = (f32[2,32,512]{2,1,0:T(8,128)S(1)}, f32[2,32,512]{2,1,0:T(8,128)S(1)}, u32[]{:S(2)}, u32[]{:S(2)}) collective-permute-start(f32[2,32,512]{2,1,0:T(8,128)S(1)} %dynamic-slice_bitcast_fusion), channel_id=1, source_target_pairs={{0,1},{1,0},{2,3},{3,2},{4,5},{5,4},{6,7},{7,6},{8,9},{9,8},{10,11... | collective-permute-start | bytes 393224 | tf_op jit(solution)/shard_map/ppermute | solution.py:21
  43.2 5.4 %collective-permute-start.12 = (f32[2,2,8,512]{3,2,1,0:T(8,128)S(1)}, f32[2,2,8,512]{3,2,1,0:T(8,128)S(1)}, u32[]{:S(2)}, u32[]{:S(2)}) collective-permute-start(f32[2,2,8,512]{3,2,1,0:T(8,128)S(1)} %dynamic-slice_bitcast_fusion.1), channel_id=1, source_target_pairs={{0,4},{4,0},{8,12},{12,8},{16,20},{20,16},{24,28},{28,24},{1,5},{5... | collective-permute-start | bytes 196616 | tf_op jit(solution)/shard_map/ppermute | solution.py:21
  45.9 5.2 %collective-permute-start.8 = (f32[32,512]{1,0:T(8,128)S(1)}, f32[32,512]{1,0:T(8,128)S(1)}, u32[]{:S(2)}, u32[]{:S(2)}) collective-permute-start(f32[32,512]{1,0:T(8,128)S(1)} %dynamic-slice_bitcast_fusion.2), channel_id=1, source_target_pairs={{0,2},{1,3},{2,0},{3,1},{4,6},{5,7},{6,4},{7,5},{8,10},{9,11},{10,... | collective-permute-start | bytes 196616 | tf_op jit(solution)/shard_map/ppermute | solution.py:21
  51.2 4.5 %collective-permute-start.9 = (f32[32,512]{1,0:T(8,128)S(1)}, f32[32,512]{1,0:T(8,128)S(1)}, u32[]{:S(2)}, u32[]{:S(2)}) collective-permute-start(f32[32,512]{1,0:T(8,128)S(1)} %bitcast_add_fusion.3), channel_id=1, source_target_pairs={{0,16},{4,20},{8,24},{12,28},{16,0},{20,4},{24,8},{28,12},{1,17},{... | collective-permute-start | bytes 196616 | tf_op jit(solution)/shard_map/ppermute | solution.py:21
  51.7 5.3 %collective-permute-start.13 = (f32[2,8,512]{2,1,0:T(8,128)S(1)}, f32[2,8,512]{2,1,0:T(8,128)S(1)}, u32[]{:S(2)}, u32[]{:S(2)}) collective-permute-start(f32[2,8,512]{2,1,0:T(8,128)S(1)} %dynamic-slice_bitcast_fusion.3), channel_id=1, source_target_pairs={{0,8},{4,12},{8,0},{12,4},{16,24},{20,28},{24,16},{28,20},{1,9},{5... | collective-permute-start | bytes 98312 | tf_op jit(solution)/shard_map/ppermute | solution.py:21
  55.7 5.0 %collective-permute-start.10 = (f32[2,32,512]{2,1,0:T(8,128)S(1)}, f32[2,32,512]{2,1,0:T(8,128)S(1)}, u32[]{:S(2)}, u32[]{:S(2)}) collective-permute-start(f32[2,32,512]{2,1,0:T(8,128)S(1)} %pad_maximum_fusion.5), channel_id=1, source_target_pairs={{0,8},{4,12},{8,0},{12,4},{16,24},{20,28},{24,16},{28,20},{1,9},{5... | collective-permute-start | bytes 393224 | tf_op jit(solution)/shard_map/ppermute | solution.py:21
  57.1 3.8 %collective-permute-start.14 = (f32[8,512]{1,0:T(8,128)S(1)}, f32[8,512]{1,0:T(8,128)S(1)}, u32[]{:S(2)}, u32[]{:S(2)}) collective-permute-start(f32[8,512]{1,0:T(8,128)S(1)} %dynamic-slice_bitcast_fusion.4), channel_id=1, source_target_pairs={{0,16},{4,20},{8,24},{12,28},{16,0},{20,4},{24,8},{28,12},{1,17},{... | collective-permute-start | bytes 49160 | tf_op jit(solution)/shard_map/ppermute | solution.py:21
  60.8 9.2 %collective-permute-start.11 = (f32[2,2,32,512]{3,2,0,1:T(8,128)S(1)}, f32[2,2,32,512]{3,2,0,1:T(8,128)S(1)}, u32[]{:S(2)}, u32[]{:S(2)}) collective-permute-start(f32[2,2,32,512]{3,2,0,1:T(8,128)S(1)} %pad_maximum_fusion.4), channel_id=1, source_target_pairs={{0,4},{4,0},{8,12},{12,8},{16,20},{20,16},{24,28},{28,24},{1,5},{5... | collective-permute-start | bytes 786440 | tf_op jit(solution)/shard_map/ppermute | solution.py:21
  60.9 3.8 %collective-permute-start.15 = (f32[8,512]{1,0:T(8,128)S(1)}, f32[8,512]{1,0:T(8,128)S(1)}, u32[]{:S(2)}, u32[]{:S(2)}) collective-permute-start(f32[8,512]{1,0:T(8,128)S(1)} %bitcast_add_fusion.5), channel_id=1, source_target_pairs={{0,1},{1,0},{2,3},{3,2},{4,5},{5,4},{6,7},{7,6},{8,9},{9,8},{10,11... | collective-permute-start | bytes 49160 | tf_op jit(solution)/shard_map/ppermute | solution.py:21
  64.7 4.6 %collective-permute-start.16 = (f32[8,512]{1,0:T(8,128)S(1)}, f32[8,512]{1,0:T(8,128)S(1)}, u32[]{:S(2)}, u32[]{:S(2)}) collective-permute-start(f32[8,512]{1,0:T(8,128)S(1)} %add.150), channel_id=1, source_target_pairs={{0,2},{1,3},{2,0},{3,1},{4,6},{5,7},{6,4},{7,5},{8,10},{9,11},{10,... | collective-permute-start | bytes 49160 | tf_op jit(solution)/shard_map/ppermute | solution.py:21

commit v4 on v3

--- a/solution.py
+++ b/solution.py
@@ -21,7 +21,7 @@
     return lax.ppermute(value, axis, [(i, i ^ (1 << bit)) for i in range(count)])
 
 
-def scatter_sum(value, axis, at, order, other=None):
+def scatter_sum(value, axis, at, order, other=None, after_first=None):
     count = lax.axis_size(axis)
     levels = log2(count)
     me = lax.axis_index(axis)
@@ -47,6 +47,9 @@
             send = jnp.where(first, parts[0][1], parts[1][1])
             pairs = [(i, i ^ (1 << (bit if i & 1 == 0 else bit_b))) for i in range(count)]
             value = keep + lax.ppermute(send, axis, pairs)
+        if after_first is not None:
+            value = after_first(value)
+            after_first = None
     assert held[0] == held[1] or levels == 0
     return value
 
@@ -69,6 +72,19 @@
     return value.reshape((count,) + rest)
 
 
+def gather_once(value, axis):
+    count = lax.axis_size(axis)
+    me = lax.axis_index(axis)
+    got = [value] + [swap_by(value, axis, k) for k in range(1, count)]
+    got = jnp.stack(got, axis=0)
+    return jnp.take(got, me ^ lax.broadcasted_iota(jnp.int32, (count,), 0), axis=0)
+
+
+def swap_by(value, axis, mask):
+    count = lax.axis_size(axis)
+    return lax.ppermute(value, axis, [(i, i ^ mask) for i in range(count)])
+
+
 def sum_all(value, axis):
     for bit in range(log2(lax.axis_size(axis))):
         value = value + swap(value, axis, bit)
@@ -88,7 +104,7 @@
     up = list(range(log2(regions)))
     down = up[::-1]
     prev = shifted(feats[rows - tile :], "dom", 1)
-    hub_table = gather_ordered(hub_feats, "region", down).reshape(total_hubs, width)
+    hub_table = gather_once(hub_feats, "region").reshape(total_hubs, width)
     window = jnp.concatenate([prev, feats], axis=0)
     src = tile_src.reshape(nblk, per_block)
     chosen = src[:, :, None] == lax.broadcasted_iota(jnp.int32, (nblk, per_block, nblk + 1), 2)
@@ -113,16 +129,22 @@
     partial_w = lax.dot_general(inputs, dz, (((0,), (0,)), ((), ())), preferred_element_type=jnp.float32)
     span = partial_w.shape[0] // (doms * regions)
     partial_w = partial_w.reshape(doms, regions, span, width)
-    region_w = scatter_sum(partial_w, "region", 1, up, up[:1] + up[1:][::-1])
-    piece_w = scatter_sum(region_w, "dom", 0, list(range(log2(doms))))
-    weight_grad = gather_ordered(piece_w, "region", down).reshape(regions * span, width)
     dagg = lax.dot_general(
         dz, w_stack[width:], (((1,), (1,)), ((), ())), preferred_element_type=jnp.float32
     )
     sgrad = (dagg / deg[:, None]).astype(jnp.bfloat16)
     partial_h = lax.dot_general(counts, sgrad, (((0,), (0,)), ((), ())), preferred_element_type=jnp.float32)
     partial_h = partial_h.reshape(regions, owned, width)
-    hub_grad = sum_all(scatter_sum(partial_h, "region", 0, up), "dom")
+    held = {}
+
+    def hub_first(value):
+        value, held["h"] = lax.optimization_barrier((value, partial_h))
+        return value
+
+    region_w = scatter_sum(partial_w, "region", 1, up, up[:1] + up[1:][::-1], hub_first)
+    hub_grad = sum_all(scatter_sum(held["h"], "region", 0, up), "dom")
+    piece_w = scatter_sum(region_w, "dom", 0, list(range(log2(doms))))
+    weight_grad = gather_ordered(piece_w, "region", down).reshape(regions * span, width)
     return (activ, weight_grad, hub_grad)
 
 

time: 71.1 us -> 77.2 us (1.086)
  starting transfers between devices: 23.6 us -> 31.5 us
  waiting for transfers between devices: 32.6 us -> 27.1 us
  local copies, waits for them, and re-layouts: 4.08 us -> 5.43 us
  other arithmetic: 4.73 us -> 5.88 us
  matrix products: 4.89 us -> 5.86 us
    ppermute x0 -> x7, starting transfers between devices: none -> 7.91 us  [swap_by(): return lax.ppermute(value, axis, [(i, i ^ mask) for i in range(count)])]
    ppermute x14 -> x11, waiting for transfers between devices: 19 us -> 13.3 us  [swap(): return lax.ppermute(value, axis, [(i, i ^ 1 << bit) for i in range(count)])]
    reduce_sum x2, other arithmetic: 0.36 us -> 1.59 us  [on_device(): tile_mask.reshape(nblk, per_block, tile, tile).sum(axis=(1, 3))]
    dot_general x1, matrix products: 0.68 us -> 1.89 us  [on_device(): lax.dot_general(counts, sgrad, (((0,), (0,)), ((), ())), preferred_elemen...]
    ppermute x14 -> x11, starting transfers between devices: 17.9 us -> 16.8 us  [swap(): return lax.ppermute(value, axis, [(i, i ^ 1 << bit) for i in range(count)])]
    ppermute x2, waiting for transfers between devices: 13.5 us -> 12.5 us  [scatter_sum(): value = keep + lax.ppermute(send, axis, pairs)]
    ppermute x2, starting transfers between devices: 2.13 us -> 3.15 us  [scatter_sum(): value = keep + lax.ppermute(send, axis, pairs)]
    slice x1, local copies, waits for them, and re-layouts: 0.91 us -> 0.01 us  [on_device(): prev = shifted(feats[rows - tile:], 'dom', 1)]
  transfers between devices with their start and end apart: 17 -> 21, of which waited for: 11 -> 11; matrix products, arithmetic and copies ran while one was open for 11% -> 15% of each run, Pallas kernels for 0% -> 0%
where the time goes in v4:
time: 77.2 us; the launch traced here: 76.8 us
  starting transfers between devices  31.5 us (41%)
  waiting for transfers between devices  27.1 us (35%)
  other arithmetic  5.88 us (8%)
  matrix products  5.86 us (8%)
  local copies, waits for them, and re-layouts  5.43 us (7%)
  between operations  1 us (1%)
    ppermute x11, starting transfers between devices, swap(): return lax.ppermute(value, axis, [(i, i ^ 1 << bit) for i in range(count)])  16.8 us
    ppermute x11, waiting for transfers between devices, swap(): return lax.ppermute(value, axis, [(i, i ^ 1 << bit) for i in range(count)])  13.3 us
    ppermute x2, waiting for transfers between devices, scatter_sum(): value = keep + lax.ppermute(send, axis, pairs)  12.5 us
    ppermute x7, starting transfers between devices, swap_by(): return lax.ppermute(value, axis, [(i, i ^ mask) for i in range(count)])  7.91 us
    ppermute x1, starting transfers between devices, shifted(): lax.ppermute(value, axis, [(source, source + steps) for source in range(i...  3.7 us
    ppermute x2, starting transfers between devices, scatter_sum(): value = keep + lax.ppermute(send, axis, pairs)  3.15 us
    dot_general x1, matrix products, on_device(): z = jnp.dot(inputs, w_stack, preferred_element_type=jnp.float32)  1.9 us
    dot_general x1, matrix products, on_device(): lax.dot_general(counts, sgrad, (((0,), (0,)), ((), ())), preferred_elemen...  1.89 us
  transfers between devices with their start and end apart: 21, of which 11 were waited for; matrix products, arithmetic and copies ran while one was open for 15% of the time, Pallas kernels for 0%

profile of v4, /device:TPU:0, one launch (start us, length us, event | category | flops | bytes accessed | tf_op | source)
XLA Modules:
  0.0 76.8 jit_solution(6531576677669669837)
XLA Ops:
  0.6 2.5 %collective-permute-start.5 = (bf16[8,512]{1,0:T(8,128)(2,1)}, bf16[8,512]{1,0:T(8,128)(2,1)S(1)}, u32[]{:S(2)}, u32[]{:S(2)}) collective-permute-start(bf16[8,512]{1,0:T(8,128)(2,1)} %param.8), channel_id=1, source_target_pairs={{0,20},{4,16},{8,28},{12,24},{16,4},{20,0},{24,12},{28,8},{1,21},{... | collective-permute-start | bytes 24584 | tf_op jit(solution)/shard_map/ppermute | solution.py:85
  3.1 0.6 collective-permute-start.4
  3.8 1.4 %collective-permute-start.3 = (bf16[8,512]{1,0:T(8,128)(2,1)}, bf16[8,512]{1,0:T(8,128)(2,1)S(1)}, u32[]{:S(2)}, u32[]{:S(2)}) collective-permute-start(bf16[8,512]{1,0:T(8,128)(2,1)} %param.8), channel_id=1, source_target_pairs={{0,12},{4,8},{8,4},{12,0},{16,28},{20,24},{24,20},{28,16},{1,13},{... | collective-permute-start | bytes 24584 | tf_op jit(solution)/shard_map/ppermute | solution.py:85
  5.1 0.3 collective-permute-start.2
  5.5 0.2 collective-permute-start.1
  5.6 0.7 constant_dynamic-update-slice_fusion.7
  6.3 0.7 eq.66
  7.1 0.1 iota_compare_fusion.4
  7.2 1.6 %reduce_sum.26 = s32[16,128]{1,0:T(8,128)S(1)} reduce(s32[16,128,128]{2,1,0:T(8,128)} %param.11, s32[]{:T(128)} %constant.88.clone.1), dimensions={2}, to_apply=%region_1.2 | reduce | flops 260096 | bytes 1056772 | tf_op jit(solution)/shard_map/reduce_sum | solution.py:115
  8.8 0.9 %fusion.27 = (s32[512,1]{0,1:T(1,128)S(1)}, s32[512,1]{0,1:T(1,128)S(1)}, s32[512,1]{0,1:T(1,128)S(1)}, s32[512,1]{0,1:T(1,128)S(1)}) fusion(s32[512,4]{0,1:T(4,128)} %param.9), kind=kLoop, calls=%fused_computation.83 | loop fusion | bytes 16384 | tf_op jit(solution)/shard_map/slice | solution.py:120
  9.6 1.9 %select_reduce_fusion = s32[4,128,5,128]{3,1,2,0:T(8,128)S(1)} fusion(s32[4,4,128,128]{3,2,1,0:T(8,128)} %bitcast.115, pred[4,4,5]{2,1,0:T(4,128)(4,1)S(1)} %iota_compare_fusion.4), kind=kLoop, calls=%fused_computation.1 | loop fusion | flops 2293760 | bytes 2359376 | tf_op jit(solution)/shard_map/reduce_sum | solution.py:112
  11.6 0.0 copy-start.2
  11.6 0.2 copy.42
  11.8 0.1 broadcast_in_dim.43
  11.9 0.1 broadcast_in_dim.44
  12.0 0.1 convert_element_type.48
  12.1 0.9 %copy.41 = bf16[4,128,5,128]{1,0,3,2:T(4,128)(2,1)S(1)} copy(bf16[4,128,5,128]{3,1,2,0:T(8,128)(2,1)S(1)} %convert_element_type.48) | data formatting | bytes 1310720 | tf_op jit(solution)/shard_map/convert_element_type | solution.py:114
  13.0 0.0 collective-permute-done.1
  13.1 2.7 %collective-permute-start.7 = (bf16[8,512]{1,0:T(8,128)(2,1)S(1)}, bf16[8,512]{1,0:T(8,128)(2,1)S(1)}, u32[]{:S(2)}, u32[]{:S(2)}) collective-permute-start(bf16[8,512]{1,0:T(8,128)(2,1)S(1)} %copy-done.2), channel_id=1, source_target_pairs={{0,28},{4,24},{8,20},{12,16},{16,12},{20,8},{24,4},{28,0},{1,29},{... | collective-permute-start | bytes 24584 | tf_op jit(solution)/shard_map/ppermute | solution.py:85
  15.7 0.0 collective-permute-done.2
  15.7 0.3 collective-permute-start.6
  16.0 3.7 %collective-permute-start = (bf16[128,512]{1,0:T(8,128)(2,1)S(1)}, bf16[128,512]{1,0:T(8,128)(2,1)S(1)}, u32[]{:S(2)}, u32[]{:S(2)}) collective-permute-start(bf16[128,512]{1,0:T(8,128)(2,1)S(1)} %slice.18), channel_id=1, source_target_pairs={{0,1},{1,2},{2,3},{4,5},{5,6},{6,7},{8,9},{9,10},{10,11},{12,13},{... | collective-permute-start | bytes 393224 | tf_op jit(solution)/shard_map/ppermute | solution.py:10
  19.7 0.5 collective-permute-done.6
  20.3 0.6 gather_fusion
  20.8 0.7 fusion.19
  21.6 0.8 %collective-permute-done = bf16[128,512]{1,0:T(8,128)(2,1)S(1)} collective-permute-done((bf16[128,512]{1,0:T(8,128)(2,1)S(1)}, bf16[128,512]{1,0:T(8,128)(2,1)S(1)}, u32[]{:S(2)}, u32[]{:S(2)}) %collective-permute-start) | collective-permute-done | bytes 131104 | tf_op jit(solution)/shard_map/ppermute | solution.py:10
  22.3 0.7 fusion.2
  23.0 0.6 copy-done.3
  23.6 0.1 copy-done.4
  23.7 1.9 %multiply_convert_fusion = (bf16[512,512]{1,0:T(8,128)(2,1)S(1)}, bf16[512,512]{1,0:T(8,128)(2,1)}) fusion(bf16[512,512]{1,0:T(8,128)(2,1)S(1)} %copy-done.4, bf16[1024,512]{1,0:T(8,128)(2,1)S(1)} %copy-done.3, bf16[512,512]{0,1:T(8,128)(2,1)S(1)} %fusion.2, bf16[512,512]{0,1:T(8,128)(2,1)S(1)} %copy.42), kind=kOutput, calls=%fused_computation.13 | convolution fusion | flops 542113792 | bytes 3670016 | tf_op jit(solution)/shard_map/dot_general | solution.py:125
  25.6 0.7 fusion.6
  26.3 0.1 copy-done.1
  26.4 0.2 constant_dynamic-slice_fusion.3
  26.6 0.1 copy.65
  26.7 0.1 collective-permute-start.8
  26.8 1.9 %fusion.5 = f32[8,8,512]{2,1,0:T(8,128)S(1)} fusion(bf16[512,512]{1,0:T(8,128)(2,1)} %copy-done.1, bf16[1024,512]{1,0:T(8,128)(2,1)} %param.12, f32[512]{0:T(512)S(1)} %add_bitcast_fusion, s32[512]{0:T(512)S(1)} %bitcast.129, s32[512]{0:T(512)S(1)} %bitcast.131, s32[512]{0:T(512)S(1)} %bitcast.127, s32[512]{0:T(512)S(1)} %bitcast.125), kind=kOutput, calls=%fused_computation.9 | convolution fusion | flops 302907392 | bytes 1189888 | tf_op jit(solution)/shard_map/dot_general | solution.py:136
  28.7 0.7 collective-permute-done.8
  29.5 0.2 bitcast_add_fusion
  29.7 0.1 constant_dynamic-slice_fusion.1
  29.8 0.1 bitcast_select_fusion
  29.9 1.6 %collective-permute-start.9 = (f32[4,2,32,512]{3,2,1,0:T(8,128)S(1)}, f32[4,2,32,512]{3,2,1,0:T(8,128)S(1)}, u32[]{:S(2)}, u32[]{:S(2)}) collective-permute-start(f32[4,2,32,512]{3,2,1,0:T(8,128)S(1)} %bitcast_select_fusion), channel_id=1, source_target_pairs={{0,8},{4,20},{8,0},{12,28},{16,24},{20,4},{24,16},{28,12},{1,9},{5... | collective-permute-start | bytes 1572872 | tf_op jit(solution)/shard_map/ppermute | solution.py:49
  31.5 7.7 %collective-permute-done.9 = f32[4,2,32,512]{3,2,1,0:T(8,128)S(1)} collective-permute-done((f32[4,2,32,512]{3,2,1,0:T(8,128)S(1)}, f32[4,2,32,512]{3,2,1,0:T(8,128)S(1)}, u32[]{:S(2)}, u32[]{:S(2)}) %collective-permute-start.9) | collective-permute-done | bytes 524320 | tf_op jit(solution)/shard_map/ppermute | solution.py:49
  39.1 0.1 fusion.13
  39.3 1.6 %collective-permute-start.10 = (f32[4,32,512]{2,1,0:T(8,128)S(1)}, f32[4,32,512]{2,1,0:T(8,128)S(1)}, u32[]{:S(2)}, u32[]{:S(2)}) collective-permute-start(f32[4,32,512]{2,1,0:T(8,128)S(1)} %select_bitcast_fusion.2), channel_id=1, source_target_pairs={{0,16},{4,12},{8,24},{12,4},{16,0},{20,28},{24,8},{28,20},{1,17},{... | collective-permute-start | bytes 786440 | tf_op jit(solution)/shard_map/ppermute | solution.py:49
  40.9 4.8 %collective-permute-done.10 = f32[4,32,512]{2,1,0:T(8,128)S(1)} collective-permute-done((f32[4,32,512]{2,1,0:T(8,128)S(1)}, f32[4,32,512]{2,1,0:T(8,128)S(1)}, u32[]{:S(2)}, u32[]{:S(2)}) %collective-permute-start.10) | collective-permute-done | bytes 262176 | tf_op jit(solution)/shard_map/ppermute | solution.py:49
  45.8 0.1 fusion.18
  45.9 2.5 %collective-permute-start.11 = (f32[2,32,512]{2,1,0:T(8,128)S(1)}, f32[2,32,512]{2,1,0:T(8,128)S(1)}, u32[]{:S(2)}, u32[]{:S(2)}) collective-permute-start(f32[2,32,512]{2,1,0:T(8,128)S(1)} %dynamic-slice_bitcast_fusion), channel_id=1, source_target_pairs={{0,1},{1,0},{2,3},{3,2},{4,5},{5,4},{6,7},{7,6},{8,9},{9,8},{10,11... | collective-permute-start | bytes 393224 | tf_op jit(solution)/shard_map/ppermute | solution.py:21
  48.4 2.9 %collective-permute-done.11 = f32[2,32,512]{2,1,0:T(8,128)S(1)} collective-permute-done((f32[2,32,512]{2,1,0:T(8,128)S(1)}, f32[2,32,512]{2,1,0:T(8,128)S(1)}, u32[]{:S(2)}, u32[]{:S(2)}) %collective-permute-start.11) | collective-permute-done | bytes 131104 | tf_op jit(solution)/shard_map/ppermute | solution.py:21
  51.4 3.2 %collective-permute-start.12 = (f32[32,512]{1,0:T(8,128)S(1)}, f32[32,512]{1,0:T(8,128)S(1)}, u32[]{:S(2)}, u32[]{:S(2)}) collective-permute-start(f32[32,512]{1,0:T(8,128)S(1)} %dynamic-slice_bitcast_fusion.2), channel_id=1, source_target_pairs={{0,2},{1,3},{2,0},{3,1},{4,6},{5,7},{6,4},{7,5},{8,10},{9,11},{10,... | collective-permute-start | bytes 196616 | tf_op jit(solution)/shard_map/ppermute | solution.py:21
  54.7 2.2 %collective-permute-done.12 = f32[32,512]{1,0:T(8,128)S(1)} collective-permute-done((f32[32,512]{1,0:T(8,128)S(1)}, f32[32,512]{1,0:T(8,128)S(1)}, u32[]{:S(2)}, u32[]{:S(2)}) %collective-permute-start.12) | collective-permute-done | bytes 65568 | tf_op jit(solution)/shard_map/ppermute | solution.py:21
  56.9 1.6 %collective-permute-start.13 = (f32[32,512]{1,0:T(8,128)S(1)}, f32[32,512]{1,0:T(8,128)S(1)}, u32[]{:S(2)}, u32[]{:S(2)}) collective-permute-start(f32[32,512]{1,0:T(8,128)S(1)} %bitcast_add_fusion.3), channel_id=1, source_target_pairs={{0,16},{4,20},{8,24},{12,28},{16,0},{20,4},{24,8},{28,12},{1,17},{... | collective-permute-start | bytes 196616 | tf_op jit(solution)/shard_map/ppermute | solution.py:21
  58.5 1.5 %collective-permute-start.17 = (f32[2,8,512]{2,1,0:T(8,128)S(1)}, f32[2,8,512]{2,1,0:T(8,128)S(1)}, u32[]{:S(2)}, u32[]{:S(2)}) collective-permute-start(f32[2,8,512]{2,1,0:T(8,128)S(1)} %dynamic-slice_bitcast_fusion.3), channel_id=1, source_target_pairs={{0,8},{4,12},{8,0},{12,4},{16,24},{20,28},{24,16},{28,20},{1,9},{5... | collective-permute-start | bytes 98312 | tf_op jit(solution)/shard_map/ppermute | solution.py:21
  60.0 1.4 %collective-permute-done.13 = f32[32,512]{1,0:T(8,128)S(1)} collective-permute-done((f32[32,512]{1,0:T(8,128)S(1)}, f32[32,512]{1,0:T(8,128)S(1)}, u32[]{:S(2)}, u32[]{:S(2)}) %collective-permute-start.13) | collective-permute-done | bytes 65568 | tf_op jit(solution)/shard_map/ppermute | solution.py:21
  61.5 1.4 %collective-permute-start.14 = (f32[2,32,512]{2,1,0:T(8,128)S(1)}, f32[2,32,512]{2,1,0:T(8,128)S(1)}, u32[]{:S(2)}, u32[]{:S(2)}) collective-permute-start(f32[2,32,512]{2,1,0:T(8,128)S(1)} %pad_maximum_fusion.5), channel_id=1, source_target_pairs={{0,8},{4,12},{8,0},{12,4},{16,24},{20,28},{24,16},{28,20},{1,9},{5... | collective-permute-start | bytes 393224 | tf_op jit(solution)/shard_map/ppermute | solution.py:21
  62.9 1.6 %collective-permute-start.18 = (f32[8,512]{1,0:T(8,128)S(1)}, f32[8,512]{1,0:T(8,128)S(1)}, u32[]{:S(2)}, u32[]{:S(2)}) collective-permute-start(f32[8,512]{1,0:T(8,128)S(1)} %dynamic-slice_bitcast_fusion.4), channel_id=1, source_target_pairs={{0,16},{4,20},{8,24},{12,28},{16,0},{20,4},{24,8},{28,12},{1,17},{... | collective-permute-start | bytes 49160 | tf_op jit(solution)/shard_map/ppermute | solution.py:21
  64.4 2.0 %collective-permute-done.14 = f32[2,32,512]{2,1,0:T(8,128)S(1)} collective-permute-done((f32[2,32,512]{2,1,0:T(8,128)S(1)}, f32[2,32,512]{2,1,0:T(8,128)S(1)}, u32[]{:S(2)}, u32[]{:S(2)}) %collective-permute-start.14) | collective-permute-done | bytes 131104 | tf_op jit(solution)/shard_map/ppermute | solution.py:21
  66.5 0.1 collective-permute-start.15
  66.6 0.0 collective-permute-done.18
  66.7 1.8 %collective-permute-start.19 = (f32[8,512]{1,0:T(8,128)S(1)}, f32[8,512]{1,0:T(8,128)S(1)}, u32[]{:S(2)}, u32[]{:S(2)}) collective-permute-start(f32[8,512]{1,0:T(8,128)S(1)} %bitcast_add_fusion.5), channel_id=1, source_target_pairs={{0,1},{1,0},{2,3},{3,2},{4,5},{5,4},{6,7},{7,6},{8,9},{9,8},{10,11... | collective-permute-start | bytes 49160 | tf_op jit(solution)/shard_map/ppermute | solution.py:21
  68.5 2.0 %collective-permute-done.19 = f32[8,512]{1,0:T(8,128)S(1)} collective-permute-done((f32[8,512]{1,0:T(8,128)S(1)}, f32[8,512]{1,0:T(8,128)S(1)}, u32[]{:S(2)}, u32[]{:S(2)}) %collective-permute-start.19) | collective-permute-done | bytes 16416 | tf_op jit(solution)/shard_map/ppermute | solution.py:21
  70.5 3.0 %collective-permute-start.20 = (f32[8,512]{1,0:T(8,128)S(1)}, f32[8,512]{1,0:T(8,128)S(1)}, u32[]{:S(2)}, u32[]{:S(2)}) collective-permute-start(f32[8,512]{1,0:T(8,128)S(1)} %add.167), channel_id=1, source_target_pairs={{0,2},{1,3},{2,0},{3,1},{4,6},{5,7},{6,4},{7,5},{8,10},{9,11},{10,... | collective-permute-start | bytes 49160 | tf_op jit(solution)/shard_map/ppermute | solution.py:21
  73.5 1.9 %collective-permute-done.20 = f32[8,512]{1,0:T(8,128)S(1)} collective-permute-done((f32[8,512]{1,0:T(8,128)S(1)}, f32[8,512]{1,0:T(8,128)S(1)}, u32[]{:S(2)}, u32[]{:S(2)}) %collective-permute-start.20) | collective-permute-done | bytes 16416 | tf_op jit(solution)/shard_map/ppermute | solution.py:21
  75.3 0.6 add.168
  76.0 0.8 %pad_maximum_fusion.3 = f32[2,2,2,32,512]{4,3,0,1,2:T(8,128)} fusion(f32[1,2,2,32,512]{4,3,0,1,2:T(8,128)S(1)} %get-tuple-element.14, f32[1,2,2,32,512]{4,3,0,1,2:T(8,128)S(1)} %get-tuple-element.13), kind=kLoop, calls=%fused_computation.23 | loop fusion | flops 131072 | bytes 1048576 | tf_op jit(solution)/shard_map/stack | solution.py:68
  (44 shorter events, 0.4 us)
Async XLA Ops:
  0.6 10.9 %copy-start = (bf16[512,512]{1,0:T(8,128)(2,1)S(1)}, bf16[512,512]{1,0:T(8,128)(2,1)}, u32[]{:S(2)}) copy-start(bf16[512,512]{1,0:T(8,128)(2,1)} %param.7) | copy-start | bytes 1572868
  0.6 19.1 %collective-permute-start.5 = (bf16[8,512]{1,0:T(8,128)(2,1)}, bf16[8,512]{1,0:T(8,128)(2,1)S(1)}, u32[]{:S(2)}, u32[]{:S(2)}) collective-permute-start(bf16[8,512]{1,0:T(8,128)(2,1)} %param.8), channel_id=1, source_target_pairs={{0,20},{4,16},{8,28},{12,24},{16,4},{20,0},{24,12},{28,8},{1,21},{... | collective-permute-start | bytes 24584 | tf_op jit(solution)/shard_map/ppermute | solution.py:85
  3.1 16.6 %collective-permute-start.4 = (bf16[8,512]{1,0:T(8,128)(2,1)}, bf16[8,512]{1,0:T(8,128)(2,1)S(1)}, u32[]{:S(2)}, u32[]{:S(2)}) collective-permute-start(bf16[8,512]{1,0:T(8,128)(2,1)} %param.8), channel_id=1, source_target_pairs={{0,16},{4,20},{8,24},{12,28},{16,0},{20,4},{24,8},{28,12},{1,17},{... | collective-permute-start | bytes 24584 | tf_op jit(solution)/shard_map/ppermute | solution.py:85
  3.8 12.2 %collective-permute-start.3 = (bf16[8,512]{1,0:T(8,128)(2,1)}, bf16[8,512]{1,0:T(8,128)(2,1)S(1)}, u32[]{:S(2)}, u32[]{:S(2)}) collective-permute-start(bf16[8,512]{1,0:T(8,128)(2,1)} %param.8), channel_id=1, source_target_pairs={{0,12},{4,8},{8,4},{12,0},{16,28},{20,24},{24,20},{28,16},{1,13},{... | collective-permute-start | bytes 24584 | tf_op jit(solution)/shard_map/ppermute | solution.py:85
  5.1 10.6 %collective-permute-start.2 = (bf16[8,512]{1,0:T(8,128)(2,1)}, bf16[8,512]{1,0:T(8,128)(2,1)S(1)}, u32[]{:S(2)}, u32[]{:S(2)}) collective-permute-start(bf16[8,512]{1,0:T(8,128)(2,1)} %param.8), channel_id=1, source_target_pairs={{0,8},{4,12},{8,0},{12,4},{16,24},{20,28},{24,16},{28,20},{1,9},{5... | collective-permute-start | bytes 24584 | tf_op jit(solution)/shard_map/ppermute | solution.py:85
  5.5 7.6 %collective-permute-start.1 = (bf16[8,512]{1,0:T(8,128)(2,1)}, bf16[8,512]{1,0:T(8,128)(2,1)S(1)}, u32[]{:S(2)}, u32[]{:S(2)}) collective-permute-start(bf16[8,512]{1,0:T(8,128)(2,1)} %param.8), channel_id=1, source_target_pairs={{0,4},{4,0},{8,12},{12,8},{16,20},{20,16},{24,28},{28,24},{1,5},{5... | collective-permute-start | bytes 24584 | tf_op jit(solution)/shard_map/ppermute | solution.py:85
  11.6 1.5 %copy-start.2 = (bf16[8,512]{1,0:T(8,128)(2,1)S(1)}, bf16[8,512]{1,0:T(8,128)(2,1)}, u32[]{:S(2)}) copy-start(bf16[8,512]{1,0:T(8,128)(2,1)} %param.8) | copy-start | bytes 24580
  13.1 7.2 %collective-permute-start.7 = (bf16[8,512]{1,0:T(8,128)(2,1)S(1)}, bf16[8,512]{1,0:T(8,128)(2,1)S(1)}, u32[]{:S(2)}, u32[]{:S(2)}) collective-permute-start(bf16[8,512]{1,0:T(8,128)(2,1)S(1)} %copy-done.2), channel_id=1, source_target_pairs={{0,28},{4,24},{8,20},{12,16},{16,12},{20,8},{24,4},{28,0},{1,29},{... | collective-permute-start | bytes 24584 | tf_op jit(solution)/shard_map/ppermute | solution.py:85
  15.7 4.6 %collective-permute-start.6 = (bf16[8,512]{1,0:T(8,128)(2,1)S(1)}, bf16[8,512]{1,0:T(8,128)(2,1)S(1)}, u32[]{:S(2)}, u32[]{:S(2)}) collective-permute-start(bf16[8,512]{1,0:T(8,128)(2,1)S(1)} %copy-done.2), channel_id=1, source_target_pairs={{0,24},{4,28},{8,16},{12,20},{16,8},{20,12},{24,0},{28,4},{1,25},{... | collective-permute-start | bytes 24584 | tf_op jit(solution)/shard_map/ppermute | solution.py:85
  16.0 6.4 %collective-permute-start = (bf16[128,512]{1,0:T(8,128)(2,1)S(1)}, bf16[128,512]{1,0:T(8,128)(2,1)S(1)}, u32[]{:S(2)}, u32[]{:S(2)}) collective-permute-start(bf16[128,512]{1,0:T(8,128)(2,1)S(1)} %slice.18), channel_id=1, source_target_pairs={{0,1},{1,2},{2,3},{4,5},{5,6},{6,7},{8,9},{9,10},{10,11},{12,13},{... | collective-permute-start | bytes 393224 | tf_op jit(solution)/shard_map/ppermute | solution.py:10
  22.3 1.2 %copy-start.3 = (bf16[1024,512]{1,0:T(8,128)(2,1)S(1)}, bf16[1024,512]{1,0:T(8,128)(2,1)}, u32[]{:S(2)}) copy-start(bf16[1024,512]{1,0:T(8,128)(2,1)} %param.12) | copy-start | bytes 3145732
  22.3 1.4 %copy-start.4 = (bf16[512,512]{1,0:T(8,128)(2,1)S(1)}, bf16[512,512]{1,0:T(8,128)(2,1)}, u32[]{:S(2)}) copy-start(bf16[512,512]{1,0:T(8,128)(2,1)} %param.13) | copy-start | bytes 1572868
  25.6 0.8 %copy-start.1 = (bf16[512,512]{1,0:T(8,128)(2,1)}, bf16[512,512]{1,0:T(8,128)(2,1)S(1)}, u32[]{:S(2)}) copy-start(bf16[512,512]{1,0:T(8,128)(2,1)S(1)} %get-tuple-element.11) | copy-start | bytes 1572868
  26.7 2.7 %collective-permute-start.8 = (f32[4,2,2,32,512]{4,3,1,0,2:T(8,128)S(1)}, f32[4,2,2,32,512]{4,3,1,0,2:T(8,128)S(1)}, u32[]{:S(2)}, u32[]{:S(2)}) collective-permute-start(f32[4,2,2,32,512]{4,3,1,0,2:T(8,128)S(1)} %bitcast.118), channel_id=1, source_target_pairs={{0,4},{4,0},{8,12},{12,8},{16,20},{20,16},{24,28},{28,24},{1,5},{5... | collective-permute-start | bytes 3145736 | tf_op jit(solution)/shard_map/ppermute | solution.py:21
  29.9 9.2 %collective-permute-start.9 = (f32[4,2,32,512]{3,2,1,0:T(8,128)S(1)}, f32[4,2,32,512]{3,2,1,0:T(8,128)S(1)}, u32[]{:S(2)}, u32[]{:S(2)}) collective-permute-start(f32[4,2,32,512]{3,2,1,0:T(8,128)S(1)} %bitcast_select_fusion), channel_id=1, source_target_pairs={{0,8},{4,20},{8,0},{12,28},{16,24},{20,4},{24,16},{28,12},{1,9},{5... | collective-permute-start | bytes 1572872 | tf_op jit(solution)/shard_map/ppermute | solution.py:49
  39.3 6.4 %collective-permute-start.10 = (f32[4,32,512]{2,1,0:T(8,128)S(1)}, f32[4,32,512]{2,1,0:T(8,128)S(1)}, u32[]{:S(2)}, u32[]{:S(2)}) collective-permute-start(f32[4,32,512]{2,1,0:T(8,128)S(1)} %select_bitcast_fusion.2), channel_id=1, source_target_pairs={{0,16},{4,12},{8,24},{12,4},{16,0},{20,28},{24,8},{28,20},{1,17},{... | collective-permute-start | bytes 786440 | tf_op jit(solution)/shard_map/ppermute | solution.py:49
  45.9 5.5 %collective-permute-start.11 = (f32[2,32,512]{2,1,0:T(8,128)S(1)}, f32[2,32,512]{2,1,0:T(8,128)S(1)}, u32[]{:S(2)}, u32[]{:S(2)}) collective-permute-start(f32[2,32,512]{2,1,0:T(8,128)S(1)} %dynamic-slice_bitcast_fusion), channel_id=1, source_target_pairs={{0,1},{1,0},{2,3},{3,2},{4,5},{5,4},{6,7},{7,6},{8,9},{9,8},{10,11... | collective-permute-start | bytes 393224 | tf_op jit(solution)/shard_map/ppermute | solution.py:21
  48.4 6.2 %collective-permute-start.16 = (f32[2,2,8,512]{3,2,1,0:T(8,128)S(1)}, f32[2,2,8,512]{3,2,1,0:T(8,128)S(1)}, u32[]{:S(2)}, u32[]{:S(2)}) collective-permute-start(f32[2,2,8,512]{3,2,1,0:T(8,128)S(1)} %dynamic-slice_bitcast_fusion.1), channel_id=1, source_target_pairs={{0,4},{4,0},{8,12},{12,8},{16,20},{20,16},{24,28},{28,24},{1,5},{5... | collective-permute-start | bytes 196616 | tf_op jit(solution)/shard_map/ppermute | solution.py:21
  51.4 5.5 %collective-permute-start.12 = (f32[32,512]{1,0:T(8,128)S(1)}, f32[32,512]{1,0:T(8,128)S(1)}, u32[]{:S(2)}, u32[]{:S(2)}) collective-permute-start(f32[32,512]{1,0:T(8,128)S(1)} %dynamic-slice_bitcast_fusion.2), channel_id=1, source_target_pairs={{0,2},{1,3},{2,0},{3,1},{4,6},{5,7},{6,4},{7,5},{8,10},{9,11},{10,... | collective-permute-start | bytes 196616 | tf_op jit(solution)/shard_map/ppermute | solution.py:21
  56.9 4.5 %collective-permute-start.13 = (f32[32,512]{1,0:T(8,128)S(1)}, f32[32,512]{1,0:T(8,128)S(1)}, u32[]{:S(2)}, u32[]{:S(2)}) collective-permute-start(f32[32,512]{1,0:T(8,128)S(1)} %bitcast_add_fusion.3), channel_id=1, source_target_pairs={{0,16},{4,20},{8,24},{12,28},{16,0},{20,4},{24,8},{28,12},{1,17},{... | collective-permute-start | bytes 196616 | tf_op jit(solution)/shard_map/ppermute | solution.py:21
  58.5 4.3 %collective-permute-start.17 = (f32[2,8,512]{2,1,0:T(8,128)S(1)}, f32[2,8,512]{2,1,0:T(8,128)S(1)}, u32[]{:S(2)}, u32[]{:S(2)}) collective-permute-start(f32[2,8,512]{2,1,0:T(8,128)S(1)} %dynamic-slice_bitcast_fusion.3), channel_id=1, source_target_pairs={{0,8},{4,12},{8,0},{12,4},{16,24},{20,28},{24,16},{28,20},{1,9},{5... | collective-permute-start | bytes 98312 | tf_op jit(solution)/shard_map/ppermute | solution.py:21
  61.5 5.0 %collective-permute-start.14 = (f32[2,32,512]{2,1,0:T(8,128)S(1)}, f32[2,32,512]{2,1,0:T(8,128)S(1)}, u32[]{:S(2)}, u32[]{:S(2)}) collective-permute-start(f32[2,32,512]{2,1,0:T(8,128)S(1)} %pad_maximum_fusion.5), channel_id=1, source_target_pairs={{0,8},{4,12},{8,0},{12,4},{16,24},{20,28},{24,16},{28,20},{1,9},{5... | collective-permute-start | bytes 393224 | tf_op jit(solution)/shard_map/ppermute | solution.py:21
  62.9 3.8 %collective-permute-start.18 = (f32[8,512]{1,0:T(8,128)S(1)}, f32[8,512]{1,0:T(8,128)S(1)}, u32[]{:S(2)}, u32[]{:S(2)}) collective-permute-start(f32[8,512]{1,0:T(8,128)S(1)} %dynamic-slice_bitcast_fusion.4), channel_id=1, source_target_pairs={{0,16},{4,20},{8,24},{12,28},{16,0},{20,4},{24,8},{28,12},{1,17},{... | collective-permute-start | bytes 49160 | tf_op jit(solution)/shard_map/ppermute | solution.py:21
  66.5 9.4 %collective-permute-start.15 = (f32[2,2,32,512]{3,2,0,1:T(8,128)S(1)}, f32[2,2,32,512]{3,2,0,1:T(8,128)S(1)}, u32[]{:S(2)}, u32[]{:S(2)}) collective-permute-start(f32[2,2,32,512]{3,2,0,1:T(8,128)S(1)} %pad_maximum_fusion.4), channel_id=1, source_target_pairs={{0,4},{4,0},{8,12},{12,8},{16,20},{20,16},{24,28},{28,24},{1,5},{5... | collective-permute-start | bytes 786440 | tf_op jit(solution)/shard_map/ppermute | solution.py:21
  66.7 3.8 %collective-permute-start.19 = (f32[8,512]{1,0:T(8,128)S(1)}, f32[8,512]{1,0:T(8,128)S(1)}, u32[]{:S(2)}, u32[]{:S(2)}) collective-permute-start(f32[8,512]{1,0:T(8,128)S(1)} %bitcast_add_fusion.5), channel_id=1, source_target_pairs={{0,1},{1,0},{2,3},{3,2},{4,5},{5,4},{6,7},{7,6},{8,9},{9,8},{10,11... | collective-permute-start | bytes 49160 | tf_op jit(solution)/shard_map/ppermute | solution.py:21
  70.5 4.9 %collective-permute-start.20 = (f32[8,512]{1,0:T(8,128)S(1)}, f32[8,512]{1,0:T(8,128)S(1)}, u32[]{:S(2)}, u32[]{:S(2)}) collective-permute-start(f32[8,512]{1,0:T(8,128)S(1)} %add.167), channel_id=1, source_target_pairs={{0,2},{1,3},{2,0},{3,1},{4,6},{5,7},{6,4},{7,5},{8,10},{9,11},{10,... | collective-permute-start | bytes 49160 | tf_op jit(solution)/shard_map/ppermute | solution.py:21

commit v5 on v3

--- a/solution.py
+++ b/solution.py
@@ -21,34 +21,53 @@
     return lax.ppermute(value, axis, [(i, i ^ (1 << bit)) for i in range(count)])
 
 
-def scatter_sum(value, axis, at, order, other=None):
+def exchange(sends, axis, pairs):
+    width = sends[0].shape[-1]
+    flat = jnp.concatenate([x.reshape(-1, width) for x in sends], axis=0)
+    flat = lax.ppermute(flat, axis, pairs)
+    got, start = [], 0
+    for x in sends:
+        size = x.size // width
+        got.append(flat[start : start + size].reshape(x.shape))
+        start += size
+    return got
+
+
+def scatter_sum(values, axis, ats, order, other=None, riders=()):
     count = lax.axis_size(axis)
     levels = log2(count)
     me = lax.axis_index(axis)
     other = order if other is None else other
     first = (me & 1) == 0
-    shape = value.shape
-    value = value.reshape(shape[:at] + (2,) * levels + shape[at + 1 :])
+    values = [
+        v.reshape(v.shape[:at] + (2,) * levels + v.shape[at + 1 :]) for v, at in zip(values, ats)
+    ]
+    riders = list(riders)
     held = [[levels - 1 - k for k in range(levels)] for _ in range(2)]
     for bit, bit_b in zip(order, other):
-        parts = []
+        dims = []
         for group, b in enumerate((bit, bit_b)):
-            dim = at + held[group].index(b)
-            mine = (me >> b) & 1
-            keep = lax.dynamic_index_in_dim(value, mine, axis=dim, keepdims=False)
-            send = lax.dynamic_index_in_dim(value, 1 - mine, axis=dim, keepdims=False)
-            parts.append((keep, send))
+            dims.append(held[group].index(b))
             held[group].remove(b)
-        if bit == bit_b:
-            keep, send = parts[0]
-            value = keep + swap(send, axis, bit)
-        else:
-            keep = jnp.where(first, parts[0][0], parts[1][0])
-            send = jnp.where(first, parts[0][1], parts[1][1])
-            pairs = [(i, i ^ (1 << (bit if i & 1 == 0 else bit_b))) for i in range(count)]
-            value = keep + lax.ppermute(send, axis, pairs)
-    assert held[0] == held[1] or levels == 0
-    return value
+        keeps, sends = [], []
+        for v, at in zip(values, ats):
+            parts = []
+            for b, dim in zip((bit, bit_b), dims):
+                mine = (me >> b) & 1
+                keep = lax.dynamic_index_in_dim(v, mine, axis=at + dim, keepdims=False)
+                send = lax.dynamic_index_in_dim(v, 1 - mine, axis=at + dim, keepdims=False)
+                parts.append((keep, send))
+            if bit == bit_b:
+                keeps.append(parts[0][0])
+                sends.append(parts[0][1])
+            else:
+                keeps.append(jnp.where(first, parts[0][0], parts[1][0]))
+                sends.append(jnp.where(first, parts[0][1], parts[1][1]))
+        pairs = [(i, i ^ (1 << (bit if i & 1 == 0 else bit_b))) for i in range(count)]
+        got = exchange(sends + riders, axis, pairs)
+        values = [k + g for k, g in zip(keeps, got)]
+        riders = [r + g for r, g in zip(riders, got[len(keeps) :])]
+    return values, riders
 
 
 def gather_ordered(value, axis, order):
@@ -67,12 +86,6 @@
     natural = [held.index(levels - 1 - k) for k in range(levels)]
     value = jnp.transpose(value, natural + list(range(levels, levels + len(rest))))
     return value.reshape((count,) + rest)
-
-
-def sum_all(value, axis):
-    for bit in range(log2(lax.axis_size(axis))):
-        value = value + swap(value, axis, bit)
-    return value
 
 
 def on_device(feats, hub_feats, hub_ids, tile_src, tile_mask, w_stack, cotangent):
@@ -113,16 +126,19 @@
     partial_w = lax.dot_general(inputs, dz, (((0,), (0,)), ((), ())), preferred_element_type=jnp.float32)
     span = partial_w.shape[0] // (doms * regions)
     partial_w = partial_w.reshape(doms, regions, span, width)
-    region_w = scatter_sum(partial_w, "region", 1, up, up[:1] + up[1:][::-1])
-    piece_w = scatter_sum(region_w, "dom", 0, list(range(log2(doms))))
-    weight_grad = gather_ordered(piece_w, "region", down).reshape(regions * span, width)
     dagg = lax.dot_general(
         dz, w_stack[width:], (((1,), (1,)), ((), ())), preferred_element_type=jnp.float32
     )
     sgrad = (dagg / deg[:, None]).astype(jnp.bfloat16)
     partial_h = lax.dot_general(counts, sgrad, (((0,), (0,)), ((), ())), preferred_element_type=jnp.float32)
     partial_h = partial_h.reshape(regions, owned, width)
-    hub_grad = sum_all(scatter_sum(partial_h, "region", 0, up), "dom")
+    (region_w, region_h), _ = scatter_sum(
+        [partial_w, partial_h], "region", [1, 0], up, up[:1] + up[1:][::-1]
+    )
+    (piece_w,), (hub_grad,) = scatter_sum(
+        [region_w], "dom", [0], list(range(log2(doms))), riders=[region_h]
+    )
+    weight_grad = gather_ordered(piece_w, "region", down).reshape(regions * span, width)
     return (activ, weight_grad, hub_grad)
 
 

time: 71.1 us -> 69.4 us (0.976)
  starting transfers between devices: 23.6 us -> 17.3 us
  matrix products: 4.89 us -> 7.05 us
  other arithmetic: 4.73 us -> 5.94 us
    ppermute x14 -> x6, starting transfers between devices: 17.9 us -> 6.88 us  [swap(): return lax.ppermute(value, axis, [(i, i ^ 1 << bit) for i in range(count)])]
    ppermute x2 -> x5, waiting for transfers between devices: 13.5 us -> 23 us  [exchange(): flat = lax.ppermute(flat, axis, pairs)]
    ppermute x14 -> x6, waiting for transfers between devices: 19 us -> 10 us  [swap(): return lax.ppermute(value, axis, [(i, i ^ 1 << bit) for i in range(count)])]
    ppermute x2 -> x5, starting transfers between devices: 2.13 us -> 6.9 us  [exchange(): flat = lax.ppermute(flat, axis, pairs)]
    concatenate x0 -> x5, other arithmetic: none -> 1.19 us  [exchange(): flat = jnp.concatenate([x.reshape(-1, width) for x in sends], axis=0)]
    dot_general x1, matrix products: 0.68 us -> 1.78 us  [on_device(): lax.dot_general(counts, sgrad, (((0,), (0,)), ((), ())), preferred_elemen...]
    dot_general x1, matrix products: 0.7 us -> 1.75 us  [on_device(): lax.dot_general(inputs, dz, (((0,), (0,)), ((), ())), preferred_element_t...]
  transfers between devices with their start and end apart: 17 -> 12, of which waited for: 11 -> 9; matrix products, arithmetic and copies ran while one was open for 11% -> 10% of each run, Pallas kernels for 0% -> 0%
where the time goes in v5:
time: 69.4 us; the launch traced here: 69.1 us
  waiting for transfers between devices  33 us (48%)
  starting transfers between devices  17.3 us (25%)
  matrix products  7.05 us (10%)
  other arithmetic  5.94 us (9%)
  local copies, waits for them, and re-layouts  4.77 us (7%)
  between operations  1.12 us (2%)
    ppermute x5, waiting for transfers between devices, exchange(): flat = lax.ppermute(flat, axis, pairs)  23 us
    ppermute x6, waiting for transfers between devices, swap(): return lax.ppermute(value, axis, [(i, i ^ 1 << bit) for i in range(count)])  10 us
    ppermute x5, starting transfers between devices, exchange(): flat = lax.ppermute(flat, axis, pairs)  6.9 us
    ppermute x6, starting transfers between devices, swap(): return lax.ppermute(value, axis, [(i, i ^ 1 << bit) for i in range(count)])  6.88 us
    ppermute x1, starting transfers between devices, shifted(): lax.ppermute(value, axis, [(source, source + steps) for source in range(i...  3.49 us
    dot_general x1, matrix products, on_device(): z = jnp.dot(inputs, w_stack, preferred_element_type=jnp.float32)  1.92 us
    reduce_sum x1, other arithmetic, on_device(): links = jnp.where(chosen[:, :, None, :, None], masks, 0).sum(axis=1)  1.88 us
    dot_general x1, matrix products, on_device(): lax.dot_general(counts, sgrad, (((0,), (0,)), ((), ())), preferred_elemen...  1.78 us
  transfers between devices with their start and end apart: 12, of which 9 were waited for; matrix products, arithmetic and copies ran while one was open for 10% of the time, Pallas kernels for 0%

profile of v5, /device:TPU:0, one launch (start us, length us, event | category | flops | bytes accessed | tf_op | source)
XLA Modules:
  0.0 69.1 jit_solution(15183691106047293338)
XLA Ops:
  0.6 0.0 copy-start.6
  0.6 0.0 copy-start.1
  0.7 0.0 copy-start
  0.7 0.0 copy-start.5
  0.7 3.1 %collective-permute-start.1 = (bf16[8,512]{1,0:T(8,128)(2,1)}, bf16[8,512]{1,0:T(8,128)(2,1)S(1)}, u32[]{:S(2)}, u32[]{:S(2)}) collective-permute-start(bf16[8,512]{1,0:T(8,128)(2,1)} %param.8), channel_id=1, source_target_pairs={{0,16},{4,20},{8,24},{12,28},{16,0},{20,4},{24,8},{28,12},{1,17},{... | collective-permute-start | bytes 24584 | tf_op jit(solution)/shard_map/ppermute | solution.py:21
  3.7 0.9 %slice.48 = bf16[128,512]{1,0:T(8,128)(2,1)S(1)} slice(bf16[512,512]{1,0:T(8,128)(2,1)} %param.7), slice={[384:512], [0:512]} | slice | bytes 262144 | tf_op jit(solution)/shard_map/slice | solution.py:103
  4.6 3.5 %collective-permute-start = (bf16[128,512]{1,0:T(8,128)(2,1)S(1)}, bf16[128,512]{1,0:T(8,128)(2,1)S(1)}, u32[]{:S(2)}, u32[]{:S(2)}) collective-permute-start(bf16[128,512]{1,0:T(8,128)(2,1)S(1)} %slice.48), channel_id=1, source_target_pairs={{0,1},{1,2},{2,3},{4,5},{5,6},{6,7},{8,9},{9,10},{10,11},{12,13},{... | collective-permute-start | bytes 393224 | tf_op jit(solution)/shard_map/ppermute | solution.py:10
  8.1 0.7 %eq.69 = s32[4,4]{1,0:T(4,128)S(1)} reshape(s32[16]{0:T(128)} %param.10) | data formatting | bytes 128 | tf_op jit(solution)/shard_map/eq | solution.py:107
  8.9 0.1 iota_compare_fusion.4
  9.0 1.9 %select_reduce_fusion = s32[4,128,5,128]{3,1,2,0:T(8,128)S(1)} fusion(s32[4,4,128,128]{3,2,1,0:T(8,128)} %bitcast.111, pred[4,4,5]{2,1,0:T(4,128)(4,1)S(1)} %iota_compare_fusion.4), kind=kLoop, calls=%fused_computation | loop fusion | flops 2293760 | bytes 2359376 | tf_op jit(solution)/shard_map/reduce_sum | solution.py:109
  10.9 0.0 collective-permute-done.1
  10.9 0.0 copy-done.6
  10.9 1.6 %collective-permute-start.2 = (bf16[2,8,512]{2,1,0:T(8,128)(2,1)S(1)}, bf16[2,8,512]{2,1,0:T(8,128)(2,1)S(1)}, u32[]{:S(2)}, u32[]{:S(2)}) collective-permute-start(bf16[2,8,512]{2,1,0:T(8,128)(2,1)S(1)} %pad_maximum_fusion.13), channel_id=1, source_target_pairs={{0,8},{4,12},{8,0},{12,4},{16,24},{20,28},{24,16},{28,20},{1,9},{5... | collective-permute-start | bytes 49160 | tf_op jit(solution)/shard_map/ppermute | solution.py:21
  12.5 0.0 copy-done.5
  12.5 0.0 copy-done
  12.5 0.3 reduce_sum.26
  12.9 1.8 %collective-permute-done.2 = bf16[2,8,512]{2,1,0:T(8,128)(2,1)S(1)} collective-permute-done((bf16[2,8,512]{2,1,0:T(8,128)(2,1)S(1)}, bf16[2,8,512]{2,1,0:T(8,128)(2,1)S(1)}, u32[]{:S(2)}, u32[]{:S(2)}) %collective-permute-start.2) | collective-permute-done | bytes 16416 | tf_op jit(solution)/shard_map/ppermute | solution.py:21
  14.7 0.1 collective-permute-start.3
  14.8 0.0 copy-done.1
  14.8 0.2 copy.28
  15.0 0.1 convert_element_type.48
  15.2 0.9 %copy.25 = bf16[4,128,5,128]{1,0,3,2:T(4,128)(2,1)S(1)} copy(bf16[4,128,5,128]{3,1,2,0:T(8,128)(2,1)S(1)} %convert_element_type.48) | data formatting | bytes 1310720 | tf_op jit(solution)/shard_map/convert_element_type | solution.py:111
  16.1 0.0 collective-permute-done.3
  16.2 0.9 %fusion.16 = f32[512,512]{0,1:T(8,128)S(1)} fusion(bf16[64,512]{1,0:T(8,128)(2,1)S(1)} %bitcast.120, s32[512]{0:T(512)S(1)} %bitcast.130, s32[512]{0:T(512)S(1)} %bitcast.132, s32[512]{0:T(512)S(1)} %bitcast.128, s32[512]{0:T(512)S(1)} %bitcast.126), kind=kOutput, calls=%fused_computation.44 | convolution fusion | flops 33947648 | bytes 1122304 | tf_op jit(solution)/shard_map/dot_general | solution.py:119
  17.1 0.0 collective-permute-done
  17.1 0.0 copy-start.7
  17.1 0.0 copy-start.8
  17.2 0.7 fusion.2
  17.8 0.5 copy-done.7
  18.4 0.1 copy-done.8
  18.5 0.0 copy-start.2
  18.5 1.9 %multiply_convert_fusion = (bf16[512,512]{1,0:T(8,128)(2,1)S(1)}, bf16[512,512]{1,0:T(8,128)(2,1)}) fusion(bf16[512,512]{1,0:T(8,128)(2,1)S(1)} %copy-done.8, bf16[1024,512]{1,0:T(8,128)(2,1)S(1)} %copy-done.7, bf16[512,512]{0,1:T(8,128)(2,1)S(1)} %fusion.2, bf16[512,512]{0,1:T(8,128)(2,1)S(1)} %copy.28), kind=kOutput, calls=%fused_computation.11 | convolution fusion | flops 542113792 | bytes 3670016 | tf_op jit(solution)/shard_map/dot_general | solution.py:122
  20.4 0.0 copy-done.2
  20.4 0.8 %copy-done.4 = bf16[512,512]{1,0:T(8,128)(2,1)} copy-done((bf16[512,512]{1,0:T(8,128)(2,1)}, bf16[512,512]{1,0:T(8,128)(2,1)S(1)}, u32[]{:S(2)}) %copy-start.4) | copy-done | bytes 524312
  21.2 1.8 %fusion.4 = f32[64,512]{1,0:T(8,128)S(1)} fusion(bf16[512,512]{1,0:T(8,128)(2,1)S(1)} %get-tuple-element.7, bf16[1024,512]{1,0:T(8,128)(2,1)} %param.12, f32[512]{0:T(512)S(1)} %add_bitcast_fusion, s32[512]{0:T(512)S(1)} %bitcast.131, s32[512]{0:T(512)S(1)} %bitcast.133, s32[512]{0:T(512)S(1)} %bitcast.129, s32[512]{0:T(512)S(1)} %bitcast.127), kind=kOutput, calls=%fused_computation.7 | convolution fusion | flops 302907392 | bytes 1189888 | tf_op jit(solution)/shard_map/dot_general | solution.py:133
  23.0 0.0 copy-done.3
  23.0 1.7 %fusion.5 = f32[1024,512]{1,0:T(8,128)S(1)} fusion(bf16[512,512]{1,0:T(8,128)(2,1)} %copy-done.4, bf16[512,512]{0,1:T(8,128)(2,1)S(1)} %copy-done.3, bf16[512,512]{0,1:T(8,128)(2,1)S(1)} %copy.28), kind=kOutput, calls=%fused_computation.14 | convolution fusion | flops 538968064 | bytes 3670016 | tf_op jit(solution)/shard_map/dot_general | solution.py:126
  24.8 0.1 constant_dynamic-slice_fusion.6
  24.9 1.1 %pad_maximum_fusion = f32[544,512]{1,0:T(8,128)} fusion(f32[32,512]{1,0:T(8,128)S(1)} %bitcast.121, f32[512,512]{1,0:T(8,128)S(1)} %bitcast.109), kind=kLoop, calls=%fused_computation.8 | loop fusion | flops 278528 | bytes 2228224 | tf_op jit(solution)/shard_map/concatenate | solution.py:26
  26.0 0.5 collective-permute-start.4
  26.5 2.6 %collective-permute-done.4 = f32[544,512]{1,0:T(8,128)S(1)} collective-permute-done((f32[544,512]{1,0:T(8,128)}, f32[544,512]{1,0:T(8,128)S(1)}, u32[]{:S(2)}, u32[]{:S(2)}) %collective-permute-start.4) | collective-permute-done | bytes 1114144 | tf_op jit(solution)/shard_map/ppermute | solution.py:27
  29.1 0.1 slice.64
  29.2 0.2 bitcast_add_fusion
  29.4 0.1 constant_dynamic-slice_fusion.3
  29.5 0.1 constant_dynamic-slice_fusion.4
  29.6 0.1 bitcast_select_fusion
  29.7 1.6 %collective-permute-start.5 = (f32[272,512]{1,0:T(8,128)S(1)}, f32[272,512]{1,0:T(8,128)S(1)}, u32[]{:S(2)}, u32[]{:S(2)}) collective-permute-start(f32[272,512]{1,0:T(8,128)S(1)} %pad_maximum_fusion.4), channel_id=1, source_target_pairs={{0,8},{4,20},{8,0},{12,28},{16,24},{20,4},{24,16},{28,12},{1,9},{5... | collective-permute-start | bytes 1671176 | tf_op jit(solution)/shard_map/ppermute | solution.py:27
  31.3 8.0 %collective-permute-done.5 = f32[272,512]{1,0:T(8,128)S(1)} collective-permute-done((f32[272,512]{1,0:T(8,128)S(1)}, f32[272,512]{1,0:T(8,128)S(1)}, u32[]{:S(2)}, u32[]{:S(2)}) %collective-permute-start.5) | collective-permute-done | bytes 557088 | tf_op jit(solution)/shard_map/ppermute | solution.py:27
  39.4 0.1 fusion.12
  39.6 0.1 dynamic-slice_select_fusion.1
  39.7 0.6 collective-permute-start.6
  40.3 6.0 %collective-permute-done.6 = f32[136,512]{1,0:T(8,128)S(1)} collective-permute-done((f32[136,512]{1,0:T(8,128)S(1)}, f32[136,512]{1,0:T(8,128)S(1)}, u32[]{:S(2)}, u32[]{:S(2)}) %collective-permute-start.6) | collective-permute-done | bytes 278560 | tf_op jit(solution)/shard_map/ppermute | solution.py:27
  46.5 1.6 %collective-permute-start.7 = (f32[72,512]{1,0:T(8,128)S(1)}, f32[72,512]{1,0:T(8,128)S(1)}, u32[]{:S(2)}, u32[]{:S(2)}) collective-permute-start(f32[72,512]{1,0:T(8,128)S(1)} %pad_maximum_fusion.8), channel_id=1, source_target_pairs={{0,1},{1,0},{2,3},{3,2},{4,5},{5,4},{6,7},{7,6},{8,9},{9,8},{10,11... | collective-permute-start | bytes 442376 | tf_op jit(solution)/shard_map/ppermute | solution.py:27
  48.1 3.6 %collective-permute-done.7 = f32[72,512]{1,0:T(8,128)S(1)} collective-permute-done((f32[72,512]{1,0:T(8,128)S(1)}, f32[72,512]{1,0:T(8,128)S(1)}, u32[]{:S(2)}, u32[]{:S(2)}) %collective-permute-start.7) | collective-permute-done | bytes 147488 | tf_op jit(solution)/shard_map/ppermute | solution.py:27
  51.8 2.7 %collective-permute-start.8 = (f32[40,512]{1,0:T(8,128)S(1)}, f32[40,512]{1,0:T(8,128)S(1)}, u32[]{:S(2)}, u32[]{:S(2)}) collective-permute-start(f32[40,512]{1,0:T(8,128)S(1)} %pad_maximum_fusion.10), channel_id=1, source_target_pairs={{0,2},{1,3},{2,0},{3,1},{4,6},{5,7},{6,4},{7,5},{8,10},{9,11},{10,... | collective-permute-start | bytes 245768 | tf_op jit(solution)/shard_map/ppermute | solution.py:27
  54.4 2.7 %collective-permute-done.8 = f32[40,512]{1,0:T(8,128)S(1)} collective-permute-done((f32[40,512]{1,0:T(8,128)S(1)}, f32[40,512]{1,0:T(8,128)S(1)}, u32[]{:S(2)}, u32[]{:S(2)}) %collective-permute-start.8) | collective-permute-done | bytes 81952 | tf_op jit(solution)/shard_map/ppermute | solution.py:27
  57.2 0.6 collective-permute-start.9
  57.8 3.8 %collective-permute-done.9 = f32[32,512]{1,0:T(8,128)S(1)} collective-permute-done((f32[32,512]{1,0:T(8,128)S(1)}, f32[32,512]{1,0:T(8,128)S(1)}, u32[]{:S(2)}, u32[]{:S(2)}) %collective-permute-start.9) | collective-permute-done | bytes 65568 | tf_op jit(solution)/shard_map/ppermute | solution.py:21
  61.6 1.6 %collective-permute-start.10 = (f32[2,32,512]{2,1,0:T(8,128)S(1)}, f32[2,32,512]{2,1,0:T(8,128)S(1)}, u32[]{:S(2)}, u32[]{:S(2)}) collective-permute-start(f32[2,32,512]{2,1,0:T(8,128)S(1)} %pad_maximum_fusion.9), channel_id=1, source_target_pairs={{0,8},{4,12},{8,0},{12,4},{16,24},{20,28},{24,16},{28,20},{1,9},{5... | collective-permute-start | bytes 393224 | tf_op jit(solution)/shard_map/ppermute | solution.py:21
  63.1 3.5 %collective-permute-done.10 = f32[2,32,512]{2,1,0:T(8,128)S(1)} collective-permute-done((f32[2,32,512]{2,1,0:T(8,128)S(1)}, f32[2,32,512]{2,1,0:T(8,128)S(1)}, u32[]{:S(2)}, u32[]{:S(2)}) %collective-permute-start.10) | collective-permute-done | bytes 131104 | tf_op jit(solution)/shard_map/ppermute | solution.py:21
  66.6 0.1 collective-permute-start.11
  66.7 0.6 slice_add_fusion.1
  67.3 0.9 %collective-permute-done.11 = f32[2,2,32,512]{3,2,0,1:T(8,128)S(1)} collective-permute-done((f32[2,2,32,512]{3,2,0,1:T(8,128)S(1)}, f32[2,2,32,512]{3,2,0,1:T(8,128)S(1)}, u32[]{:S(2)}, u32[]{:S(2)}) %collective-permute-start.11) | collective-permute-done | bytes 262176 | tf_op jit(solution)/shard_map/ppermute | solution.py:21
  68.3 0.8 %pad_maximum_fusion.5 = f32[2,2,2,32,512]{4,3,0,1,2:T(8,128)} fusion(f32[1,2,2,32,512]{4,3,0,1,2:T(8,128)S(1)} %get-tuple-element.10, f32[1,2,2,32,512]{4,3,0,1,2:T(8,128)S(1)} %get-tuple-element.9), kind=kLoop, calls=%fused_computation.22 | loop fusion | flops 131072 | bytes 1048576 | tf_op jit(solution)/shard_map/stack | solution.py:84
  (36 shorter events, 0.5 us)
Async XLA Ops:
  0.6 10.2 %copy-start.6 = (bf16[8,512]{1,0:T(8,128)(2,1)S(1)}, bf16[8,512]{1,0:T(8,128)(2,1)}, u32[]{:S(2)}) copy-start(bf16[8,512]{1,0:T(8,128)(2,1)} %param.8) | copy-start | bytes 24580
  0.6 14.2 %copy-start.1 = (bf16[512,512]{1,0:T(8,128)(2,1)S(1)}, bf16[512,512]{1,0:T(8,128)(2,1)}, u32[]{:S(2)}) copy-start(bf16[512,512]{1,0:T(8,128)(2,1)} %param.7) | copy-start | bytes 1572868
  0.7 11.8 %copy-start = (s32[16,128,128]{2,1,0:T(8,128)S(1)}, s32[16,128,128]{2,1,0:T(8,128)}, u32[]{:S(2)}) copy-start(s32[16,128,128]{2,1,0:T(8,128)} %param.11) | copy-start | bytes 3145732
  0.7 11.8 %copy-start.5 = (s32[512,4]{0,1:T(4,128)S(1)}, s32[512,4]{0,1:T(4,128)}, u32[]{:S(2)}) copy-start(s32[512,4]{0,1:T(4,128)} %param.9) | copy-start | bytes 24580
  0.7 10.2 %collective-permute-start.1 = (bf16[8,512]{1,0:T(8,128)(2,1)}, bf16[8,512]{1,0:T(8,128)(2,1)S(1)}, u32[]{:S(2)}, u32[]{:S(2)}) collective-permute-start(bf16[8,512]{1,0:T(8,128)(2,1)} %param.8), channel_id=1, source_target_pairs={{0,16},{4,20},{8,24},{12,28},{16,0},{20,4},{24,8},{28,12},{1,17},{... | collective-permute-start | bytes 24584 | tf_op jit(solution)/shard_map/ppermute | solution.py:21
  4.6 12.5 %collective-permute-start = (bf16[128,512]{1,0:T(8,128)(2,1)S(1)}, bf16[128,512]{1,0:T(8,128)(2,1)S(1)}, u32[]{:S(2)}, u32[]{:S(2)}) collective-permute-start(bf16[128,512]{1,0:T(8,128)(2,1)S(1)} %slice.48), channel_id=1, source_target_pairs={{0,1},{1,2},{2,3},{4,5},{5,6},{6,7},{8,9},{9,10},{10,11},{12,13},{... | collective-permute-start | bytes 393224 | tf_op jit(solution)/shard_map/ppermute | solution.py:10
  10.9 3.8 %collective-permute-start.2 = (bf16[2,8,512]{2,1,0:T(8,128)(2,1)S(1)}, bf16[2,8,512]{2,1,0:T(8,128)(2,1)S(1)}, u32[]{:S(2)}, u32[]{:S(2)}) collective-permute-start(bf16[2,8,512]{2,1,0:T(8,128)(2,1)S(1)} %pad_maximum_fusion.13), channel_id=1, source_target_pairs={{0,8},{4,12},{8,0},{12,4},{16,24},{20,28},{24,16},{28,20},{1,9},{5... | collective-permute-start | bytes 49160 | tf_op jit(solution)/shard_map/ppermute | solution.py:21
  14.7 1.4 %collective-permute-start.3 = (bf16[2,2,8,512]{3,2,0,1:T(8,128)(2,1)S(1)}, bf16[2,2,8,512]{3,2,0,1:T(8,128)(2,1)S(1)}, u32[]{:S(2)}, u32[]{:S(2)}) collective-permute-start(bf16[2,2,8,512]{3,2,0,1:T(8,128)(2,1)S(1)} %pad_maximum_fusion.12), channel_id=1, source_target_pairs={{0,4},{4,0},{8,12},{12,8},{16,20},{20,16},{24,28},{28,24},{1,5},{5... | collective-permute-start | bytes 98312 | tf_op jit(solution)/shard_map/ppermute | solution.py:21
  17.1 1.2 %copy-start.7 = (bf16[1024,512]{1,0:T(8,128)(2,1)S(1)}, bf16[1024,512]{1,0:T(8,128)(2,1)}, u32[]{:S(2)}) copy-start(bf16[1024,512]{1,0:T(8,128)(2,1)} %param.12) | copy-start | bytes 3145732
  17.1 1.3 %copy-start.8 = (bf16[512,512]{1,0:T(8,128)(2,1)S(1)}, bf16[512,512]{1,0:T(8,128)(2,1)}, u32[]{:S(2)}) copy-start(bf16[512,512]{1,0:T(8,128)(2,1)} %param.13) | copy-start | bytes 1572868
  18.5 1.9 %copy-start.2 = (bf16[512,512]{0,1:T(8,128)(2,1)}, bf16[512,512]{0,1:T(8,128)(2,1)S(1)}, u32[]{:S(2)}) copy-start(bf16[512,512]{0,1:T(8,128)(2,1)S(1)} %fusion.2) | copy-start | bytes 1572868
  20.4 0.8 %copy-start.4 = (bf16[512,512]{1,0:T(8,128)(2,1)}, bf16[512,512]{1,0:T(8,128)(2,1)S(1)}, u32[]{:S(2)}) copy-start(bf16[512,512]{1,0:T(8,128)(2,1)S(1)} %get-tuple-element.7) | copy-start | bytes 1572868
  21.2 1.8 %copy-start.3 = (bf16[512,512]{0,1:T(8,128)(2,1)S(1)}, bf16[512,512]{0,1:T(8,128)(2,1)}, u32[]{:S(2)}) copy-start(bf16[512,512]{0,1:T(8,128)(2,1)} %copy-done.2) | copy-start | bytes 1572868
  26.0 3.1 %collective-permute-start.4 = (f32[544,512]{1,0:T(8,128)}, f32[544,512]{1,0:T(8,128)S(1)}, u32[]{:S(2)}, u32[]{:S(2)}) collective-permute-start(f32[544,512]{1,0:T(8,128)} %pad_maximum_fusion), channel_id=1, source_target_pairs={{0,4},{4,0},{8,12},{12,8},{16,20},{20,16},{24,28},{28,24},{1,5},{5... | collective-permute-start | bytes 3342344 | tf_op jit(solution)/shard_map/ppermute | solution.py:27
  29.7 9.6 %collective-permute-start.5 = (f32[272,512]{1,0:T(8,128)S(1)}, f32[272,512]{1,0:T(8,128)S(1)}, u32[]{:S(2)}, u32[]{:S(2)}) collective-permute-start(f32[272,512]{1,0:T(8,128)S(1)} %pad_maximum_fusion.4), channel_id=1, source_target_pairs={{0,8},{4,20},{8,0},{12,28},{16,24},{20,4},{24,16},{28,12},{1,9},{5... | collective-permute-start | bytes 1671176 | tf_op jit(solution)/shard_map/ppermute | solution.py:27
  39.7 6.6 %collective-permute-start.6 = (f32[136,512]{1,0:T(8,128)S(1)}, f32[136,512]{1,0:T(8,128)S(1)}, u32[]{:S(2)}, u32[]{:S(2)}) collective-permute-start(f32[136,512]{1,0:T(8,128)S(1)} %pad_maximum_fusion.6), channel_id=1, source_target_pairs={{0,16},{4,12},{8,24},{12,4},{16,0},{20,28},{24,8},{28,20},{1,17},{... | collective-permute-start | bytes 835592 | tf_op jit(solution)/shard_map/ppermute | solution.py:27
  46.5 5.2 %collective-permute-start.7 = (f32[72,512]{1,0:T(8,128)S(1)}, f32[72,512]{1,0:T(8,128)S(1)}, u32[]{:S(2)}, u32[]{:S(2)}) collective-permute-start(f32[72,512]{1,0:T(8,128)S(1)} %pad_maximum_fusion.8), channel_id=1, source_target_pairs={{0,1},{1,0},{2,3},{3,2},{4,5},{5,4},{6,7},{7,6},{8,9},{9,8},{10,11... | collective-permute-start | bytes 442376 | tf_op jit(solution)/shard_map/ppermute | solution.py:27
  51.8 5.4 %collective-permute-start.8 = (f32[40,512]{1,0:T(8,128)S(1)}, f32[40,512]{1,0:T(8,128)S(1)}, u32[]{:S(2)}, u32[]{:S(2)}) collective-permute-start(f32[40,512]{1,0:T(8,128)S(1)} %pad_maximum_fusion.10), channel_id=1, source_target_pairs={{0,2},{1,3},{2,0},{3,1},{4,6},{5,7},{6,4},{7,5},{8,10},{9,11},{10,... | collective-permute-start | bytes 245768 | tf_op jit(solution)/shard_map/ppermute | solution.py:27
  57.2 4.3 %collective-permute-start.9 = (f32[32,512]{1,0:T(8,128)S(1)}, f32[32,512]{1,0:T(8,128)S(1)}, u32[]{:S(2)}, u32[]{:S(2)}) collective-permute-start(f32[32,512]{1,0:T(8,128)S(1)} %slice_add_fusion), channel_id=1, source_target_pairs={{0,16},{4,20},{8,24},{12,28},{16,0},{20,4},{24,8},{28,12},{1,17},{... | collective-permute-start | bytes 196616 | tf_op jit(solution)/shard_map/ppermute | solution.py:21
  61.6 5.0 %collective-permute-start.10 = (f32[2,32,512]{2,1,0:T(8,128)S(1)}, f32[2,32,512]{2,1,0:T(8,128)S(1)}, u32[]{:S(2)}, u32[]{:S(2)}) collective-permute-start(f32[2,32,512]{2,1,0:T(8,128)S(1)} %pad_maximum_fusion.9), channel_id=1, source_target_pairs={{0,8},{4,12},{8,0},{12,4},{16,24},{20,28},{24,16},{28,20},{1,9},{5... | collective-permute-start | bytes 393224 | tf_op jit(solution)/shard_map/ppermute | solution.py:21
  66.6 1.6 %collective-permute-start.11 = (f32[2,2,32,512]{3,2,0,1:T(8,128)S(1)}, f32[2,2,32,512]{3,2,0,1:T(8,128)S(1)}, u32[]{:S(2)}, u32[]{:S(2)}) collective-permute-start(f32[2,2,32,512]{3,2,0,1:T(8,128)S(1)} %pad_maximum_fusion.7), channel_id=1, source_target_pairs={{0,4},{4,0},{8,12},{12,8},{16,20},{20,16},{24,28},{28,24},{1,5},{5... | collective-permute-start | bytes 786440 | tf_op jit(solution)/shard_map/ppermute | solution.py:21

commit v6 on v5

--- a/solution.py
+++ b/solution.py
@@ -33,29 +33,30 @@
     return got
 
 
-def scatter_sum(values, axis, ats, order, other=None, riders=()):
+def scatter_sum(values, axis, ats, order, other=None, riders=(), joins=None):
     count = lax.axis_size(axis)
     levels = log2(count)
     me = lax.axis_index(axis)
     other = order if other is None else other
+    joins = [0] * len(values) if joins is None else joins
     first = (me & 1) == 0
     values = [
         v.reshape(v.shape[:at] + (2,) * levels + v.shape[at + 1 :]) for v, at in zip(values, ats)
     ]
     riders = list(riders)
-    held = [[levels - 1 - k for k in range(levels)] for _ in range(2)]
-    for bit, bit_b in zip(order, other):
-        dims = []
-        for group, b in enumerate((bit, bit_b)):
-            dims.append(held[group].index(b))
-            held[group].remove(b)
+    held = [[[levels - 1 - k for k in range(levels)] for _ in range(2)] for _ in values]
+    for step, (bit, bit_b) in enumerate(zip(order, other)):
+        active = [i for i in range(len(values)) if joins[i] <= step]
         keeps, sends = [], []
-        for v, at in zip(values, ats):
+        for i in active:
+            v, at = values[i], ats[i]
             parts = []
-            for b, dim in zip((bit, bit_b), dims):
+            for group, b in enumerate((bit, bit_b)):
+                dim = at + held[i][group].index(b)
+                held[i][group].remove(b)
                 mine = (me >> b) & 1
-                keep = lax.dynamic_index_in_dim(v, mine, axis=at + dim, keepdims=False)
-                send = lax.dynamic_index_in_dim(v, 1 - mine, axis=at + dim, keepdims=False)
+                keep = lax.dynamic_index_in_dim(v, mine, axis=dim, keepdims=False)
+                send = lax.dynamic_index_in_dim(v, 1 - mine, axis=dim, keepdims=False)
                 parts.append((keep, send))
             if bit == bit_b:
                 keeps.append(parts[0][0])
@@ -65,27 +66,34 @@
                 sends.append(jnp.where(first, parts[0][1], parts[1][1]))
         pairs = [(i, i ^ (1 << (bit if i & 1 == 0 else bit_b))) for i in range(count)]
         got = exchange(sends + riders, axis, pairs)
-        values = [k + g for k, g in zip(keeps, got)]
+        for i, k, g in zip(active, keeps, got):
+            values[i] = k + g
         riders = [r + g for r, g in zip(riders, got[len(keeps) :])]
     return values, riders
 
 
-def gather_ordered(value, axis, order):
+def gather_ordered(value, axis, order, rider=None):
     count = lax.axis_size(axis)
     levels = log2(count)
     me = lax.axis_index(axis)
     rest = value.shape
     held = []
     for bit in order:
-        other = swap(value, axis, bit)
-        mine = ((me >> bit) & 1) == 0
-        low = jnp.where(mine, value, other)
-        high = jnp.where(mine, other, value)
+        mine = (me >> bit) & 1
+        if rider is not None and bit == 0:
+            keep = lax.dynamic_index_in_dim(rider, mine, axis=0, keepdims=False)
+            send = lax.dynamic_index_in_dim(rider, 1 - mine, axis=0, keepdims=False)
+            other, got = exchange([value, send], axis, [(i, i ^ 1) for i in range(count)])
+            rider = keep + got
+        else:
+            other = swap(value, axis, bit)
+        low = jnp.where(mine == 0, value, other)
+        high = jnp.where(mine == 0, other, value)
         value = jnp.stack([low, high], axis=0)
         held.insert(0, bit)
     natural = [held.index(levels - 1 - k) for k in range(levels)]
     value = jnp.transpose(value, natural + list(range(levels, levels + len(rest))))
-    return value.reshape((count,) + rest)
+    return value.reshape((count,) + rest), rider
 
 
 def on_device(feats, hub_feats, hub_ids, tile_src, tile_mask, w_stack, cotangent):
@@ -101,7 +109,7 @@
     up = list(range(log2(regions)))
     down = up[::-1]
     prev = shifted(feats[rows - tile :], "dom", 1)
-    hub_table = gather_ordered(hub_feats, "region", down).reshape(total_hubs, width)
+    hub_table = gather_ordered(hub_feats, "region", down)[0].reshape(total_hubs, width)
     window = jnp.concatenate([prev, feats], axis=0)
     src = tile_src.reshape(nblk, per_block)
     chosen = src[:, :, None] == lax.broadcasted_iota(jnp.int32, (nblk, per_block, nblk + 1), 2)
@@ -133,12 +141,13 @@
     partial_h = lax.dot_general(counts, sgrad, (((0,), (0,)), ((), ())), preferred_element_type=jnp.float32)
     partial_h = partial_h.reshape(regions, owned, width)
     (region_w, region_h), _ = scatter_sum(
-        [partial_w, partial_h], "region", [1, 0], up, up[:1] + up[1:][::-1]
+        [partial_w, partial_h], "region", [1, 0], up, up[:1] + up[1:][::-1], joins=[0, 1]
     )
-    (piece_w,), (hub_grad,) = scatter_sum(
+    (piece_w,), (region_h,) = scatter_sum(
         [region_w], "dom", [0], list(range(log2(doms))), riders=[region_h]
     )
-    weight_grad = gather_ordered(piece_w, "region", down).reshape(regions * span, width)
+    weight_grad, hub_grad = gather_ordered(piece_w, "region", down, region_h)
+    weight_grad = weight_grad.reshape(regions * span, width)
     return (activ, weight_grad, hub_grad)
 
 

time: 69.4 us -> 67.2 us (0.968)
  matrix products: 7.05 us -> 6.08 us
  waiting for transfers between devices: 33 us -> 32.3 us
    add x8, other arithmetic: 0.5 us -> 2.3 us  [the longest x7 1.69 us: scatter_sum(): values[i] = k + g]
    concatenate x5, other arithmetic: 1.19 us -> 0.1 us  [exchange(): flat = jnp.concatenate([x.reshape(-1, width) for x in sends], axis=0)]
    dot_general x1, matrix products: 1.75 us -> 0.7 us  [on_device(): lax.dot_general(inputs, dz, (((0,), (0,)), ((), ())), preferred_element_t...]
    ppermute x6 -> x5, waiting for transfers between devices: 10 us -> 9.05 us  [swap(): return lax.ppermute(value, axis, [(i, i ^ 1 << bit) for i in range(count)])]
    another operation x12 -> x10, other arithmetic: 1.01 us -> 0.15 us  [gather_ordered(): value = jnp.stack([low, high], axis=0)]
    transpose x0 -> x1, local copies, waits for them, and re-layouts: none -> 0.84 us  [gather_ordered(): jnp.transpose(value, natural + list(range(levels, levels + len(rest))))]
    unnamed x19 -> x15, local copies, waits for them, and re-layouts: 1.7 us -> 0.91 us
    ppermute x5 -> x6, waiting for transfers between devices: 23 us -> 23.3 us  [exchange(): flat = lax.ppermute(flat, axis, pairs)]
  transfers between devices with their start and end apart: 12 -> 12, of which waited for: 9 -> 9; matrix products, arithmetic and copies ran while one was open for 10% -> 12% of each run, Pallas kernels for 0% -> 0%
where the time goes in v6:
time: 67.2 us; the launch traced here: 66.9 us
  waiting for transfers between devices  32.3 us (48%)
  starting transfers between devices  17.4 us (26%)
  matrix products  6.08 us (9%)
  other arithmetic  5.28 us (8%)
  local copies, waits for them, and re-layouts  4.68 us (7%)
  between operations  1.14 us (2%)
    ppermute x6, waiting for transfers between devices, exchange(): flat = lax.ppermute(flat, axis, pairs)  23.3 us
    ppermute x5, waiting for transfers between devices, swap(): return lax.ppermute(value, axis, [(i, i ^ 1 << bit) for i in range(count)])  9.05 us
    ppermute x6, starting transfers between devices, exchange(): flat = lax.ppermute(flat, axis, pairs)  7.05 us
    ppermute x5, starting transfers between devices, swap(): return lax.ppermute(value, axis, [(i, i ^ 1 << bit) for i in range(count)])  6.82 us
    ppermute x1, starting transfers between devices, shifted(): lax.ppermute(value, axis, [(source, source + steps) for source in range(i...  3.49 us
    dot_general x1, matrix products, on_device(): z = jnp.dot(inputs, w_stack, preferred_element_type=jnp.float32)  1.9 us
    dot_general x1, matrix products, on_device(): lax.dot_general(counts, sgrad, (((0,), (0,)), ((), ())), preferred_elemen...  1.88 us
    reduce_sum x1, other arithmetic, on_device(): links = jnp.where(chosen[:, :, None, :, None], masks, 0).sum(axis=1)  1.88 us
  transfers between devices with their start and end apart: 12, of which 9 were waited for; matrix products, arithmetic and copies ran while one was open for 12% of the time, Pallas kernels for 0%

profile of v6, /device:TPU:0, one launch (start us, length us, event | category | flops | bytes accessed | tf_op | source)
XLA Modules:
  0.0 66.9 jit_solution(2624905616109980529)
XLA Ops:
  0.6 0.0 copy-start.4
  0.6 0.0 copy-start.1
  0.7 0.0 copy-start
  0.7 0.0 copy-start.3
  0.7 3.1 %collective-permute-start.1 = (bf16[8,512]{1,0:T(8,128)(2,1)}, bf16[8,512]{1,0:T(8,128)(2,1)S(1)}, u32[]{:S(2)}, u32[]{:S(2)}) collective-permute-start(bf16[8,512]{1,0:T(8,128)(2,1)} %param.8), channel_id=1, source_target_pairs={{0,16},{4,20},{8,24},{12,28},{16,0},{20,4},{24,8},{28,12},{1,17},{... | collective-permute-start | bytes 24584 | tf_op jit(solution)/shard_map/ppermute | solution.py:21
  3.7 0.9 %slice.48 = bf16[128,512]{1,0:T(8,128)(2,1)S(1)} slice(bf16[512,512]{1,0:T(8,128)(2,1)} %param.7), slice={[384:512], [0:512]} | slice | bytes 262144 | tf_op jit(solution)/shard_map/slice | solution.py:111
  4.6 3.5 %collective-permute-start = (bf16[128,512]{1,0:T(8,128)(2,1)S(1)}, bf16[128,512]{1,0:T(8,128)(2,1)S(1)}, u32[]{:S(2)}, u32[]{:S(2)}) collective-permute-start(bf16[128,512]{1,0:T(8,128)(2,1)S(1)} %slice.48), channel_id=1, source_target_pairs={{0,1},{1,2},{2,3},{4,5},{5,6},{6,7},{8,9},{9,10},{10,11},{12,13},{... | collective-permute-start | bytes 393224 | tf_op jit(solution)/shard_map/ppermute | solution.py:10
  8.1 0.7 %eq.75 = s32[4,4]{1,0:T(4,128)S(1)} reshape(s32[16]{0:T(128)} %param.10) | data formatting | bytes 128 | tf_op jit(solution)/shard_map/eq | solution.py:115
  8.9 0.1 iota_compare_fusion.4
  9.0 1.9 %select_reduce_fusion = s32[4,128,5,128]{3,1,2,0:T(8,128)S(1)} fusion(s32[4,4,128,128]{3,2,1,0:T(8,128)} %bitcast.120, pred[4,4,5]{2,1,0:T(4,128)(4,1)S(1)} %iota_compare_fusion.4), kind=kLoop, calls=%fused_computation | loop fusion | flops 2293760 | bytes 2359376 | tf_op jit(solution)/shard_map/reduce_sum | solution.py:117
  10.9 0.0 collective-permute-done.1
  10.9 0.0 copy-done.4
  10.9 1.6 %collective-permute-start.2 = (bf16[2,8,512]{2,1,0:T(8,128)(2,1)S(1)}, bf16[2,8,512]{2,1,0:T(8,128)(2,1)S(1)}, u32[]{:S(2)}, u32[]{:S(2)}) collective-permute-start(bf16[2,8,512]{2,1,0:T(8,128)(2,1)S(1)} %pad_maximum_fusion.13), channel_id=1, source_target_pairs={{0,8},{4,12},{8,0},{12,4},{16,24},{20,28},{24,16},{28,20},{1,9},{5... | collective-permute-start | bytes 49160 | tf_op jit(solution)/shard_map/ppermute | solution.py:21
  12.5 0.0 copy-done.3
  12.5 0.0 copy-done
  12.5 0.3 reduce_sum.26
  12.9 1.8 %collective-permute-done.2 = bf16[2,8,512]{2,1,0:T(8,128)(2,1)S(1)} collective-permute-done((bf16[2,8,512]{2,1,0:T(8,128)(2,1)S(1)}, bf16[2,8,512]{2,1,0:T(8,128)(2,1)S(1)}, u32[]{:S(2)}, u32[]{:S(2)}) %collective-permute-start.2) | collective-permute-done | bytes 16416 | tf_op jit(solution)/shard_map/ppermute | solution.py:21
  14.7 0.1 collective-permute-start.3
  14.8 0.0 copy-done.1
  14.8 0.2 copy.30
  15.0 0.1 convert_element_type.48
  15.2 0.9 %copy.27 = bf16[4,128,5,128]{1,0,3,2:T(4,128)(2,1)S(1)} copy(bf16[4,128,5,128]{3,1,2,0:T(8,128)(2,1)S(1)} %convert_element_type.48) | data formatting | bytes 1310720 | tf_op jit(solution)/shard_map/convert_element_type | solution.py:119
  16.1 0.0 collective-permute-done.3
  16.2 0.9 %fusion.18 = f32[512,512]{0,1:T(8,128)S(1)} fusion(bf16[64,512]{1,0:T(8,128)(2,1)S(1)} %bitcast.135, s32[512]{0:T(512)S(1)} %bitcast.142, s32[512]{0:T(512)S(1)} %bitcast.144, s32[512]{0:T(512)S(1)} %bitcast.140, s32[512]{0:T(512)S(1)} %bitcast.138), kind=kOutput, calls=%fused_computation.44 | convolution fusion | flops 33947648 | bytes 1122304 | tf_op jit(solution)/shard_map/dot_general | solution.py:127
  17.1 0.0 collective-permute-done
  17.1 0.0 copy-start.5
  17.1 0.0 copy-start.6
  17.2 0.7 fusion.2
  17.8 0.5 copy-done.5
  18.4 0.1 copy-done.6
  18.5 1.9 %multiply_convert_fusion = (bf16[512,512]{1,0:T(8,128)(2,1)S(1)}, bf16[512,512]{1,0:T(8,128)(2,1)}) fusion(bf16[512,512]{1,0:T(8,128)(2,1)S(1)} %copy-done.6, bf16[1024,512]{1,0:T(8,128)(2,1)S(1)} %copy-done.5, bf16[512,512]{0,1:T(8,128)(2,1)S(1)} %fusion.2, bf16[512,512]{0,1:T(8,128)(2,1)S(1)} %copy.30), kind=kOutput, calls=%fused_computation.10 | convolution fusion | flops 542113792 | bytes 3670016 | tf_op jit(solution)/shard_map/dot_general | solution.py:130
  20.4 0.0 copy-start.2
  20.4 0.7 %fusion.5 = f32[1024,512]{1,0:T(8,128)S(1)} fusion(bf16[512,512]{1,0:T(8,128)(2,1)S(1)} %get-tuple-element.3, bf16[512,512]{0,1:T(8,128)(2,1)S(1)} %fusion.2, bf16[512,512]{0,1:T(8,128)(2,1)S(1)} %copy.30), kind=kOutput, calls=%fused_computation.13 | convolution fusion | flops 538968064 | bytes 3670016 | tf_op jit(solution)/shard_map/dot_general | solution.py:134
  21.1 0.1 constant_dynamic-slice_fusion.5
  21.2 0.0 copy-done.2
  21.2 0.6 collective-permute-start.4
  21.8 1.9 %fusion.4 = f32[64,512]{1,0:T(8,128)S(1)} fusion(bf16[512,512]{1,0:T(8,128)(2,1)} %copy-done.2, bf16[1024,512]{1,0:T(8,128)(2,1)} %param.12, f32[512]{0:T(512)S(1)} %add_bitcast_fusion, s32[512]{0:T(512)S(1)} %bitcast.143, s32[512]{0:T(512)S(1)} %bitcast.145, s32[512]{0:T(512)S(1)} %bitcast.141, s32[512]{0:T(512)S(1)} %bitcast.139), kind=kOutput, calls=%fused_computation.7 | convolution fusion | flops 302907392 | bytes 1189888 | tf_op jit(solution)/shard_map/dot_general | solution.py:141
  23.7 0.5 collective-permute-done.4
  24.2 1.4 %bitcast_add_fusion = f32[4,2,2,32,512]{4,3,2,1,0:T(8,128)S(1)} fusion(f32[4,2,2,32,512]{4,3,2,1,0:T(8,128)} %bitcast.20, f32[4,2,2,2,32,512]{5,4,3,2,1,0:T(8,128)S(1)} %bitcast.119, s32[]{:T(128)S(6)} %select_n.233), kind=kLoop, calls=%fused_computation.9 | loop fusion | flops 262144 | bytes 3145732 | tf_op jit(solution)/shard_map/add | solution.py:70
  25.7 0.1 bitcast_select_fusion
  25.8 1.6 %collective-permute-start.5 = (f32[288,512]{1,0:T(8,128)S(1)}, f32[288,512]{1,0:T(8,128)S(1)}, u32[]{:S(2)}, u32[]{:S(2)}) collective-permute-start(f32[288,512]{1,0:T(8,128)S(1)} %pad_maximum_fusion.3), channel_id=1, source_target_pairs={{0,8},{4,20},{8,0},{12,28},{16,24},{20,4},{24,16},{28,12},{1,9},{5... | collective-permute-start | bytes 1769480 | tf_op jit(solution)/shard_map/ppermute | solution.py:27
  27.4 8.4 %collective-permute-done.5 = f32[288,512]{1,0:T(8,128)S(1)} collective-permute-done((f32[288,512]{1,0:T(8,128)S(1)}, f32[288,512]{1,0:T(8,128)S(1)}, u32[]{:S(2)}, u32[]{:S(2)}) %collective-permute-start.5) | collective-permute-done | bytes 589856 | tf_op jit(solution)/shard_map/ppermute | solution.py:27
  35.9 0.2 fusion.12
  36.0 0.1 dynamic-slice_select_fusion.1
  36.2 0.6 collective-permute-start.6
  36.7 6.2 %collective-permute-done.6 = f32[144,512]{1,0:T(8,128)S(1)} collective-permute-done((f32[144,512]{1,0:T(8,128)S(1)}, f32[144,512]{1,0:T(8,128)S(1)}, u32[]{:S(2)}, u32[]{:S(2)}) %collective-permute-start.6) | collective-permute-done | bytes 294944 | tf_op jit(solution)/shard_map/ppermute | solution.py:27
  43.1 1.6 %collective-permute-start.7 = (f32[80,512]{1,0:T(8,128)S(1)}, f32[80,512]{1,0:T(8,128)S(1)}, u32[]{:S(2)}, u32[]{:S(2)}) collective-permute-start(f32[80,512]{1,0:T(8,128)S(1)} %pad_maximum_fusion.8), channel_id=1, source_target_pairs={{0,1},{1,0},{2,3},{3,2},{4,5},{5,4},{6,7},{7,6},{8,9},{9,8},{10,11... | collective-permute-start | bytes 491528 | tf_op jit(solution)/shard_map/ppermute | solution.py:27
  44.7 3.8 %collective-permute-done.7 = f32[80,512]{1,0:T(8,128)S(1)} collective-permute-done((f32[80,512]{1,0:T(8,128)S(1)}, f32[80,512]{1,0:T(8,128)S(1)}, u32[]{:S(2)}, u32[]{:S(2)}) %collective-permute-start.7) | collective-permute-done | bytes 163872 | tf_op jit(solution)/shard_map/ppermute | solution.py:27
  48.6 2.7 %collective-permute-start.8 = (f32[48,512]{1,0:T(8,128)S(1)}, f32[48,512]{1,0:T(8,128)S(1)}, u32[]{:S(2)}, u32[]{:S(2)}) collective-permute-start(f32[48,512]{1,0:T(8,128)S(1)} %pad_maximum_fusion.10), channel_id=1, source_target_pairs={{0,2},{1,3},{2,0},{3,1},{4,6},{5,7},{6,4},{7,5},{8,10},{9,11},{10,... | collective-permute-start | bytes 294920 | tf_op jit(solution)/shard_map/ppermute | solution.py:27
  51.2 2.9 %collective-permute-done.8 = f32[48,512]{1,0:T(8,128)S(1)} collective-permute-done((f32[48,512]{1,0:T(8,128)S(1)}, f32[48,512]{1,0:T(8,128)S(1)}, u32[]{:S(2)}, u32[]{:S(2)}) %collective-permute-start.8) | collective-permute-done | bytes 98336 | tf_op jit(solution)/shard_map/ppermute | solution.py:27
  54.2 0.6 collective-permute-start.9
  54.7 3.8 %collective-permute-done.9 = f32[32,512]{1,0:T(8,128)S(1)} collective-permute-done((f32[32,512]{1,0:T(8,128)S(1)}, f32[32,512]{1,0:T(8,128)S(1)}, u32[]{:S(2)}, u32[]{:S(2)}) %collective-permute-start.9) | collective-permute-done | bytes 65568 | tf_op jit(solution)/shard_map/ppermute | solution.py:21
  58.5 1.6 %collective-permute-start.10 = (f32[2,32,512]{2,1,0:T(8,128)S(1)}, f32[2,32,512]{2,1,0:T(8,128)S(1)}, u32[]{:S(2)}, u32[]{:S(2)}) collective-permute-start(f32[2,32,512]{2,1,0:T(8,128)S(1)} %pad_maximum_fusion.9), channel_id=1, source_target_pairs={{0,8},{4,12},{8,0},{12,4},{16,24},{20,28},{24,16},{28,20},{1,9},{5... | collective-permute-start | bytes 393224 | tf_op jit(solution)/shard_map/ppermute | solution.py:21
  60.1 3.4 %collective-permute-done.10 = f32[2,32,512]{2,1,0:T(8,128)S(1)} collective-permute-done((f32[2,32,512]{2,1,0:T(8,128)S(1)}, f32[2,32,512]{2,1,0:T(8,128)S(1)}, u32[]{:S(2)}, u32[]{:S(2)}) %collective-permute-start.10) | collective-permute-done | bytes 131104 | tf_op jit(solution)/shard_map/ppermute | solution.py:21
  63.6 0.1 fusion.21
  63.7 0.1 collective-permute-start.11
  63.8 1.5 %collective-permute-done.11 = f32[136,512]{1,0:T(8,128)S(1)} collective-permute-done((f32[136,512]{1,0:T(8,128)S(1)}, f32[136,512]{1,0:T(8,128)S(1)}, u32[]{:S(2)}, u32[]{:S(2)}) %collective-permute-start.11) | collective-permute-done | bytes 278560 | tf_op jit(solution)/shard_map/ppermute | solution.py:27
  65.4 0.8 %copy.32 = f32[2,2,2,32,512]{4,3,2,1,0:T(8,128)} copy(f32[2,2,2,32,512]{4,3,0,1,2:T(8,128)S(1)} %maximum_bitcast_fusion) | data formatting | bytes 1048576 | tf_op jit(solution)/shard_map/transpose | solution.py:95
  66.3 0.6 slice_add_fusion.2
  (40 shorter events, 0.7 us)
Async XLA Ops:
  0.6 10.2 %copy-start.4 = (bf16[8,512]{1,0:T(8,128)(2,1)S(1)}, bf16[8,512]{1,0:T(8,128)(2,1)}, u32[]{:S(2)}) copy-start(bf16[8,512]{1,0:T(8,128)(2,1)} %param.8) | copy-start | bytes 24580
  0.6 14.2 %copy-start.1 = (bf16[512,512]{1,0:T(8,128)(2,1)S(1)}, bf16[512,512]{1,0:T(8,128)(2,1)}, u32[]{:S(2)}) copy-start(bf16[512,512]{1,0:T(8,128)(2,1)} %param.7) | copy-start | bytes 1572868
  0.7 11.8 %copy-start = (s32[16,128,128]{2,1,0:T(8,128)S(1)}, s32[16,128,128]{2,1,0:T(8,128)}, u32[]{:S(2)}) copy-start(s32[16,128,128]{2,1,0:T(8,128)} %param.11) | copy-start | bytes 3145732
  0.7 11.8 %copy-start.3 = (s32[512,4]{0,1:T(4,128)S(1)}, s32[512,4]{0,1:T(4,128)}, u32[]{:S(2)}) copy-start(s32[512,4]{0,1:T(4,128)} %param.9) | copy-start | bytes 24580
  0.7 10.2 %collective-permute-start.1 = (bf16[8,512]{1,0:T(8,128)(2,1)}, bf16[8,512]{1,0:T(8,128)(2,1)S(1)}, u32[]{:S(2)}, u32[]{:S(2)}) collective-permute-start(bf16[8,512]{1,0:T(8,128)(2,1)} %param.8), channel_id=1, source_target_pairs={{0,16},{4,20},{8,24},{12,28},{16,0},{20,4},{24,8},{28,12},{1,17},{... | collective-permute-start | bytes 24584 | tf_op jit(solution)/shard_map/ppermute | solution.py:21
  4.6 12.5 %collective-permute-start = (bf16[128,512]{1,0:T(8,128)(2,1)S(1)}, bf16[128,512]{1,0:T(8,128)(2,1)S(1)}, u32[]{:S(2)}, u32[]{:S(2)}) collective-permute-start(bf16[128,512]{1,0:T(8,128)(2,1)S(1)} %slice.48), channel_id=1, source_target_pairs={{0,1},{1,2},{2,3},{4,5},{5,6},{6,7},{8,9},{9,10},{10,11},{12,13},{... | collective-permute-start | bytes 393224 | tf_op jit(solution)/shard_map/ppermute | solution.py:10
  10.9 3.8 %collective-permute-start.2 = (bf16[2,8,512]{2,1,0:T(8,128)(2,1)S(1)}, bf16[2,8,512]{2,1,0:T(8,128)(2,1)S(1)}, u32[]{:S(2)}, u32[]{:S(2)}) collective-permute-start(bf16[2,8,512]{2,1,0:T(8,128)(2,1)S(1)} %pad_maximum_fusion.13), channel_id=1, source_target_pairs={{0,8},{4,12},{8,0},{12,4},{16,24},{20,28},{24,16},{28,20},{1,9},{5... | collective-permute-start | bytes 49160 | tf_op jit(solution)/shard_map/ppermute | solution.py:21
  14.7 1.4 %collective-permute-start.3 = (bf16[2,2,8,512]{3,2,0,1:T(8,128)(2,1)S(1)}, bf16[2,2,8,512]{3,2,0,1:T(8,128)(2,1)S(1)}, u32[]{:S(2)}, u32[]{:S(2)}) collective-permute-start(bf16[2,2,8,512]{3,2,0,1:T(8,128)(2,1)S(1)} %pad_maximum_fusion.12), channel_id=1, source_target_pairs={{0,4},{4,0},{8,12},{12,8},{16,20},{20,16},{24,28},{28,24},{1,5},{5... | collective-permute-start | bytes 98312 | tf_op jit(solution)/shard_map/ppermute | solution.py:21
  17.1 1.2 %copy-start.5 = (bf16[1024,512]{1,0:T(8,128)(2,1)S(1)}, bf16[1024,512]{1,0:T(8,128)(2,1)}, u32[]{:S(2)}) copy-start(bf16[1024,512]{1,0:T(8,128)(2,1)} %param.12) | copy-start | bytes 3145732
  17.1 1.3 %copy-start.6 = (bf16[512,512]{1,0:T(8,128)(2,1)S(1)}, bf16[512,512]{1,0:T(8,128)(2,1)}, u32[]{:S(2)}) copy-start(bf16[512,512]{1,0:T(8,128)(2,1)} %param.13) | copy-start | bytes 1572868
  20.4 0.8 %copy-start.2 = (bf16[512,512]{1,0:T(8,128)(2,1)}, bf16[512,512]{1,0:T(8,128)(2,1)S(1)}, u32[]{:S(2)}) copy-start(bf16[512,512]{1,0:T(8,128)(2,1)S(1)} %get-tuple-element.3) | copy-start | bytes 1572868
  21.2 3.0 %collective-permute-start.4 = (f32[512,512]{1,0:T(8,128)S(1)}, f32[512,512]{1,0:T(8,128)}, u32[]{:S(2)}, u32[]{:S(2)}) collective-permute-start(f32[512,512]{1,0:T(8,128)S(1)} %bitcast.122), channel_id=1, source_target_pairs={{0,4},{4,0},{8,12},{12,8},{16,20},{20,16},{24,28},{28,24},{1,5},{5... | collective-permute-start | bytes 3145736 | tf_op jit(solution)/shard_map/ppermute | solution.py:27
  25.8 9.9 %collective-permute-start.5 = (f32[288,512]{1,0:T(8,128)S(1)}, f32[288,512]{1,0:T(8,128)S(1)}, u32[]{:S(2)}, u32[]{:S(2)}) collective-permute-start(f32[288,512]{1,0:T(8,128)S(1)} %pad_maximum_fusion.3), channel_id=1, source_target_pairs={{0,8},{4,20},{8,0},{12,28},{16,24},{20,4},{24,16},{28,12},{1,9},{5... | collective-permute-start | bytes 1769480 | tf_op jit(solution)/shard_map/ppermute | solution.py:27
  36.2 6.8 %collective-permute-start.6 = (f32[144,512]{1,0:T(8,128)S(1)}, f32[144,512]{1,0:T(8,128)S(1)}, u32[]{:S(2)}, u32[]{:S(2)}) collective-permute-start(f32[144,512]{1,0:T(8,128)S(1)} %pad_maximum_fusion.4), channel_id=1, source_target_pairs={{0,16},{4,12},{8,24},{12,4},{16,0},{20,28},{24,8},{28,20},{1,17},{... | collective-permute-start | bytes 884744 | tf_op jit(solution)/shard_map/ppermute | solution.py:27
  43.1 5.4 %collective-permute-start.7 = (f32[80,512]{1,0:T(8,128)S(1)}, f32[80,512]{1,0:T(8,128)S(1)}, u32[]{:S(2)}, u32[]{:S(2)}) collective-permute-start(f32[80,512]{1,0:T(8,128)S(1)} %pad_maximum_fusion.8), channel_id=1, source_target_pairs={{0,1},{1,0},{2,3},{3,2},{4,5},{5,4},{6,7},{7,6},{8,9},{9,8},{10,11... | collective-permute-start | bytes 491528 | tf_op jit(solution)/shard_map/ppermute | solution.py:27
  48.6 5.6 %collective-permute-start.8 = (f32[48,512]{1,0:T(8,128)S(1)}, f32[48,512]{1,0:T(8,128)S(1)}, u32[]{:S(2)}, u32[]{:S(2)}) collective-permute-start(f32[48,512]{1,0:T(8,128)S(1)} %pad_maximum_fusion.10), channel_id=1, source_target_pairs={{0,2},{1,3},{2,0},{3,1},{4,6},{5,7},{6,4},{7,5},{8,10},{9,11},{10,... | collective-permute-start | bytes 294920 | tf_op jit(solution)/shard_map/ppermute | solution.py:27
  54.2 4.3 %collective-permute-start.9 = (f32[32,512]{1,0:T(8,128)S(1)}, f32[32,512]{1,0:T(8,128)S(1)}, u32[]{:S(2)}, u32[]{:S(2)}) collective-permute-start(f32[32,512]{1,0:T(8,128)S(1)} %slice_add_fusion), channel_id=1, source_target_pairs={{0,16},{4,20},{8,24},{12,28},{16,0},{20,4},{24,8},{28,12},{1,17},{... | collective-permute-start | bytes 196616 | tf_op jit(solution)/shard_map/ppermute | solution.py:21
  58.5 5.0 %collective-permute-start.10 = (f32[2,32,512]{2,1,0:T(8,128)S(1)}, f32[2,32,512]{2,1,0:T(8,128)S(1)}, u32[]{:S(2)}, u32[]{:S(2)}) collective-permute-start(f32[2,32,512]{2,1,0:T(8,128)S(1)} %pad_maximum_fusion.9), channel_id=1, source_target_pairs={{0,8},{4,12},{8,0},{12,4},{16,24},{20,28},{24,16},{28,20},{1,9},{5... | collective-permute-start | bytes 393224 | tf_op jit(solution)/shard_map/ppermute | solution.py:21
  63.7 1.6 %collective-permute-start.11 = (f32[136,512]{1,0:T(8,128)S(1)}, f32[136,512]{1,0:T(8,128)S(1)}, u32[]{:S(2)}, u32[]{:S(2)}) collective-permute-start(f32[136,512]{1,0:T(8,128)S(1)} %pad_maximum_fusion.5), channel_id=1, source_target_pairs={{0,4},{4,0},{8,12},{12,8},{16,20},{20,16},{24,28},{28,24},{1,5},{5... | collective-permute-start | bytes 835592 | tf_op jit(solution)/shard_map/ppermute | solution.py:27

commit v7 on v6

--- a/solution.py
+++ b/solution.py
@@ -21,10 +21,12 @@
     return lax.ppermute(value, axis, [(i, i ^ (1 << bit)) for i in range(count)])
 
 
-def exchange(sends, axis, pairs):
+def exchange(sends, axis, pairs, wire=None):
     width = sends[0].shape[-1]
     flat = jnp.concatenate([x.reshape(-1, width) for x in sends], axis=0)
-    flat = lax.ppermute(flat, axis, pairs)
+    kind = flat.dtype
+    flat = flat if wire is None else flat.astype(wire)
+    flat = lax.ppermute(flat, axis, pairs).astype(kind)
     got, start = [], 0
     for x in sends:
         size = x.size // width
@@ -33,7 +35,7 @@
     return got
 
 
-def scatter_sum(values, axis, ats, order, other=None, riders=(), joins=None):
+def scatter_sum(values, axis, ats, order, other=None, riders=(), joins=None, wires=None):
     count = lax.axis_size(axis)
     levels = log2(count)
     me = lax.axis_index(axis)
@@ -65,35 +67,49 @@
                 keeps.append(jnp.where(first, parts[0][0], parts[1][0]))
                 sends.append(jnp.where(first, parts[0][1], parts[1][1]))
         pairs = [(i, i ^ (1 << (bit if i & 1 == 0 else bit_b))) for i in range(count)]
-        got = exchange(sends + riders, axis, pairs)
+        got = exchange(sends + riders, axis, pairs, None if wires is None else wires[step])
         for i, k, g in zip(active, keeps, got):
             values[i] = k + g
         riders = [r + g for r, g in zip(riders, got[len(keeps) :])]
     return values, riders
 
 
-def gather_ordered(value, axis, order, rider=None):
+def gather_ordered(value, axis, order, rider=None, other=None):
     count = lax.axis_size(axis)
     levels = log2(count)
     me = lax.axis_index(axis)
+    other = order if other is None else other
+    first = (me & 1) == 0
     rest = value.shape
-    held = []
-    for bit in order:
-        mine = (me >> bit) & 1
+    held = [[], []]
+    for bit, bit_b in zip(order, other):
+        if bit == bit_b and held[0] != held[1]:
+            swapped = [held[1].index(b) for b in held[0]]
+            tail = list(range(len(swapped), value.ndim))
+            value = jnp.where(first, value, jnp.transpose(value, swapped + tail))
+            held[1] = list(held[0])
+        pairs = [(i, i ^ (1 << (bit if i & 1 == 0 else bit_b))) for i in range(count)]
         if rider is not None and bit == 0:
+            mine = me & 1
             keep = lax.dynamic_index_in_dim(rider, mine, axis=0, keepdims=False)
             send = lax.dynamic_index_in_dim(rider, 1 - mine, axis=0, keepdims=False)
-            other, got = exchange([value, send], axis, [(i, i ^ 1) for i in range(count)])
-            rider = keep + got
+            got, got_rider = exchange([value, send], axis, pairs)
+            rider = keep + got_rider
         else:
-            other = swap(value, axis, bit)
-        low = jnp.where(mine == 0, value, other)
-        high = jnp.where(mine == 0, other, value)
+            got = lax.ppermute(value, axis, pairs)
+        mine = jnp.where(first, (me >> bit) & 1, (me >> bit_b) & 1)
+        low = jnp.where(mine == 0, value, got)
+        high = jnp.where(mine == 0, got, value)
         value = jnp.stack([low, high], axis=0)
-        held.insert(0, bit)
-    natural = [held.index(levels - 1 - k) for k in range(levels)]
-    value = jnp.transpose(value, natural + list(range(levels, levels + len(rest))))
-    return value.reshape((count,) + rest), rider
+        held[0].insert(0, bit)
+        held[1].insert(0, bit_b)
+    tail = list(range(levels, levels + len(rest)))
+    ways = []
+    for group in range(2):
+        natural = [held[group].index(levels - 1 - k) for k in range(levels)]
+        ways.append(jnp.transpose(value, natural + tail).reshape((count,) + rest))
+    value = ways[0] if held[0] == held[1] else jnp.where(first, ways[0], ways[1])
+    return value, rider
 
 
 def on_device(feats, hub_feats, hub_ids, tile_src, tile_mask, w_stack, cotangent):
@@ -141,12 +157,16 @@
     partial_h = lax.dot_general(counts, sgrad, (((0,), (0,)), ((), ())), preferred_element_type=jnp.float32)
     partial_h = partial_h.reshape(regions, owned, width)
     (region_w, region_h), _ = scatter_sum(
-        [partial_w, partial_h], "region", [1, 0], up, up[:1] + up[1:][::-1], joins=[0, 1]
+        [partial_w, partial_h], "region", [1, 0], up, up[:1] + up[1:][::-1], joins=[0, 1],
+        wires=None,
     )
     (piece_w,), (region_h,) = scatter_sum(
-        [region_w], "dom", [0], list(range(log2(doms))), riders=[region_h]
+        [region_w], "dom", [0], list(range(log2(doms))), riders=[region_h],
+        wires=None,
     )
-    weight_grad, hub_grad = gather_ordered(piece_w, "region", down, region_h)
+    weight_grad, hub_grad = gather_ordered(
+        piece_w, "region", down, region_h, down[:-1][::-1] + down[-1:]
+    )
     weight_grad = weight_grad.reshape(regions * span, width)
     return (activ, weight_grad, hub_grad)
 

time: 67.2 us -> 67.5 us (level)
  no operation moved by 1% of the time
where the time goes in v7:
time: 67.5 us; the launch traced here: 67.2 us
  waiting for transfers between devices  32.7 us (48%)
  starting transfers between devices  17.3 us (26%)
  matrix products  6.09 us (9%)
  other arithmetic  5.28 us (8%)
  local copies, waits for them, and re-layouts  4.68 us (7%)
  between operations  1.15 us (2%)
    ppermute x6, waiting for transfers between devices, exchange(): flat = lax.ppermute(flat, axis, pairs).astype(kind)  23.3 us
    ppermute x5, waiting for transfers between devices, gather_ordered(): got = lax.ppermute(value, axis, pairs)  9.37 us
    ppermute x6, starting transfers between devices, exchange(): flat = lax.ppermute(flat, axis, pairs).astype(kind)  7.03 us
    ppermute x5, starting transfers between devices, gather_ordered(): got = lax.ppermute(value, axis, pairs)  6.81 us
    ppermute x1, starting transfers between devices, shifted(): lax.ppermute(value, axis, [(source, source + steps) for source in range(i...  3.49 us
    dot_general x1, matrix products, on_device(): z = jnp.dot(inputs, w_stack, preferred_element_type=jnp.float32)  1.9 us
    reduce_sum x1, other arithmetic, on_device(): links = jnp.where(chosen[:, :, None, :, None], masks, 0).sum(axis=1)  1.88 us
    dot_general x1, matrix products, on_device(): lax.dot_general(counts, sgrad, (((0,), (0,)), ((), ())), preferred_elemen...  1.88 us
  transfers between devices with their start and end apart: 12, of which 9 were waited for; matrix products, arithmetic and copies ran while one was open for 12% of the time, Pallas kernels for 0%

profile of v7, /device:TPU:0, one launch (start us, length us, event | category | flops | bytes accessed | tf_op | source)
XLA Modules:
  0.0 67.2 jit_solution(7521132227013564737)
XLA Ops:
  0.6 0.0 copy-start.4
  0.6 0.0 copy-start.1
  0.7 0.0 copy-start
  0.7 0.0 copy-start.3
  0.7 3.1 %collective-permute-start.1 = (bf16[8,512]{1,0:T(8,128)(2,1)}, bf16[8,512]{1,0:T(8,128)(2,1)S(1)}, u32[]{:S(2)}, u32[]{:S(2)}) collective-permute-start(bf16[8,512]{1,0:T(8,128)(2,1)} %param.8), channel_id=1, source_target_pairs={{0,16},{4,20},{8,24},{12,28},{16,0},{20,4},{24,8},{28,12},{1,17},{... | collective-permute-start | bytes 24584 | tf_op jit(solution)/shard_map/ppermute | solution.py:99
  3.7 0.9 %slice.48 = bf16[128,512]{1,0:T(8,128)(2,1)S(1)} slice(bf16[512,512]{1,0:T(8,128)(2,1)} %param.7), slice={[384:512], [0:512]} | slice | bytes 262144 | tf_op jit(solution)/shard_map/slice | solution.py:127
  4.6 3.5 %collective-permute-start = (bf16[128,512]{1,0:T(8,128)(2,1)S(1)}, bf16[128,512]{1,0:T(8,128)(2,1)S(1)}, u32[]{:S(2)}, u32[]{:S(2)}) collective-permute-start(bf16[128,512]{1,0:T(8,128)(2,1)S(1)} %slice.48), channel_id=1, source_target_pairs={{0,1},{1,2},{2,3},{4,5},{5,6},{6,7},{8,9},{9,10},{10,11},{12,13},{... | collective-permute-start | bytes 393224 | tf_op jit(solution)/shard_map/ppermute | solution.py:10
  8.1 0.7 %eq.81 = s32[4,4]{1,0:T(4,128)S(1)} reshape(s32[16]{0:T(128)} %param.10) | data formatting | bytes 128 | tf_op jit(solution)/shard_map/eq | solution.py:131
  8.9 0.1 iota_compare_fusion.4
  9.0 1.9 %select_reduce_fusion = s32[4,128,5,128]{3,1,2,0:T(8,128)S(1)} fusion(s32[4,4,128,128]{3,2,1,0:T(8,128)} %bitcast.126, pred[4,4,5]{2,1,0:T(4,128)(4,1)S(1)} %iota_compare_fusion.4), kind=kLoop, calls=%fused_computation | loop fusion | flops 2293760 | bytes 2359376 | tf_op jit(solution)/shard_map/reduce_sum | solution.py:133
  10.9 0.0 collective-permute-done.1
  10.9 0.0 copy-done.4
  10.9 1.6 %collective-permute-start.2 = (bf16[2,8,512]{2,1,0:T(8,128)(2,1)S(1)}, bf16[2,8,512]{2,1,0:T(8,128)(2,1)S(1)}, u32[]{:S(2)}, u32[]{:S(2)}) collective-permute-start(bf16[2,8,512]{2,1,0:T(8,128)(2,1)S(1)} %pad_maximum_fusion.12), channel_id=1, source_target_pairs={{0,8},{4,12},{8,0},{12,4},{16,24},{20,28},{24,16},{28,20},{1,9},{5... | collective-permute-start | bytes 49160 | tf_op jit(solution)/shard_map/ppermute | solution.py:99
  12.5 0.0 copy-done.3
  12.5 0.0 copy-done
  12.5 0.3 reduce_sum.26
  12.9 1.8 %collective-permute-done.2 = bf16[2,8,512]{2,1,0:T(8,128)(2,1)S(1)} collective-permute-done((bf16[2,8,512]{2,1,0:T(8,128)(2,1)S(1)}, bf16[2,8,512]{2,1,0:T(8,128)(2,1)S(1)}, u32[]{:S(2)}, u32[]{:S(2)}) %collective-permute-start.2) | collective-permute-done | bytes 16416 | tf_op jit(solution)/shard_map/ppermute | solution.py:99
  14.7 0.1 collective-permute-start.3
  14.8 0.0 copy-done.1
  14.8 0.2 copy.36
  15.0 0.1 convert_element_type.48
  15.2 0.9 %copy.33 = bf16[4,128,5,128]{1,0,3,2:T(4,128)(2,1)S(1)} copy(bf16[4,128,5,128]{3,1,2,0:T(8,128)(2,1)S(1)} %convert_element_type.48) | data formatting | bytes 1310720 | tf_op jit(solution)/shard_map/convert_element_type | solution.py:135
  16.1 0.0 collective-permute-done.3
  16.2 0.9 %fusion.16 = f32[512,512]{0,1:T(8,128)S(1)} fusion(bf16[64,512]{1,0:T(8,128)(2,1)S(1)} %bitcast.141, s32[512]{0:T(512)S(1)} %bitcast.148, s32[512]{0:T(512)S(1)} %bitcast.150, s32[512]{0:T(512)S(1)} %bitcast.146, s32[512]{0:T(512)S(1)} %bitcast.144), kind=kOutput, calls=%fused_computation.46 | convolution fusion | flops 33947648 | bytes 1122304 | tf_op jit(solution)/shard_map/dot_general | solution.py:143
  17.1 0.0 collective-permute-done
  17.1 0.0 copy-start.5
  17.1 0.0 copy-start.6
  17.2 0.7 fusion.2
  17.8 0.5 copy-done.5
  18.4 0.1 copy-done.6
  18.5 1.9 %multiply_convert_fusion = (bf16[512,512]{1,0:T(8,128)(2,1)S(1)}, bf16[512,512]{1,0:T(8,128)(2,1)}) fusion(bf16[512,512]{1,0:T(8,128)(2,1)S(1)} %copy-done.6, bf16[1024,512]{1,0:T(8,128)(2,1)S(1)} %copy-done.5, bf16[512,512]{0,1:T(8,128)(2,1)S(1)} %fusion.2, bf16[512,512]{0,1:T(8,128)(2,1)S(1)} %copy.36), kind=kOutput, calls=%fused_computation.10 | convolution fusion | flops 542113792 | bytes 3670016 | tf_op jit(solution)/shard_map/dot_general | solution.py:146
  20.4 0.0 copy-start.2
  20.4 0.7 %fusion.5 = f32[1024,512]{1,0:T(8,128)S(1)} fusion(bf16[512,512]{1,0:T(8,128)(2,1)S(1)} %get-tuple-element.3, bf16[512,512]{0,1:T(8,128)(2,1)S(1)} %fusion.2, bf16[512,512]{0,1:T(8,128)(2,1)S(1)} %copy.36), kind=kOutput, calls=%fused_computation.13 | convolution fusion | flops 538968064 | bytes 3670016 | tf_op jit(solution)/shard_map/dot_general | solution.py:150
  21.1 0.1 constant_dynamic-slice_fusion.5
  21.2 0.0 copy-done.2
  21.2 0.5 collective-permute-start.4
  21.8 1.9 %fusion.4 = f32[64,512]{1,0:T(8,128)S(1)} fusion(bf16[512,512]{1,0:T(8,128)(2,1)} %copy-done.2, bf16[1024,512]{1,0:T(8,128)(2,1)} %param.12, f32[512]{0:T(512)S(1)} %add_bitcast_fusion, s32[512]{0:T(512)S(1)} %bitcast.149, s32[512]{0:T(512)S(1)} %bitcast.151, s32[512]{0:T(512)S(1)} %bitcast.147, s32[512]{0:T(512)S(1)} %bitcast.145), kind=kOutput, calls=%fused_computation.7 | convolution fusion | flops 302907392 | bytes 1189888 | tf_op jit(solution)/shard_map/dot_general | solution.py:157
  23.7 0.5 collective-permute-done.4
  24.2 1.4 %bitcast_add_fusion = f32[4,2,2,32,512]{4,3,2,1,0:T(8,128)S(1)} fusion(f32[4,2,2,32,512]{4,3,2,1,0:T(8,128)} %bitcast.20, f32[4,2,2,2,32,512]{5,4,3,2,1,0:T(8,128)S(1)} %bitcast.125, s32[]{:T(128)S(6)} %select_n.243), kind=kLoop, calls=%fused_computation.9 | loop fusion | flops 262144 | bytes 3145732 | tf_op jit(solution)/shard_map/add | solution.py:72
  25.7 0.1 bitcast_select_fusion
  25.8 1.6 %collective-permute-start.5 = (f32[288,512]{1,0:T(8,128)S(1)}, f32[288,512]{1,0:T(8,128)S(1)}, u32[]{:S(2)}, u32[]{:S(2)}) collective-permute-start(f32[288,512]{1,0:T(8,128)S(1)} %pad_maximum_fusion.3), channel_id=1, source_target_pairs={{0,8},{4,20},{8,0},{12,28},{16,24},{20,4},{24,16},{28,12},{1,9},{5... | collective-permute-start | bytes 1769480 | tf_op jit(solution)/shard_map/ppermute | solution.py:29
  27.4 8.4 %collective-permute-done.5 = f32[288,512]{1,0:T(8,128)S(1)} collective-permute-done((f32[288,512]{1,0:T(8,128)S(1)}, f32[288,512]{1,0:T(8,128)S(1)}, u32[]{:S(2)}, u32[]{:S(2)}) %collective-permute-start.5) | collective-permute-done | bytes 589856 | tf_op jit(solution)/shard_map/ppermute | solution.py:29
  35.9 0.2 fusion.12
  36.0 0.1 dynamic-slice_select_fusion.1
  36.2 0.6 collective-permute-start.6
  36.7 6.2 %collective-permute-done.6 = f32[144,512]{1,0:T(8,128)S(1)} collective-permute-done((f32[144,512]{1,0:T(8,128)S(1)}, f32[144,512]{1,0:T(8,128)S(1)}, u32[]{:S(2)}, u32[]{:S(2)}) %collective-permute-start.6) | collective-permute-done | bytes 294944 | tf_op jit(solution)/shard_map/ppermute | solution.py:29
  43.1 1.6 %collective-permute-start.7 = (f32[80,512]{1,0:T(8,128)S(1)}, f32[80,512]{1,0:T(8,128)S(1)}, u32[]{:S(2)}, u32[]{:S(2)}) collective-permute-start(f32[80,512]{1,0:T(8,128)S(1)} %pad_maximum_fusion.7), channel_id=1, source_target_pairs={{0,1},{1,0},{2,3},{3,2},{4,5},{5,4},{6,7},{7,6},{8,9},{9,8},{10,11... | collective-permute-start | bytes 491528 | tf_op jit(solution)/shard_map/ppermute | solution.py:29
  44.7 3.7 %collective-permute-done.7 = f32[80,512]{1,0:T(8,128)S(1)} collective-permute-done((f32[80,512]{1,0:T(8,128)S(1)}, f32[80,512]{1,0:T(8,128)S(1)}, u32[]{:S(2)}, u32[]{:S(2)}) %collective-permute-start.7) | collective-permute-done | bytes 163872 | tf_op jit(solution)/shard_map/ppermute | solution.py:29
  48.6 2.7 %collective-permute-start.8 = (f32[48,512]{1,0:T(8,128)S(1)}, f32[48,512]{1,0:T(8,128)S(1)}, u32[]{:S(2)}, u32[]{:S(2)}) collective-permute-start(f32[48,512]{1,0:T(8,128)S(1)} %pad_maximum_fusion.9), channel_id=1, source_target_pairs={{0,2},{1,3},{2,0},{3,1},{4,6},{5,7},{6,4},{7,5},{8,10},{9,11},{10,... | collective-permute-start | bytes 294920 | tf_op jit(solution)/shard_map/ppermute | solution.py:29
  51.2 2.9 %collective-permute-done.8 = f32[48,512]{1,0:T(8,128)S(1)} collective-permute-done((f32[48,512]{1,0:T(8,128)S(1)}, f32[48,512]{1,0:T(8,128)S(1)}, u32[]{:S(2)}, u32[]{:S(2)}) %collective-permute-start.8) | collective-permute-done | bytes 98336 | tf_op jit(solution)/shard_map/ppermute | solution.py:29
  54.2 0.6 collective-permute-start.9
  54.7 4.1 %collective-permute-done.9 = f32[32,512]{1,0:T(8,128)S(1)} collective-permute-done((f32[32,512]{1,0:T(8,128)S(1)}, f32[32,512]{1,0:T(8,128)S(1)}, u32[]{:S(2)}, u32[]{:S(2)}) %collective-permute-start.9) | collective-permute-done | bytes 65568 | tf_op jit(solution)/shard_map/ppermute | solution.py:99
  58.9 1.6 %collective-permute-start.10 = (f32[2,32,512]{2,1,0:T(8,128)S(1)}, f32[2,32,512]{2,1,0:T(8,128)S(1)}, u32[]{:S(2)}, u32[]{:S(2)}) collective-permute-start(f32[2,32,512]{2,1,0:T(8,128)S(1)} %pad_maximum_fusion.8), channel_id=1, source_target_pairs={{0,8},{4,20},{8,0},{12,28},{16,24},{20,4},{24,16},{28,12},{1,9},{5... | collective-permute-start | bytes 393224 | tf_op jit(solution)/shard_map/ppermute | solution.py:99
  60.4 3.4 %collective-permute-done.10 = f32[2,32,512]{2,1,0:T(8,128)S(1)} collective-permute-done((f32[2,32,512]{2,1,0:T(8,128)S(1)}, f32[2,32,512]{2,1,0:T(8,128)S(1)}, u32[]{:S(2)}, u32[]{:S(2)}) %collective-permute-start.10) | collective-permute-done | bytes 131104 | tf_op jit(solution)/shard_map/ppermute | solution.py:99
  64.0 0.1 collective-permute-start.11
  64.1 1.5 %collective-permute-done.11 = f32[136,512]{1,0:T(8,128)S(1)} collective-permute-done((f32[136,512]{1,0:T(8,128)S(1)}, f32[136,512]{1,0:T(8,128)S(1)}, u32[]{:S(2)}, u32[]{:S(2)}) %collective-permute-start.11) | collective-permute-done | bytes 278560 | tf_op jit(solution)/shard_map/ppermute | solution.py:29
  65.6 0.1 select_bitcast_fusion.1
  65.7 0.8 %copy.40 = f32[2,2,2,32,512]{4,3,2,1,0:T(8,128)} copy(f32[2,2,2,32,512]{4,3,0,1,2:T(8,128)S(1)} %maximum_bitcast_fusion) | data formatting | bytes 1048576 | tf_op jit(solution)/shard_map/transpose | solution.py:110
  66.6 0.6 slice_add_fusion.2
  (41 shorter events, 0.7 us)
Async XLA Ops:
  0.6 10.2 %copy-start.4 = (bf16[8,512]{1,0:T(8,128)(2,1)S(1)}, bf16[8,512]{1,0:T(8,128)(2,1)}, u32[]{:S(2)}) copy-start(bf16[8,512]{1,0:T(8,128)(2,1)} %param.8) | copy-start | bytes 24580
  0.6 14.2 %copy-start.1 = (bf16[512,512]{1,0:T(8,128)(2,1)S(1)}, bf16[512,512]{1,0:T(8,128)(2,1)}, u32[]{:S(2)}) copy-start(bf16[512,512]{1,0:T(8,128)(2,1)} %param.7) | copy-start | bytes 1572868
  0.7 11.8 %copy-start = (s32[16,128,128]{2,1,0:T(8,128)S(1)}, s32[16,128,128]{2,1,0:T(8,128)}, u32[]{:S(2)}) copy-start(s32[16,128,128]{2,1,0:T(8,128)} %param.11) | copy-start | bytes 3145732
  0.7 11.8 %copy-start.3 = (s32[512,4]{0,1:T(4,128)S(1)}, s32[512,4]{0,1:T(4,128)}, u32[]{:S(2)}) copy-start(s32[512,4]{0,1:T(4,128)} %param.9) | copy-start | bytes 24580
  0.7 10.2 %collective-permute-start.1 = (bf16[8,512]{1,0:T(8,128)(2,1)}, bf16[8,512]{1,0:T(8,128)(2,1)S(1)}, u32[]{:S(2)}, u32[]{:S(2)}) collective-permute-start(bf16[8,512]{1,0:T(8,128)(2,1)} %param.8), channel_id=1, source_target_pairs={{0,16},{4,20},{8,24},{12,28},{16,0},{20,4},{24,8},{28,12},{1,17},{... | collective-permute-start | bytes 24584 | tf_op jit(solution)/shard_map/ppermute | solution.py:99
  4.6 12.5 %collective-permute-start = (bf16[128,512]{1,0:T(8,128)(2,1)S(1)}, bf16[128,512]{1,0:T(8,128)(2,1)S(1)}, u32[]{:S(2)}, u32[]{:S(2)}) collective-permute-start(bf16[128,512]{1,0:T(8,128)(2,1)S(1)} %slice.48), channel_id=1, source_target_pairs={{0,1},{1,2},{2,3},{4,5},{5,6},{6,7},{8,9},{9,10},{10,11},{12,13},{... | collective-permute-start | bytes 393224 | tf_op jit(solution)/shard_map/ppermute | solution.py:10
  10.9 3.8 %collective-permute-start.2 = (bf16[2,8,512]{2,1,0:T(8,128)(2,1)S(1)}, bf16[2,8,512]{2,1,0:T(8,128)(2,1)S(1)}, u32[]{:S(2)}, u32[]{:S(2)}) collective-permute-start(bf16[2,8,512]{2,1,0:T(8,128)(2,1)S(1)} %pad_maximum_fusion.12), channel_id=1, source_target_pairs={{0,8},{4,12},{8,0},{12,4},{16,24},{20,28},{24,16},{28,20},{1,9},{5... | collective-permute-start | bytes 49160 | tf_op jit(solution)/shard_map/ppermute | solution.py:99
  14.7 1.4 %collective-permute-start.3 = (bf16[2,2,8,512]{3,2,0,1:T(8,128)(2,1)S(1)}, bf16[2,2,8,512]{3,2,0,1:T(8,128)(2,1)S(1)}, u32[]{:S(2)}, u32[]{:S(2)}) collective-permute-start(bf16[2,2,8,512]{3,2,0,1:T(8,128)(2,1)S(1)} %pad_maximum_fusion.11), channel_id=1, source_target_pairs={{0,4},{4,0},{8,12},{12,8},{16,20},{20,16},{24,28},{28,24},{1,5},{5... | collective-permute-start | bytes 98312 | tf_op jit(solution)/shard_map/ppermute | solution.py:99
  17.1 1.2 %copy-start.5 = (bf16[1024,512]{1,0:T(8,128)(2,1)S(1)}, bf16[1024,512]{1,0:T(8,128)(2,1)}, u32[]{:S(2)}) copy-start(bf16[1024,512]{1,0:T(8,128)(2,1)} %param.12) | copy-start | bytes 3145732
  17.1 1.3 %copy-start.6 = (bf16[512,512]{1,0:T(8,128)(2,1)S(1)}, bf16[512,512]{1,0:T(8,128)(2,1)}, u32[]{:S(2)}) copy-start(bf16[512,512]{1,0:T(8,128)(2,1)} %param.13) | copy-start | bytes 1572868
  20.4 0.8 %copy-start.2 = (bf16[512,512]{1,0:T(8,128)(2,1)}, bf16[512,512]{1,0:T(8,128)(2,1)S(1)}, u32[]{:S(2)}) copy-start(bf16[512,512]{1,0:T(8,128)(2,1)S(1)} %get-tuple-element.3) | copy-start | bytes 1572868
  21.2 3.0 %collective-permute-start.4 = (f32[512,512]{1,0:T(8,128)S(1)}, f32[512,512]{1,0:T(8,128)}, u32[]{:S(2)}, u32[]{:S(2)}) collective-permute-start(f32[512,512]{1,0:T(8,128)S(1)} %bitcast.128), channel_id=1, source_target_pairs={{0,4},{4,0},{8,12},{12,8},{16,20},{20,16},{24,28},{28,24},{1,5},{5... | collective-permute-start | bytes 3145736 | tf_op jit(solution)/shard_map/ppermute | solution.py:29
  25.8 9.9 %collective-permute-start.5 = (f32[288,512]{1,0:T(8,128)S(1)}, f32[288,512]{1,0:T(8,128)S(1)}, u32[]{:S(2)}, u32[]{:S(2)}) collective-permute-start(f32[288,512]{1,0:T(8,128)S(1)} %pad_maximum_fusion.3), channel_id=1, source_target_pairs={{0,8},{4,20},{8,0},{12,28},{16,24},{20,4},{24,16},{28,12},{1,9},{5... | collective-permute-start | bytes 1769480 | tf_op jit(solution)/shard_map/ppermute | solution.py:29
  36.2 6.8 %collective-permute-start.6 = (f32[144,512]{1,0:T(8,128)S(1)}, f32[144,512]{1,0:T(8,128)S(1)}, u32[]{:S(2)}, u32[]{:S(2)}) collective-permute-start(f32[144,512]{1,0:T(8,128)S(1)} %pad_maximum_fusion.4), channel_id=1, source_target_pairs={{0,16},{4,12},{8,24},{12,4},{16,0},{20,28},{24,8},{28,20},{1,17},{... | collective-permute-start | bytes 884744 | tf_op jit(solution)/shard_map/ppermute | solution.py:29
  43.1 5.4 %collective-permute-start.7 = (f32[80,512]{1,0:T(8,128)S(1)}, f32[80,512]{1,0:T(8,128)S(1)}, u32[]{:S(2)}, u32[]{:S(2)}) collective-permute-start(f32[80,512]{1,0:T(8,128)S(1)} %pad_maximum_fusion.7), channel_id=1, source_target_pairs={{0,1},{1,0},{2,3},{3,2},{4,5},{5,4},{6,7},{7,6},{8,9},{9,8},{10,11... | collective-permute-start | bytes 491528 | tf_op jit(solution)/shard_map/ppermute | solution.py:29
  48.6 5.6 %collective-permute-start.8 = (f32[48,512]{1,0:T(8,128)S(1)}, f32[48,512]{1,0:T(8,128)S(1)}, u32[]{:S(2)}, u32[]{:S(2)}) collective-permute-start(f32[48,512]{1,0:T(8,128)S(1)} %pad_maximum_fusion.9), channel_id=1, source_target_pairs={{0,2},{1,3},{2,0},{3,1},{4,6},{5,7},{6,4},{7,5},{8,10},{9,11},{10,... | collective-permute-start | bytes 294920 | tf_op jit(solution)/shard_map/ppermute | solution.py:29
  54.2 4.6 %collective-permute-start.9 = (f32[32,512]{1,0:T(8,128)S(1)}, f32[32,512]{1,0:T(8,128)S(1)}, u32[]{:S(2)}, u32[]{:S(2)}) collective-permute-start(f32[32,512]{1,0:T(8,128)S(1)} %slice_add_fusion), channel_id=1, source_target_pairs={{0,16},{4,12},{8,24},{12,4},{16,0},{20,28},{24,8},{28,20},{1,17},{... | collective-permute-start | bytes 196616 | tf_op jit(solution)/shard_map/ppermute | solution.py:99
  58.9 5.0 %collective-permute-start.10 = (f32[2,32,512]{2,1,0:T(8,128)S(1)}, f32[2,32,512]{2,1,0:T(8,128)S(1)}, u32[]{:S(2)}, u32[]{:S(2)}) collective-permute-start(f32[2,32,512]{2,1,0:T(8,128)S(1)} %pad_maximum_fusion.8), channel_id=1, source_target_pairs={{0,8},{4,20},{8,0},{12,28},{16,24},{20,4},{24,16},{28,12},{1,9},{5... | collective-permute-start | bytes 393224 | tf_op jit(solution)/shard_map/ppermute | solution.py:99
  64.0 1.6 %collective-permute-start.11 = (f32[136,512]{1,0:T(8,128)S(1)}, f32[136,512]{1,0:T(8,128)S(1)}, u32[]{:S(2)}, u32[]{:S(2)}) collective-permute-start(f32[136,512]{1,0:T(8,128)S(1)} %pad_maximum_fusion.5), channel_id=1, source_target_pairs={{0,4},{4,0},{8,12},{12,8},{16,20},{20,16},{24,28},{28,24},{1,5},{5... | collective-permute-start | bytes 835592 | tf_op jit(solution)/shard_map/ppermute | solution.py:29

commit v8 on v7

--- a/solution.py
+++ b/solution.py
@@ -74,7 +74,7 @@
     return values, riders
 
 
-def gather_ordered(value, axis, order, rider=None, other=None):
+def gather_ordered(value, axis, order, rider=None, other=None, hook=None):
     count = lax.axis_size(axis)
     levels = log2(count)
     me = lax.axis_index(axis)
@@ -101,6 +101,9 @@
         low = jnp.where(mine == 0, value, got)
         high = jnp.where(mine == 0, got, value)
         value = jnp.stack([low, high], axis=0)
+        if hook is not None:
+            value = hook(value)
+            hook = None
         held[0].insert(0, bit)
         held[1].insert(0, bit_b)
     tail = list(range(levels, levels + len(rest)))
@@ -125,7 +128,15 @@
     up = list(range(log2(regions)))
     down = up[::-1]
     prev = shifted(feats[rows - tile :], "dom", 1)
-    hub_table = gather_ordered(hub_feats, "region", down)[0].reshape(total_hubs, width)
+    held = {}
+
+    def mask_after(value):
+        value, held["mask"] = lax.optimization_barrier((value, tile_mask))
+        return value
+
+    hub_table = gather_ordered(hub_feats, "region", down, hook=mask_after)[0]
+    hub_table = hub_table.reshape(total_hubs, width)
+    tile_mask = held["mask"]
     window = jnp.concatenate([prev, feats], axis=0)
     src = tile_src.reshape(nblk, per_block)
     chosen = src[:, :, None] == lax.broadcasted_iota(jnp.int32, (nblk, per_block, nblk + 1), 2)

time: 67.5 us -> 70.9 us (1.050)
  waiting for transfers between devices: 32.7 us -> 34.6 us
  local copies, waits for them, and re-layouts: 4.68 us -> 6.55 us
  matrix products: 6.09 us -> 7.11 us
  starting transfers between devices: 17.3 us -> 16.5 us
    ppermute x6, waiting for transfers between devices: 23.3 us -> 25.6 us  [exchange(): flat = lax.ppermute(flat, axis, pairs).astype(kind)]
    reduce_sum x1, other arithmetic: 1.88 us -> 0.5 us  [on_device(): links = jnp.where(chosen[:, :, None, :, None], masks, 0).sum(axis=1)]
    ppermute x6, starting transfers between devices: 7.03 us -> 5.67 us  [exchange(): flat = lax.ppermute(flat, axis, pairs).astype(kind)]
    dot_general x1, matrix products: 0.67 us -> 1.68 us  [on_device(): jnp.dot(links.astype(jnp.bfloat16), window, preferred_element_type=jnp.fl...]
    slice x1, local copies, waits for them, and re-layouts: 0.01 us -> 0.85 us  [on_device(): hub_ids[:, slot:slot + 1] == hub_cols]
  transfers between devices with their start and end apart: 12 -> 12, of which waited for: 9 -> 10; matrix products, arithmetic and copies ran while one was open for 12% -> 14% of each run, Pallas kernels for 0% -> 0%
where the time goes in v8:
time: 70.9 us; the launch traced here: 70.5 us
  waiting for transfers between devices  34.6 us (49%)
  starting transfers between devices  16.5 us (23%)
  matrix products  7.11 us (10%)
  local copies, waits for them, and re-layouts  6.55 us (9%)
  other arithmetic  4.6 us (6%)
  between operations  1.09 us (2%)
    ppermute x6, waiting for transfers between devices, exchange(): flat = lax.ppermute(flat, axis, pairs).astype(kind)  25.6 us
    ppermute x5, waiting for transfers between devices, gather_ordered(): got = lax.ppermute(value, axis, pairs)  8.97 us
    ppermute x5, starting transfers between devices, gather_ordered(): got = lax.ppermute(value, axis, pairs)  6.75 us
    ppermute x6, starting transfers between devices, exchange(): flat = lax.ppermute(flat, axis, pairs).astype(kind)  5.67 us
    ppermute x1, starting transfers between devices, shifted(): lax.ppermute(value, axis, [(source, source + steps) for source in range(i...  4.13 us
    dot_general x1, matrix products, on_device(): z = jnp.dot(inputs, w_stack, preferred_element_type=jnp.float32)  1.91 us
    dot_general x1, matrix products, on_device(): lax.dot_general(counts, sgrad, (((0,), (0,)), ((), ())), preferred_elemen...  1.88 us
    add x7, other arithmetic, scatter_sum(): values[i] = k + g  1.69 us
  transfers between devices with their start and end apart: 12, of which 10 were waited for; matrix products, arithmetic and copies ran while one was open for 14% of the time, Pallas kernels for 0%

profile of v8, /device:TPU:0, one launch (start us, length us, event | category | flops | bytes accessed | tf_op | source)
XLA Modules:
  0.0 70.5 jit_solution(6074326320969291192)
XLA Ops:
  0.6 0.0 copy-start
  0.6 3.1 %collective-permute-start = (bf16[8,512]{1,0:T(8,128)(2,1)}, bf16[8,512]{1,0:T(8,128)(2,1)S(1)}, u32[]{:S(2)}, u32[]{:S(2)}) collective-permute-start(bf16[8,512]{1,0:T(8,128)(2,1)} %param.8), channel_id=1, source_target_pairs={{0,16},{4,20},{8,24},{12,28},{16,0},{20,4},{24,8},{28,12},{1,17},{... | collective-permute-start | bytes 24584 | tf_op jit(solution)/shard_map/ppermute | solution.py:99
  3.7 1.6 %slice.48 = bf16[128,512]{1,0:T(8,128)(2,1)} slice(bf16[512,512]{1,0:T(8,128)(2,1)} %param.7), slice={[384:512], [0:512]} | slice | bytes 262144 | tf_op jit(solution)/shard_map/slice | solution.py:130
  5.3 4.1 %collective-permute-start.1 = (bf16[128,512]{1,0:T(8,128)(2,1)}, bf16[128,512]{1,0:T(8,128)(2,1)}, u32[]{:S(2)}, u32[]{:S(2)}) collective-permute-start(bf16[128,512]{1,0:T(8,128)(2,1)} %slice.48), channel_id=1, source_target_pairs={{0,1},{1,2},{2,3},{4,5},{5,6},{6,7},{8,9},{9,10},{10,11},{12,13},{... | collective-permute-start | bytes 393224 | tf_op jit(solution)/shard_map/ppermute | solution.py:10
  9.4 0.9 %fusion.22 = (s32[512,1]{0,1:T(1,128)S(1)}, s32[512,1]{0,1:T(1,128)S(1)}, s32[512,1]{0,1:T(1,128)S(1)}, s32[512,1]{0,1:T(1,128)S(1)}) fusion(s32[512,4]{0,1:T(4,128)} %param.9), kind=kLoop, calls=%fused_computation.85 | loop fusion | bytes 16384 | tf_op jit(solution)/shard_map/slice | solution.py:152
  10.3 0.7 %eq.81 = s32[4,4]{1,0:T(4,128)S(1)} reshape(s32[16]{0:T(128)} %param.10) | data formatting | bytes 128 | tf_op jit(solution)/shard_map/eq | solution.py:142
  11.0 0.1 iota_compare_fusion.4
  11.1 1.3 %copy.36 = bf16[512,512]{0,1:T(8,128)(2,1)S(1)} copy(bf16[512,512]{1,0:T(8,128)(2,1)} %param.7) | data formatting | bytes 1048576 | tf_op args[0]
  12.3 0.0 collective-permute-done
  12.4 0.7 select_bitcast_fusion.12
  13.1 1.5 %collective-permute-start.2 = (bf16[2,8,512]{2,1,0:T(8,128)(2,1)S(1)}, bf16[2,8,512]{2,1,0:T(8,128)(2,1)S(1)}, u32[]{:S(2)}, u32[]{:S(2)}) collective-permute-start(bf16[2,8,512]{2,1,0:T(8,128)(2,1)S(1)} %pad_maximum_fusion.12), channel_id=1, source_target_pairs={{0,8},{4,12},{8,0},{12,4},{16,24},{20,28},{24,16},{28,20},{1,9},{5... | collective-permute-start | bytes 49160 | tf_op jit(solution)/shard_map/ppermute | solution.py:99
  14.6 0.0 copy-done
  14.6 0.5 select_reduce_fusion
  15.1 0.3 reduce_sum.26
  15.4 1.4 %collective-permute-done.2 = bf16[2,8,512]{2,1,0:T(8,128)(2,1)S(1)} collective-permute-done((bf16[2,8,512]{2,1,0:T(8,128)(2,1)S(1)}, bf16[2,8,512]{2,1,0:T(8,128)(2,1)S(1)}, u32[]{:S(2)}, u32[]{:S(2)}) %collective-permute-start.2) | collective-permute-done | bytes 16416 | tf_op jit(solution)/shard_map/ppermute | solution.py:99
  16.8 0.1 collective-permute-start.3
  16.9 0.0 copy-start.1
  16.9 0.1 convert_element_type.48
  17.1 0.9 %copy.33 = bf16[4,128,5,128]{1,0,3,2:T(4,128)(2,1)S(1)} copy(bf16[4,128,5,128]{3,1,2,0:T(8,128)(2,1)S(1)} %convert_element_type.48) | data formatting | bytes 1310720 | tf_op jit(solution)/shard_map/convert_element_type | solution.py:146
  18.0 0.1 collective-permute-done.3
  18.1 0.9 %fusion.16 = f32[512,512]{0,1:T(8,128)S(1)} fusion(bf16[64,512]{1,0:T(8,128)(2,1)S(1)} %bitcast.141, s32[512]{0:T(512)S(1)} %bitcast.148, s32[512]{0:T(512)S(1)} %bitcast.150, s32[512]{0:T(512)S(1)} %bitcast.146, s32[512]{0:T(512)S(1)} %bitcast.144), kind=kOutput, calls=%fused_computation.46 | convolution fusion | flops 33947648 | bytes 1122304 | tf_op jit(solution)/shard_map/dot_general | solution.py:154
  19.1 0.0 collective-permute-done.1
  19.1 0.0 copy-done.1
  19.1 0.0 copy-start.3
  19.1 0.0 copy-start.4
  19.1 1.7 %fusion.2 = bf16[512,512]{0,1:T(8,128)(2,1)S(1)} fusion(f32[512,512]{0,1:T(8,128)S(1)} %fusion.16, bf16[512,512]{0,1:T(8,128)(2,1)S(1)} %copy.36, bf16[80,8,4,128]{3,2,1,0:T(4,128)(2,1)S(1)} %bitcast.134, bf16[512,512]{1,0:T(8,128)(2,1)S(1)} %copy-done.1, bf16[128,512]{1,0:T(8,128)(2,1)} %collective-permute-done.1, f32[512]{0:T(512)S(1)} %add_bitcast_fusion), kind=kOutput, calls=%fused_computation.5 | convolution fusion | flops 338165760 | bytes 3409920 | tf_op jit(solution)/shard_map/dot_general | solution.py:146
  20.8 0.0 copy-done.3
  20.8 0.0 copy-done.4
  20.8 1.9 %multiply_convert_fusion = (bf16[512,512]{1,0:T(8,128)(2,1)S(1)}, bf16[512,512]{1,0:T(8,128)(2,1)}) fusion(bf16[512,512]{1,0:T(8,128)(2,1)S(1)} %copy-done.4, bf16[1024,512]{1,0:T(8,128)(2,1)S(1)} %copy-done.3, bf16[512,512]{0,1:T(8,128)(2,1)S(1)} %fusion.2, bf16[512,512]{0,1:T(8,128)(2,1)S(1)} %copy.36), kind=kOutput, calls=%fused_computation.10 | convolution fusion | flops 542113792 | bytes 3670016 | tf_op jit(solution)/shard_map/dot_general | solution.py:157
  22.7 0.0 copy-start.2
  22.7 0.7 fusion.5
  23.4 0.1 constant_dynamic-slice_fusion.5
  23.6 0.0 copy-done.2
  23.6 0.5 collective-permute-start.4
  24.0 1.9 %fusion.4 = f32[64,512]{1,0:T(8,128)S(1)} fusion(bf16[512,512]{1,0:T(8,128)(2,1)} %copy-done.2, bf16[1024,512]{1,0:T(8,128)(2,1)} %param.12, f32[512]{0:T(512)S(1)} %add_bitcast_fusion, s32[512]{0:T(512)S(1)} %bitcast.149, s32[512]{0:T(512)S(1)} %bitcast.151, s32[512]{0:T(512)S(1)} %bitcast.147, s32[512]{0:T(512)S(1)} %bitcast.145), kind=kOutput, calls=%fused_computation.7 | convolution fusion | flops 302907392 | bytes 1189888 | tf_op jit(solution)/shard_map/dot_general | solution.py:168
  26.0 0.5 collective-permute-done.4
  26.4 1.4 %bitcast_add_fusion = f32[4,2,2,32,512]{4,3,2,1,0:T(8,128)S(1)} fusion(f32[4,2,2,32,512]{4,3,2,1,0:T(8,128)} %bitcast.20, f32[4,2,2,2,32,512]{5,4,3,2,1,0:T(8,128)S(1)} %bitcast.125, s32[]{:T(128)S(6)} %select_n.243), kind=kLoop, calls=%fused_computation.9 | loop fusion | flops 262144 | bytes 3145732 | tf_op jit(solution)/shard_map/add | solution.py:72
  28.0 0.1 bitcast_select_fusion
  28.1 1.6 %collective-permute-start.5 = (f32[288,512]{1,0:T(8,128)S(1)}, f32[288,512]{1,0:T(8,128)S(1)}, u32[]{:S(2)}, u32[]{:S(2)}) collective-permute-start(f32[288,512]{1,0:T(8,128)S(1)} %pad_maximum_fusion.3), channel_id=1, source_target_pairs={{0,8},{4,20},{8,0},{12,28},{16,24},{20,4},{24,16},{28,12},{1,9},{5... | collective-permute-start | bytes 1769480 | tf_op jit(solution)/shard_map/ppermute | solution.py:29
  29.6 8.4 %collective-permute-done.5 = f32[288,512]{1,0:T(8,128)S(1)} collective-permute-done((f32[288,512]{1,0:T(8,128)S(1)}, f32[288,512]{1,0:T(8,128)S(1)}, u32[]{:S(2)}, u32[]{:S(2)}) %collective-permute-start.5) | collective-permute-done | bytes 589856 | tf_op jit(solution)/shard_map/ppermute | solution.py:29
  38.1 0.2 fusion.12
  38.3 0.1 dynamic-slice_select_fusion.1
  38.4 0.6 collective-permute-start.6
  39.0 6.2 %collective-permute-done.6 = f32[144,512]{1,0:T(8,128)S(1)} collective-permute-done((f32[144,512]{1,0:T(8,128)S(1)}, f32[144,512]{1,0:T(8,128)S(1)}, u32[]{:S(2)}, u32[]{:S(2)}) %collective-permute-start.6) | collective-permute-done | bytes 294944 | tf_op jit(solution)/shard_map/ppermute | solution.py:29
  45.4 1.0 %collective-permute-start.7 = (f32[80,512]{1,0:T(8,128)S(1)}, f32[80,512]{1,0:T(8,128)S(1)}, u32[]{:S(2)}, u32[]{:S(2)}) collective-permute-start(f32[80,512]{1,0:T(8,128)S(1)} %pad_maximum_fusion.7), channel_id=1, source_target_pairs={{0,1},{1,0},{2,3},{3,2},{4,5},{5,4},{6,7},{7,6},{8,9},{9,8},{10,11... | collective-permute-start | bytes 491528 | tf_op jit(solution)/shard_map/ppermute | solution.py:29
  46.3 4.4 %collective-permute-done.7 = f32[80,512]{1,0:T(8,128)S(1)} collective-permute-done((f32[80,512]{1,0:T(8,128)S(1)}, f32[80,512]{1,0:T(8,128)S(1)}, u32[]{:S(2)}, u32[]{:S(2)}) %collective-permute-start.7) | collective-permute-done | bytes 163872 | tf_op jit(solution)/shard_map/ppermute | solution.py:29
  50.8 2.0 %collective-permute-start.8 = (f32[48,512]{1,0:T(8,128)S(1)}, f32[48,512]{1,0:T(8,128)S(1)}, u32[]{:S(2)}, u32[]{:S(2)}) collective-permute-start(f32[48,512]{1,0:T(8,128)S(1)} %pad_maximum_fusion.9), channel_id=1, source_target_pairs={{0,2},{1,3},{2,0},{3,1},{4,6},{5,7},{6,4},{7,5},{8,10},{9,11},{10,... | collective-permute-start | bytes 294920 | tf_op jit(solution)/shard_map/ppermute | solution.py:29
  52.8 4.6 %collective-permute-done.8 = f32[48,512]{1,0:T(8,128)S(1)} collective-permute-done((f32[48,512]{1,0:T(8,128)S(1)}, f32[48,512]{1,0:T(8,128)S(1)}, u32[]{:S(2)}, u32[]{:S(2)}) %collective-permute-start.8) | collective-permute-done | bytes 98336 | tf_op jit(solution)/shard_map/ppermute | solution.py:29
  57.5 0.6 collective-permute-start.9
  58.1 4.1 %collective-permute-done.9 = f32[32,512]{1,0:T(8,128)S(1)} collective-permute-done((f32[32,512]{1,0:T(8,128)S(1)}, f32[32,512]{1,0:T(8,128)S(1)}, u32[]{:S(2)}, u32[]{:S(2)}) %collective-permute-start.9) | collective-permute-done | bytes 65568 | tf_op jit(solution)/shard_map/ppermute | solution.py:99
  62.2 1.6 %collective-permute-start.10 = (f32[2,32,512]{2,1,0:T(8,128)S(1)}, f32[2,32,512]{2,1,0:T(8,128)S(1)}, u32[]{:S(2)}, u32[]{:S(2)}) collective-permute-start(f32[2,32,512]{2,1,0:T(8,128)S(1)} %pad_maximum_fusion.8), channel_id=1, source_target_pairs={{0,8},{4,20},{8,0},{12,28},{16,24},{20,4},{24,16},{28,12},{1,9},{5... | collective-permute-start | bytes 393224 | tf_op jit(solution)/shard_map/ppermute | solution.py:99
  63.7 3.4 %collective-permute-done.10 = f32[2,32,512]{2,1,0:T(8,128)S(1)} collective-permute-done((f32[2,32,512]{2,1,0:T(8,128)S(1)}, f32[2,32,512]{2,1,0:T(8,128)S(1)}, u32[]{:S(2)}, u32[]{:S(2)}) %collective-permute-start.10) | collective-permute-done | bytes 131104 | tf_op jit(solution)/shard_map/ppermute | solution.py:99
  67.3 0.1 collective-permute-start.11
  67.4 1.5 %collective-permute-done.11 = f32[136,512]{1,0:T(8,128)S(1)} collective-permute-done((f32[136,512]{1,0:T(8,128)S(1)}, f32[136,512]{1,0:T(8,128)S(1)}, u32[]{:S(2)}, u32[]{:S(2)}) %collective-permute-start.11) | collective-permute-done | bytes 278560 | tf_op jit(solution)/shard_map/ppermute | solution.py:29
  68.9 0.1 select_bitcast_fusion.1
  69.1 0.8 %copy.40 = f32[2,2,2,32,512]{4,3,2,1,0:T(8,128)} copy(f32[2,2,2,32,512]{4,3,0,1,2:T(8,128)S(1)} %maximum_bitcast_fusion) | data formatting | bytes 1048576 | tf_op jit(solution)/shard_map/transpose | solution.py:113
  69.9 0.6 slice_add_fusion.2
  (39 shorter events, 0.7 us)
Async XLA Ops:
  0.6 13.9 %copy-start = (s32[16,128,128]{2,1,0:T(8,128)S(1)}, s32[16,128,128]{2,1,0:T(8,128)}, u32[]{:S(2)}) copy-start(s32[16,128,128]{2,1,0:T(8,128)} %param.11) | copy-start | bytes 3145732
  0.6 11.7 %collective-permute-start = (bf16[8,512]{1,0:T(8,128)(2,1)}, bf16[8,512]{1,0:T(8,128)(2,1)S(1)}, u32[]{:S(2)}, u32[]{:S(2)}) collective-permute-start(bf16[8,512]{1,0:T(8,128)(2,1)} %param.8), channel_id=1, source_target_pairs={{0,16},{4,20},{8,24},{12,28},{16,0},{20,4},{24,8},{28,12},{1,17},{... | collective-permute-start | bytes 24584 | tf_op jit(solution)/shard_map/ppermute | solution.py:99
  5.3 13.8 %collective-permute-start.1 = (bf16[128,512]{1,0:T(8,128)(2,1)}, bf16[128,512]{1,0:T(8,128)(2,1)}, u32[]{:S(2)}, u32[]{:S(2)}) collective-permute-start(bf16[128,512]{1,0:T(8,128)(2,1)} %slice.48), channel_id=1, source_target_pairs={{0,1},{1,2},{2,3},{4,5},{5,6},{6,7},{8,9},{9,10},{10,11},{12,13},{... | collective-permute-start | bytes 393224 | tf_op jit(solution)/shard_map/ppermute | solution.py:10
  13.1 3.7 %collective-permute-start.2 = (bf16[2,8,512]{2,1,0:T(8,128)(2,1)S(1)}, bf16[2,8,512]{2,1,0:T(8,128)(2,1)S(1)}, u32[]{:S(2)}, u32[]{:S(2)}) collective-permute-start(bf16[2,8,512]{2,1,0:T(8,128)(2,1)S(1)} %pad_maximum_fusion.12), channel_id=1, source_target_pairs={{0,8},{4,12},{8,0},{12,4},{16,24},{20,28},{24,16},{28,20},{1,9},{5... | collective-permute-start | bytes 49160 | tf_op jit(solution)/shard_map/ppermute | solution.py:99
  16.8 1.3 %collective-permute-start.3 = (bf16[2,2,8,512]{3,2,0,1:T(8,128)(2,1)S(1)}, bf16[2,2,8,512]{3,2,0,1:T(8,128)(2,1)S(1)}, u32[]{:S(2)}, u32[]{:S(2)}) collective-permute-start(bf16[2,2,8,512]{3,2,0,1:T(8,128)(2,1)S(1)} %pad_maximum_fusion.11), channel_id=1, source_target_pairs={{0,4},{4,0},{8,12},{12,8},{16,20},{20,16},{24,28},{28,24},{1,5},{5... | collective-permute-start | bytes 98312 | tf_op jit(solution)/shard_map/ppermute | solution.py:99
  16.9 2.2 %copy-start.1 = (bf16[512,512]{1,0:T(8,128)(2,1)S(1)}, bf16[512,512]{1,0:T(8,128)(2,1)}, u32[]{:S(2)}) copy-start(bf16[512,512]{1,0:T(8,128)(2,1)} %param.7) | copy-start | bytes 1572868
  19.1 1.7 %copy-start.3 = (bf16[1024,512]{1,0:T(8,128)(2,1)S(1)}, bf16[1024,512]{1,0:T(8,128)(2,1)}, u32[]{:S(2)}) copy-start(bf16[1024,512]{1,0:T(8,128)(2,1)} %param.12) | copy-start | bytes 3145732
  19.1 1.7 %copy-start.4 = (bf16[512,512]{1,0:T(8,128)(2,1)S(1)}, bf16[512,512]{1,0:T(8,128)(2,1)}, u32[]{:S(2)}) copy-start(bf16[512,512]{1,0:T(8,128)(2,1)} %param.13) | copy-start | bytes 1572868
  22.7 0.8 %copy-start.2 = (bf16[512,512]{1,0:T(8,128)(2,1)}, bf16[512,512]{1,0:T(8,128)(2,1)S(1)}, u32[]{:S(2)}) copy-start(bf16[512,512]{1,0:T(8,128)(2,1)S(1)} %get-tuple-element.7) | copy-start | bytes 1572868
  23.6 2.9 %collective-permute-start.4 = (f32[512,512]{1,0:T(8,128)S(1)}, f32[512,512]{1,0:T(8,128)}, u32[]{:S(2)}, u32[]{:S(2)}) collective-permute-start(f32[512,512]{1,0:T(8,128)S(1)} %bitcast.128), channel_id=1, source_target_pairs={{0,4},{4,0},{8,12},{12,8},{16,20},{20,16},{24,28},{28,24},{1,5},{5... | collective-permute-start | bytes 3145736 | tf_op jit(solution)/shard_map/ppermute | solution.py:29
  28.1 9.9 %collective-permute-start.5 = (f32[288,512]{1,0:T(8,128)S(1)}, f32[288,512]{1,0:T(8,128)S(1)}, u32[]{:S(2)}, u32[]{:S(2)}) collective-permute-start(f32[288,512]{1,0:T(8,128)S(1)} %pad_maximum_fusion.3), channel_id=1, source_target_pairs={{0,8},{4,20},{8,0},{12,28},{16,24},{20,4},{24,16},{28,12},{1,9},{5... | collective-permute-start | bytes 1769480 | tf_op jit(solution)/shard_map/ppermute | solution.py:29
  38.4 6.8 %collective-permute-start.6 = (f32[144,512]{1,0:T(8,128)S(1)}, f32[144,512]{1,0:T(8,128)S(1)}, u32[]{:S(2)}, u32[]{:S(2)}) collective-permute-start(f32[144,512]{1,0:T(8,128)S(1)} %pad_maximum_fusion.4), channel_id=1, source_target_pairs={{0,16},{4,12},{8,24},{12,4},{16,0},{20,28},{24,8},{28,20},{1,17},{... | collective-permute-start | bytes 884744 | tf_op jit(solution)/shard_map/ppermute | solution.py:29
  45.4 5.4 %collective-permute-start.7 = (f32[80,512]{1,0:T(8,128)S(1)}, f32[80,512]{1,0:T(8,128)S(1)}, u32[]{:S(2)}, u32[]{:S(2)}) collective-permute-start(f32[80,512]{1,0:T(8,128)S(1)} %pad_maximum_fusion.7), channel_id=1, source_target_pairs={{0,1},{1,0},{2,3},{3,2},{4,5},{5,4},{6,7},{7,6},{8,9},{9,8},{10,11... | collective-permute-start | bytes 491528 | tf_op jit(solution)/shard_map/ppermute | solution.py:29
  50.8 6.6 %collective-permute-start.8 = (f32[48,512]{1,0:T(8,128)S(1)}, f32[48,512]{1,0:T(8,128)S(1)}, u32[]{:S(2)}, u32[]{:S(2)}) collective-permute-start(f32[48,512]{1,0:T(8,128)S(1)} %pad_maximum_fusion.9), channel_id=1, source_target_pairs={{0,2},{1,3},{2,0},{3,1},{4,6},{5,7},{6,4},{7,5},{8,10},{9,11},{10,... | collective-permute-start | bytes 294920 | tf_op jit(solution)/shard_map/ppermute | solution.py:29
  57.5 4.6 %collective-permute-start.9 = (f32[32,512]{1,0:T(8,128)S(1)}, f32[32,512]{1,0:T(8,128)S(1)}, u32[]{:S(2)}, u32[]{:S(2)}) collective-permute-start(f32[32,512]{1,0:T(8,128)S(1)} %slice_add_fusion), channel_id=1, source_target_pairs={{0,16},{4,12},{8,24},{12,4},{16,0},{20,28},{24,8},{28,20},{1,17},{... | collective-permute-start | bytes 196616 | tf_op jit(solution)/shard_map/ppermute | solution.py:99
  62.2 5.0 %collective-permute-start.10 = (f32[2,32,512]{2,1,0:T(8,128)S(1)}, f32[2,32,512]{2,1,0:T(8,128)S(1)}, u32[]{:S(2)}, u32[]{:S(2)}) collective-permute-start(f32[2,32,512]{2,1,0:T(8,128)S(1)} %pad_maximum_fusion.8), channel_id=1, source_target_pairs={{0,8},{4,20},{8,0},{12,28},{16,24},{20,4},{24,16},{28,12},{1,9},{5... | collective-permute-start | bytes 393224 | tf_op jit(solution)/shard_map/ppermute | solution.py:99
  67.3 1.6 %collective-permute-start.11 = (f32[136,512]{1,0:T(8,128)S(1)}, f32[136,512]{1,0:T(8,128)S(1)}, u32[]{:S(2)}, u32[]{:S(2)}) collective-permute-start(f32[136,512]{1,0:T(8,128)S(1)} %pad_maximum_fusion.5), channel_id=1, source_target_pairs={{0,4},{4,0},{8,12},{12,8},{16,20},{20,16},{24,28},{28,24},{1,5},{5... | collective-permute-start | bytes 835592 | tf_op jit(solution)/shard_map/ppermute | solution.py:29

commit v9 on v7

--- a/solution.py
+++ b/solution.py
@@ -110,6 +110,42 @@
         ways.append(jnp.transpose(value, natural + tail).reshape((count,) + rest))
     value = ways[0] if held[0] == held[1] else jnp.where(first, ways[0], ways[1])
     return value, rider
+
+
+def scatter_once(value, axis, riders):
+    count = lax.axis_size(axis)
+    me = lax.axis_index(axis)
+    total = lax.dynamic_index_in_dim(value, me, axis=0, keepdims=False)
+    seen = [[r] for r in riders]
+    for k in range(1, count):
+        pairs = [(i, i ^ k) for i in range(count)]
+        send = lax.dynamic_index_in_dim(value, me ^ k, axis=0, keepdims=False)
+        got = exchange([send] + list(riders), axis, pairs)
+        total = total + got[0]
+        for r, g in zip(seen, got[1:]):
+            r.append(g)
+    order = me ^ lax.broadcasted_iota(jnp.int32, (count,), 0)
+    riders = [jnp.take(jnp.stack(r, axis=0), order, axis=0).sum(axis=0) for r in seen]
+    return total, riders
+
+
+def gather_once(value, axis, rider=None):
+    count = lax.axis_size(axis)
+    me = lax.axis_index(axis)
+    got = [value]
+    for k in range(1, count):
+        pairs = [(i, i ^ k) for i in range(count)]
+        if rider is not None and k == 1:
+            mine = me & 1
+            keep = lax.dynamic_index_in_dim(rider, mine, axis=0, keepdims=False)
+            send = lax.dynamic_index_in_dim(rider, 1 - mine, axis=0, keepdims=False)
+            g, g_rider = exchange([value, send], axis, pairs)
+            rider = keep + g_rider
+        else:
+            g = lax.ppermute(value, axis, pairs)
+        got.append(g)
+    order = me ^ lax.broadcasted_iota(jnp.int32, (count,), 0)
+    return jnp.take(jnp.stack(got, axis=0), order, axis=0), rider
 
 
 def on_device(feats, hub_feats, hub_ids, tile_src, tile_mask, w_stack, cotangent):
@@ -160,13 +196,18 @@
         [partial_w, partial_h], "region", [1, 0], up, up[:1] + up[1:][::-1], joins=[0, 1],
         wires=None,
     )
-    (piece_w,), (region_h,) = scatter_sum(
-        [region_w], "dom", [0], list(range(log2(doms))), riders=[region_h],
-        wires=None,
-    )
-    weight_grad, hub_grad = gather_ordered(
-        piece_w, "region", down, region_h, down[:-1][::-1] + down[-1:]
-    )
+    if doms <= 8:
+        piece_w, (region_h,) = scatter_once(region_w, "dom", [region_h])
+    else:
+        (piece_w,), (region_h,) = scatter_sum(
+            [region_w], "dom", [0], list(range(log2(doms))), riders=[region_h]
+        )
+    if regions <= 8:
+        weight_grad, hub_grad = gather_once(piece_w, "region", region_h)
+    else:
+        weight_grad, hub_grad = gather_ordered(
+            piece_w, "region", down, region_h, down[:-1][::-1] + down[-1:]
+        )
     weight_grad = weight_grad.reshape(regions * span, width)
     return (activ, weight_grad, hub_grad)
 

time: 67.5 us -> 68.4 us (1.013)
  waiting for transfers between devices: 32.7 us -> 26.7 us
  starting transfers between devices: 17.3 us -> 21.7 us
  matrix products: 6.09 us -> 7.32 us
  other arithmetic: 5.28 us -> 6.07 us
    ppermute x5 -> x3, waiting for transfers between devices: 9.37 us -> 1.85 us  [gather_ordered(): got = lax.ppermute(value, axis, pairs)]
    ppermute x0 -> x6, starting transfers between devices: none -> 6.3 us  [gather_once(): g = lax.ppermute(value, axis, pairs)]
    ppermute x0 -> x6, waiting for transfers between devices: none -> 3.71 us  [gather_once(): g = lax.ppermute(value, axis, pairs)]
    ppermute x6 -> x7, waiting for transfers between devices: 23.3 us -> 21.2 us  [exchange(): flat = lax.ppermute(flat, axis, pairs).astype(kind)]
    ppermute x5 -> x3, starting transfers between devices: 6.81 us -> 4.69 us  [gather_ordered(): got = lax.ppermute(value, axis, pairs)]
    dot_general x1, matrix products: 0.71 us -> 1.93 us  [on_device(): lax.dot_general(inputs, dz, (((0,), (0,)), ((), ())), preferred_element_t...]
    gather x0 -> x2, local copies, waits for them, and re-layouts: none -> 1.14 us  [the longest x1 0.58 us: gather_once(): return (jnp.take(jnp.stack(got, axis=0), order, axis=0), rider)]
    transpose x1 -> x0, local copies, waits for them, and re-layouts: 0.84 us -> none  [gather_ordered(): ways.append(jnp.transpose(value, natural + tail).reshape((count,) + rest))]
  transfers between devices with their start and end apart: 12 -> 17, of which waited for: 9 -> 10; matrix products, arithmetic and copies ran while one was open for 12% -> 12% of each run, Pallas kernels for 0% -> 0%
where the time goes in v9:
time: 68.4 us; the launch traced here: 68.1 us
  waiting for transfers between devices  26.7 us (39%)
  starting transfers between devices  21.7 us (32%)
  matrix products  7.32 us (11%)
  other arithmetic  6.07 us (9%)
  local copies, waits for them, and re-layouts  5.15 us (8%)
  between operations  1.15 us (2%)
    ppermute x7, waiting for transfers between devices, exchange(): flat = lax.ppermute(flat, axis, pairs).astype(kind)  21.2 us
    ppermute x7, starting transfers between devices, exchange(): flat = lax.ppermute(flat, axis, pairs).astype(kind)  7.2 us
    ppermute x6, starting transfers between devices, gather_once(): g = lax.ppermute(value, axis, pairs)  6.3 us
    ppermute x3, starting transfers between devices, gather_ordered(): got = lax.ppermute(value, axis, pairs)  4.69 us
    ppermute x6, waiting for transfers between devices, gather_once(): g = lax.ppermute(value, axis, pairs)  3.71 us
    ppermute x1, starting transfers between devices, shifted(): lax.ppermute(value, axis, [(source, source + steps) for source in range(i...  3.49 us
    dot_general x1, matrix products, on_device(): lax.dot_general(inputs, dz, (((0,), (0,)), ((), ())), preferred_element_t...  1.93 us
    dot_general x1, matrix products, on_device(): z = jnp.dot(inputs, w_stack, preferred_element_type=jnp.float32)  1.91 us
  transfers between devices with their start and end apart: 17, of which 10 were waited for; matrix products, arithmetic and copies ran while one was open for 12% of the time, Pallas kernels for 0%

profile of v9, /device:TPU:0, one launch (start us, length us, event | category | flops | bytes accessed | tf_op | source)
XLA Modules:
  0.0 68.1 jit_solution(2722471425838607980)
XLA Ops:
  0.7 0.0 copy-start
  0.7 3.1 %collective-permute-start.1 = (bf16[8,512]{1,0:T(8,128)(2,1)}, bf16[8,512]{1,0:T(8,128)(2,1)S(1)}, u32[]{:S(2)}, u32[]{:S(2)}) collective-permute-start(bf16[8,512]{1,0:T(8,128)(2,1)} %param.8), channel_id=1, source_target_pairs={{0,16},{4,20},{8,24},{12,28},{16,0},{20,4},{24,8},{28,12},{1,17},{... | collective-permute-start | bytes 24584 | tf_op jit(solution)/shard_map/ppermute | solution.py:99
  3.7 0.9 %slice.54 = bf16[128,512]{1,0:T(8,128)(2,1)S(1)} slice(bf16[512,512]{1,0:T(8,128)(2,1)} %param.7), slice={[384:512], [0:512]} | slice | bytes 262144 | tf_op jit(solution)/shard_map/slice | solution.py:163
  4.6 3.5 %collective-permute-start = (bf16[128,512]{1,0:T(8,128)(2,1)S(1)}, bf16[128,512]{1,0:T(8,128)(2,1)S(1)}, u32[]{:S(2)}, u32[]{:S(2)}) collective-permute-start(bf16[128,512]{1,0:T(8,128)(2,1)S(1)} %slice.54), channel_id=1, source_target_pairs={{0,1},{1,2},{2,3},{4,5},{5,6},{6,7},{8,9},{9,10},{10,11},{12,13},{... | collective-permute-start | bytes 393224 | tf_op jit(solution)/shard_map/ppermute | solution.py:10
  8.1 0.7 %eq.70 = s32[4,4]{1,0:T(4,128)S(1)} reshape(s32[16]{0:T(128)} %param.10) | data formatting | bytes 128 | tf_op jit(solution)/shard_map/eq | solution.py:167
  8.9 0.1 iota_compare_fusion.4
  9.0 1.9 %select_reduce_fusion = s32[4,128,5,128]{3,1,2,0:T(8,128)S(1)} fusion(s32[4,4,128,128]{3,2,1,0:T(8,128)} %bitcast.123, pred[4,4,5]{2,1,0:T(4,128)(4,1)S(1)} %iota_compare_fusion.4), kind=kLoop, calls=%fused_computation.2 | loop fusion | flops 2293760 | bytes 2359376 | tf_op jit(solution)/shard_map/reduce_sum | solution.py:169
  10.9 0.0 collective-permute-done.1
  10.9 1.6 %collective-permute-start.2 = (bf16[2,8,512]{2,1,0:T(8,128)(2,1)S(1)}, bf16[2,8,512]{2,1,0:T(8,128)(2,1)S(1)}, u32[]{:S(2)}, u32[]{:S(2)}) collective-permute-start(bf16[2,8,512]{2,1,0:T(8,128)(2,1)S(1)} %pad_maximum_fusion.12), channel_id=1, source_target_pairs={{0,8},{4,12},{8,0},{12,4},{16,24},{20,28},{24,16},{28,20},{1,9},{5... | collective-permute-start | bytes 49160 | tf_op jit(solution)/shard_map/ppermute | solution.py:99
  12.5 0.3 reduce_sum.35
  12.9 1.8 %collective-permute-done.2 = bf16[2,8,512]{2,1,0:T(8,128)(2,1)S(1)} collective-permute-done((bf16[2,8,512]{2,1,0:T(8,128)(2,1)S(1)}, bf16[2,8,512]{2,1,0:T(8,128)(2,1)S(1)}, u32[]{:S(2)}, u32[]{:S(2)}) %collective-permute-start.2) | collective-permute-done | bytes 16416 | tf_op jit(solution)/shard_map/ppermute | solution.py:99
  14.7 0.1 collective-permute-start.3
  14.8 0.2 copy.30
  15.1 0.1 convert_element_type.48
  15.2 0.9 %copy.27 = bf16[4,128,5,128]{1,0,3,2:T(4,128)(2,1)S(1)} copy(bf16[4,128,5,128]{3,1,2,0:T(8,128)(2,1)S(1)} %convert_element_type.48) | data formatting | bytes 1310720 | tf_op jit(solution)/shard_map/convert_element_type | solution.py:171
  16.1 0.0 collective-permute-done.3
  16.2 0.9 %fusion.16 = f32[512,512]{0,1:T(8,128)S(1)} fusion(bf16[64,512]{1,0:T(8,128)(2,1)S(1)} %bitcast.132, s32[512]{0:T(512)S(1)} %bitcast.139, s32[512]{0:T(512)S(1)} %bitcast.141, s32[512]{0:T(512)S(1)} %bitcast.137, s32[512]{0:T(512)S(1)} %bitcast.135), kind=kOutput, calls=%fused_computation.42 | convolution fusion | flops 33947648 | bytes 1122304 | tf_op jit(solution)/shard_map/dot_general | solution.py:179
  17.1 0.0 collective-permute-done
  17.1 0.0 copy-start.6
  17.2 0.0 copy-start.7
  17.2 0.7 fusion.2
  17.8 0.5 copy-done.6
  18.4 0.1 copy-done.7
  18.5 1.9 %multiply_convert_fusion = (bf16[512,512]{1,0:T(8,128)(2,1)S(1)}, bf16[512,512]{1,0:T(8,128)(2,1)}) fusion(bf16[512,512]{1,0:T(8,128)(2,1)S(1)} %copy-done.7, bf16[1024,512]{1,0:T(8,128)(2,1)S(1)} %copy-done.6, bf16[512,512]{0,1:T(8,128)(2,1)S(1)} %fusion.2, bf16[512,512]{0,1:T(8,128)(2,1)S(1)} %copy.30), kind=kOutput, calls=%fused_computation.12 | convolution fusion | flops 542113792 | bytes 3670016 | tf_op jit(solution)/shard_map/dot_general | solution.py:182
  20.4 1.9 %fusion.5 = f32[1024,512]{1,0:T(8,128)S(1)} fusion(bf16[512,512]{1,0:T(8,128)(2,1)S(1)} %get-tuple-element.5, bf16[512,512]{0,1:T(8,128)(2,1)S(1)} %fusion.2, bf16[512,512]{0,1:T(8,128)(2,1)} %copy-done.1), kind=kOutput, calls=%fused_computation.15 | convolution fusion | flops 538968064 | bytes 3670016 | tf_op jit(solution)/shard_map/dot_general | solution.py:186
  22.3 0.1 constant_dynamic-slice_fusion.4
  22.5 0.6 collective-permute-start.4
  23.0 1.9 %fusion.4 = f32[64,512]{1,0:T(8,128)S(1)} fusion(bf16[512,512]{1,0:T(8,128)(2,1)} %copy-done.3, bf16[1024,512]{1,0:T(8,128)(2,1)} %param.12, f32[512]{0:T(512)S(1)} %add_bitcast_fusion, s32[512]{0:T(512)S(1)} %bitcast.140, s32[512]{0:T(512)S(1)} %bitcast.142, s32[512]{0:T(512)S(1)} %bitcast.138, s32[512]{0:T(512)S(1)} %bitcast.136), kind=kOutput, calls=%fused_computation.9 | convolution fusion | flops 302907392 | bytes 1189888 | tf_op jit(solution)/shard_map/dot_general | solution.py:193
  25.0 0.5 collective-permute-done.4
  25.4 1.4 %bitcast_add_fusion = f32[4,2,2,32,512]{4,3,2,1,0:T(8,128)S(1)} fusion(f32[4,2,2,32,512]{4,3,2,1,0:T(8,128)} %bitcast.20, f32[4,2,2,2,32,512]{5,4,3,2,1,0:T(8,128)S(1)} %bitcast.122, s32[]{:T(128)S(6)} %select_n.225), kind=kLoop, calls=%fused_computation.11 | loop fusion | flops 262144 | bytes 3145732 | tf_op jit(solution)/shard_map/add | solution.py:72
  27.0 0.1 bitcast_select_fusion.1
  27.1 1.6 %collective-permute-start.5 = (f32[288,512]{1,0:T(8,128)S(1)}, f32[288,512]{1,0:T(8,128)S(1)}, u32[]{:S(2)}, u32[]{:S(2)}) collective-permute-start(f32[288,512]{1,0:T(8,128)S(1)} %pad_maximum_fusion.3), channel_id=1, source_target_pairs={{0,8},{4,20},{8,0},{12,28},{16,24},{20,4},{24,16},{28,12},{1,9},{5... | collective-permute-start | bytes 1769480 | tf_op jit(solution)/shard_map/ppermute | solution.py:29
  28.6 0.1 broadcast_in_dim.53
  28.7 0.1 broadcast_in_dim.54
  28.8 8.2 %collective-permute-done.5 = f32[288,512]{1,0:T(8,128)S(1)} collective-permute-done((f32[288,512]{1,0:T(8,128)S(1)}, f32[288,512]{1,0:T(8,128)S(1)}, u32[]{:S(2)}, u32[]{:S(2)}) %collective-permute-start.5) | collective-permute-done | bytes 589856 | tf_op jit(solution)/shard_map/ppermute | solution.py:29
  37.1 0.2 fusion.12
  37.4 0.6 collective-permute-start.6
  38.0 6.2 %collective-permute-done.6 = f32[144,512]{1,0:T(8,128)S(1)} collective-permute-done((f32[144,512]{1,0:T(8,128)S(1)}, f32[144,512]{1,0:T(8,128)S(1)}, u32[]{:S(2)}, u32[]{:S(2)}) %collective-permute-start.6) | collective-permute-done | bytes 294944 | tf_op jit(solution)/shard_map/ppermute | solution.py:29
  44.2 0.1 bitcast_add_fusion.1
  44.3 1.5 %collective-permute-start.9 = (f32[48,512]{1,0:T(8,128)S(1)}, f32[48,512]{1,0:T(8,128)S(1)}, u32[]{:S(2)}, u32[]{:S(2)}) collective-permute-start(f32[48,512]{1,0:T(8,128)S(1)} %get-tuple-element.14), channel_id=1, source_target_pairs={{0,3},{1,2},{2,1},{3,0},{4,7},{5,6},{6,5},{7,4},{8,11},{9,10},{10,... | collective-permute-start | bytes 294920 | tf_op jit(solution)/shard_map/ppermute | solution.py:29
  45.8 1.6 %collective-permute-start.8 = (f32[48,512]{1,0:T(8,128)S(1)}, f32[48,512]{1,0:T(8,128)S(1)}, u32[]{:S(2)}, u32[]{:S(2)}) collective-permute-start(f32[48,512]{1,0:T(8,128)S(1)} %get-tuple-element.13), channel_id=1, source_target_pairs={{0,2},{1,3},{2,0},{3,1},{4,6},{5,7},{6,4},{7,5},{8,10},{9,11},{10,... | collective-permute-start | bytes 294920 | tf_op jit(solution)/shard_map/ppermute | solution.py:29
  47.4 1.4 %collective-permute-start.7 = (f32[48,512]{1,0:T(8,128)S(1)}, f32[48,512]{1,0:T(8,128)S(1)}, u32[]{:S(2)}, u32[]{:S(2)}) collective-permute-start(f32[48,512]{1,0:T(8,128)S(1)} %get-tuple-element.12), channel_id=1, source_target_pairs={{0,1},{1,0},{2,3},{3,2},{4,5},{5,4},{6,7},{7,6},{8,9},{9,8},{10,11... | collective-permute-start | bytes 294920 | tf_op jit(solution)/shard_map/ppermute | solution.py:29
  48.8 3.1 %collective-permute-done.9 = f32[48,512]{1,0:T(8,128)S(1)} collective-permute-done((f32[48,512]{1,0:T(8,128)S(1)}, f32[48,512]{1,0:T(8,128)S(1)}, u32[]{:S(2)}, u32[]{:S(2)}) %collective-permute-start.9) | collective-permute-done | bytes 98336 | tf_op jit(solution)/shard_map/ppermute | solution.py:29
  51.9 3.2 %collective-permute-done.8 = f32[48,512]{1,0:T(8,128)S(1)} collective-permute-done((f32[48,512]{1,0:T(8,128)S(1)}, f32[48,512]{1,0:T(8,128)S(1)}, u32[]{:S(2)}, u32[]{:S(2)}) %collective-permute-start.8) | collective-permute-done | bytes 98336 | tf_op jit(solution)/shard_map/ppermute | solution.py:29
  55.1 0.0 collective-permute-done.7
  55.1 0.6 gather_fusion
  55.7 0.1 select_reduce_fusion.1
  55.8 0.1 collective-permute-start.10
  55.9 1.6 %collective-permute-start.11 = (f32[32,512]{1,0:T(8,128)S(1)}, f32[32,512]{1,0:T(8,128)S(1)}, u32[]{:S(2)}, u32[]{:S(2)}) collective-permute-start(f32[32,512]{1,0:T(8,128)S(1)} %get-tuple-element.4), channel_id=1, source_target_pairs={{0,8},{4,12},{8,0},{12,4},{16,24},{20,28},{24,16},{28,20},{1,9},{5... | collective-permute-start | bytes 196616 | tf_op jit(solution)/shard_map/ppermute | solution.py:145
  57.5 0.3 collective-permute-start.12
  57.8 0.5 collective-permute-start.13
  58.3 1.2 %collective-permute-start.14 = (f32[32,512]{1,0:T(8,128)S(1)}, f32[32,512]{1,0:T(8,128)S(1)}, u32[]{:S(2)}, u32[]{:S(2)}) collective-permute-start(f32[32,512]{1,0:T(8,128)S(1)} %get-tuple-element.4), channel_id=1, source_target_pairs={{0,20},{4,16},{8,28},{12,24},{16,4},{20,0},{24,12},{28,8},{1,21},{... | collective-permute-start | bytes 196616 | tf_op jit(solution)/shard_map/ppermute | solution.py:145
  59.5 0.0 collective-permute-done.10
  59.5 1.4 %collective-permute-start.15 = (f32[32,512]{1,0:T(8,128)S(1)}, f32[32,512]{1,0:T(8,128)S(1)}, u32[]{:S(2)}, u32[]{:S(2)}) collective-permute-start(f32[32,512]{1,0:T(8,128)S(1)} %get-tuple-element.4), channel_id=1, source_target_pairs={{0,24},{4,28},{8,16},{12,20},{16,8},{20,12},{24,0},{28,4},{1,25},{... | collective-permute-start | bytes 196616 | tf_op jit(solution)/shard_map/ppermute | solution.py:145
  60.9 0.0 collective-permute-done.11
  60.9 1.3 %collective-permute-start.16 = (f32[32,512]{1,0:T(8,128)S(1)}, f32[32,512]{1,0:T(8,128)S(1)}, u32[]{:S(2)}, u32[]{:S(2)}) collective-permute-start(f32[32,512]{1,0:T(8,128)S(1)} %get-tuple-element.4), channel_id=1, source_target_pairs={{0,28},{4,24},{8,20},{12,16},{16,12},{20,8},{24,4},{28,0},{1,29},{... | collective-permute-start | bytes 196616 | tf_op jit(solution)/shard_map/ppermute | solution.py:145
  62.2 0.0 collective-permute-done.12
  62.3 0.5 collective-permute-done.13
  62.7 0.2 collective-permute-done.14
  62.9 2.0 %collective-permute-done.15 = f32[32,512]{1,0:T(8,128)S(1)} collective-permute-done((f32[32,512]{1,0:T(8,128)S(1)}, f32[32,512]{1,0:T(8,128)S(1)}, u32[]{:S(2)}, u32[]{:S(2)}) %collective-permute-start.15) | collective-permute-done | bytes 65568 | tf_op jit(solution)/shard_map/ppermute | solution.py:145
  64.9 1.1 %collective-permute-done.16 = f32[32,512]{1,0:T(8,128)S(1)} collective-permute-done((f32[32,512]{1,0:T(8,128)S(1)}, f32[32,512]{1,0:T(8,128)S(1)}, u32[]{:S(2)}, u32[]{:S(2)}) %collective-permute-start.16) | collective-permute-done | bytes 65568 | tf_op jit(solution)/shard_map/ppermute | solution.py:145
  66.0 0.6 gather_fusion.1
  66.6 0.9 %bitcast_select_fusion = f32[256,512]{1,0:T(8,128)} fusion(f32[8,32,512]{2,1,0:T(8,128)S(1)} %gather_fusion.1, pred[256]{0:T(512)(128)(4,1)S(1)} %broadcast_in_dim.54), kind=kLoop, calls=%fused_computation.23 | loop fusion | flops 131072 | bytes 1048832 | tf_op jit(solution)/shard_map/jit(_take)/select_n | solution.py:148
  67.5 0.6 slice_add_fusion.3
  (57 shorter events, 0.6 us)
Async XLA Ops:
  0.6 10.2 %copy-start.5 = (bf16[8,512]{1,0:T(8,128)(2,1)S(1)}, bf16[8,512]{1,0:T(8,128)(2,1)}, u32[]{:S(2)}) copy-start(bf16[8,512]{1,0:T(8,128)(2,1)} %param.8) | copy-start | bytes 24580
  0.6 14.2 %copy-start.2 = (bf16[512,512]{1,0:T(8,128)(2,1)S(1)}, bf16[512,512]{1,0:T(8,128)(2,1)}, u32[]{:S(2)}) copy-start(bf16[512,512]{1,0:T(8,128)(2,1)} %param.7) | copy-start | bytes 1572868
  0.7 11.8 %copy-start = (s32[16,128,128]{2,1,0:T(8,128)S(1)}, s32[16,128,128]{2,1,0:T(8,128)}, u32[]{:S(2)}) copy-start(s32[16,128,128]{2,1,0:T(8,128)} %param.11) | copy-start | bytes 3145732
  0.7 11.8 %copy-start.4 = (s32[512,4]{0,1:T(4,128)S(1)}, s32[512,4]{0,1:T(4,128)}, u32[]{:S(2)}) copy-start(s32[512,4]{0,1:T(4,128)} %param.9) | copy-start | bytes 24580
  0.7 10.2 %collective-permute-start.1 = (bf16[8,512]{1,0:T(8,128)(2,1)}, bf16[8,512]{1,0:T(8,128)(2,1)S(1)}, u32[]{:S(2)}, u32[]{:S(2)}) collective-permute-start(bf16[8,512]{1,0:T(8,128)(2,1)} %param.8), channel_id=1, source_target_pairs={{0,16},{4,20},{8,24},{12,28},{16,0},{20,4},{24,8},{28,12},{1,17},{... | collective-permute-start | bytes 24584 | tf_op jit(solution)/shard_map/ppermute | solution.py:99
  4.6 12.5 %collective-permute-start = (bf16[128,512]{1,0:T(8,128)(2,1)S(1)}, bf16[128,512]{1,0:T(8,128)(2,1)S(1)}, u32[]{:S(2)}, u32[]{:S(2)}) collective-permute-start(bf16[128,512]{1,0:T(8,128)(2,1)S(1)} %slice.54), channel_id=1, source_target_pairs={{0,1},{1,2},{2,3},{4,5},{5,6},{6,7},{8,9},{9,10},{10,11},{12,13},{... | collective-permute-start | bytes 393224 | tf_op jit(solution)/shard_map/ppermute | solution.py:10
  10.9 3.8 %collective-permute-start.2 = (bf16[2,8,512]{2,1,0:T(8,128)(2,1)S(1)}, bf16[2,8,512]{2,1,0:T(8,128)(2,1)S(1)}, u32[]{:S(2)}, u32[]{:S(2)}) collective-permute-start(bf16[2,8,512]{2,1,0:T(8,128)(2,1)S(1)} %pad_maximum_fusion.12), channel_id=1, source_target_pairs={{0,8},{4,12},{8,0},{12,4},{16,24},{20,28},{24,16},{28,20},{1,9},{5... | collective-permute-start | bytes 49160 | tf_op jit(solution)/shard_map/ppermute | solution.py:99
  14.7 1.4 %collective-permute-start.3 = (bf16[2,2,8,512]{3,2,0,1:T(8,128)(2,1)S(1)}, bf16[2,2,8,512]{3,2,0,1:T(8,128)(2,1)S(1)}, u32[]{:S(2)}, u32[]{:S(2)}) collective-permute-start(bf16[2,2,8,512]{3,2,0,1:T(8,128)(2,1)S(1)} %pad_maximum_fusion.11), channel_id=1, source_target_pairs={{0,4},{4,0},{8,12},{12,8},{16,20},{20,16},{24,28},{28,24},{1,5},{5... | collective-permute-start | bytes 98312 | tf_op jit(solution)/shard_map/ppermute | solution.py:99
  15.0 2.8 %copy-start.1 = (bf16[512,512]{0,1:T(8,128)(2,1)}, bf16[512,512]{0,1:T(8,128)(2,1)S(1)}, u32[]{:S(2)}) copy-start(bf16[512,512]{0,1:T(8,128)(2,1)S(1)} %copy.30) | copy-start | bytes 1572868
  17.1 1.2 %copy-start.6 = (bf16[1024,512]{1,0:T(8,128)(2,1)S(1)}, bf16[1024,512]{1,0:T(8,128)(2,1)}, u32[]{:S(2)}) copy-start(bf16[1024,512]{1,0:T(8,128)(2,1)} %param.12) | copy-start | bytes 3145732
  17.2 1.3 %copy-start.7 = (bf16[512,512]{1,0:T(8,128)(2,1)S(1)}, bf16[512,512]{1,0:T(8,128)(2,1)}, u32[]{:S(2)}) copy-start(bf16[512,512]{1,0:T(8,128)(2,1)} %param.13) | copy-start | bytes 1572868
  20.4 2.0 %copy-start.3 = (bf16[512,512]{1,0:T(8,128)(2,1)}, bf16[512,512]{1,0:T(8,128)(2,1)S(1)}, u32[]{:S(2)}) copy-start(bf16[512,512]{1,0:T(8,128)(2,1)S(1)} %get-tuple-element.5) | copy-start | bytes 1572868
  22.5 3.0 %collective-permute-start.4 = (f32[512,512]{1,0:T(8,128)S(1)}, f32[512,512]{1,0:T(8,128)}, u32[]{:S(2)}, u32[]{:S(2)}) collective-permute-start(f32[512,512]{1,0:T(8,128)S(1)} %bitcast.125), channel_id=1, source_target_pairs={{0,4},{4,0},{8,12},{12,8},{16,20},{20,16},{24,28},{28,24},{1,5},{5... | collective-permute-start | bytes 3145736 | tf_op jit(solution)/shard_map/ppermute | solution.py:29
  27.1 9.9 %collective-permute-start.5 = (f32[288,512]{1,0:T(8,128)S(1)}, f32[288,512]{1,0:T(8,128)S(1)}, u32[]{:S(2)}, u32[]{:S(2)}) collective-permute-start(f32[288,512]{1,0:T(8,128)S(1)} %pad_maximum_fusion.3), channel_id=1, source_target_pairs={{0,8},{4,20},{8,0},{12,28},{16,24},{20,4},{24,16},{28,12},{1,9},{5... | collective-permute-start | bytes 1769480 | tf_op jit(solution)/shard_map/ppermute | solution.py:29
  37.4 6.8 %collective-permute-start.6 = (f32[144,512]{1,0:T(8,128)S(1)}, f32[144,512]{1,0:T(8,128)S(1)}, u32[]{:S(2)}, u32[]{:S(2)}) collective-permute-start(f32[144,512]{1,0:T(8,128)S(1)} %pad_maximum_fusion.4), channel_id=1, source_target_pairs={{0,16},{4,12},{8,24},{12,4},{16,0},{20,28},{24,8},{28,20},{1,17},{... | collective-permute-start | bytes 884744 | tf_op jit(solution)/shard_map/ppermute | solution.py:29
  44.3 7.5 %collective-permute-start.9 = (f32[48,512]{1,0:T(8,128)S(1)}, f32[48,512]{1,0:T(8,128)S(1)}, u32[]{:S(2)}, u32[]{:S(2)}) collective-permute-start(f32[48,512]{1,0:T(8,128)S(1)} %get-tuple-element.14), channel_id=1, source_target_pairs={{0,3},{1,2},{2,1},{3,0},{4,7},{5,6},{6,5},{7,4},{8,11},{9,10},{10,... | collective-permute-start | bytes 294920 | tf_op jit(solution)/shard_map/ppermute | solution.py:29
  45.8 9.3 %collective-permute-start.8 = (f32[48,512]{1,0:T(8,128)S(1)}, f32[48,512]{1,0:T(8,128)S(1)}, u32[]{:S(2)}, u32[]{:S(2)}) collective-permute-start(f32[48,512]{1,0:T(8,128)S(1)} %get-tuple-element.13), channel_id=1, source_target_pairs={{0,2},{1,3},{2,0},{3,1},{4,6},{5,7},{6,4},{7,5},{8,10},{9,11},{10,... | collective-permute-start | bytes 294920 | tf_op jit(solution)/shard_map/ppermute | solution.py:29
  47.4 7.7 %collective-permute-start.7 = (f32[48,512]{1,0:T(8,128)S(1)}, f32[48,512]{1,0:T(8,128)S(1)}, u32[]{:S(2)}, u32[]{:S(2)}) collective-permute-start(f32[48,512]{1,0:T(8,128)S(1)} %get-tuple-element.12), channel_id=1, source_target_pairs={{0,1},{1,0},{2,3},{3,2},{4,5},{5,4},{6,7},{7,6},{8,9},{9,8},{10,11... | collective-permute-start | bytes 294920 | tf_op jit(solution)/shard_map/ppermute | solution.py:29
  55.8 3.7 %collective-permute-start.10 = (f32[40,512]{1,0:T(8,128)S(1)}, f32[40,512]{1,0:T(8,128)S(1)}, u32[]{:S(2)}, u32[]{:S(2)}) collective-permute-start(f32[40,512]{1,0:T(8,128)S(1)} %pad_maximum_fusion.9), channel_id=1, source_target_pairs={{0,4},{4,0},{8,12},{12,8},{16,20},{20,16},{24,28},{28,24},{1,5},{5... | collective-permute-start | bytes 245768 | tf_op jit(solution)/shard_map/ppermute | solution.py:29
  55.9 5.0 %collective-permute-start.11 = (f32[32,512]{1,0:T(8,128)S(1)}, f32[32,512]{1,0:T(8,128)S(1)}, u32[]{:S(2)}, u32[]{:S(2)}) collective-permute-start(f32[32,512]{1,0:T(8,128)S(1)} %get-tuple-element.4), channel_id=1, source_target_pairs={{0,8},{4,12},{8,0},{12,4},{16,24},{20,28},{24,16},{28,20},{1,9},{5... | collective-permute-start | bytes 196616 | tf_op jit(solution)/shard_map/ppermute | solution.py:145
  57.5 4.8 %collective-permute-start.12 = (f32[32,512]{1,0:T(8,128)S(1)}, f32[32,512]{1,0:T(8,128)S(1)}, u32[]{:S(2)}, u32[]{:S(2)}) collective-permute-start(f32[32,512]{1,0:T(8,128)S(1)} %get-tuple-element.4), channel_id=1, source_target_pairs={{0,12},{4,8},{8,4},{12,0},{16,28},{20,24},{24,20},{28,16},{1,13},{... | collective-permute-start | bytes 196616 | tf_op jit(solution)/shard_map/ppermute | solution.py:145
  57.8 5.0 %collective-permute-start.13 = (f32[32,512]{1,0:T(8,128)S(1)}, f32[32,512]{1,0:T(8,128)S(1)}, u32[]{:S(2)}, u32[]{:S(2)}) collective-permute-start(f32[32,512]{1,0:T(8,128)S(1)} %get-tuple-element.4), channel_id=1, source_target_pairs={{0,16},{4,20},{8,24},{12,28},{16,0},{20,4},{24,8},{28,12},{1,17},{... | collective-permute-start | bytes 196616 | tf_op jit(solution)/shard_map/ppermute | solution.py:145
  58.3 4.7 %collective-permute-start.14 = (f32[32,512]{1,0:T(8,128)S(1)}, f32[32,512]{1,0:T(8,128)S(1)}, u32[]{:S(2)}, u32[]{:S(2)}) collective-permute-start(f32[32,512]{1,0:T(8,128)S(1)} %get-tuple-element.4), channel_id=1, source_target_pairs={{0,20},{4,16},{8,28},{12,24},{16,4},{20,0},{24,12},{28,8},{1,21},{... | collective-permute-start | bytes 196616 | tf_op jit(solution)/shard_map/ppermute | solution.py:145
  59.5 5.4 %collective-permute-start.15 = (f32[32,512]{1,0:T(8,128)S(1)}, f32[32,512]{1,0:T(8,128)S(1)}, u32[]{:S(2)}, u32[]{:S(2)}) collective-permute-start(f32[32,512]{1,0:T(8,128)S(1)} %get-tuple-element.4), channel_id=1, source_target_pairs={{0,24},{4,28},{8,16},{12,20},{16,8},{20,12},{24,0},{28,4},{1,25},{... | collective-permute-start | bytes 196616 | tf_op jit(solution)/shard_map/ppermute | solution.py:145
  60.9 5.1 %collective-permute-start.16 = (f32[32,512]{1,0:T(8,128)S(1)}, f32[32,512]{1,0:T(8,128)S(1)}, u32[]{:S(2)}, u32[]{:S(2)}) collective-permute-start(f32[32,512]{1,0:T(8,128)S(1)} %get-tuple-element.4), channel_id=1, source_target_pairs={{0,28},{4,24},{8,20},{12,16},{16,12},{20,8},{24,4},{28,0},{1,29},{... | collective-permute-start | bytes 196616 | tf_op jit(solution)/shard_map/ppermute | solution.py:145

commit v10 on v7

--- a/solution.py
+++ b/solution.py
@@ -158,7 +158,7 @@
     partial_h = partial_h.reshape(regions, owned, width)
     (region_w, region_h), _ = scatter_sum(
         [partial_w, partial_h], "region", [1, 0], up, up[:1] + up[1:][::-1], joins=[0, 1],
-        wires=None,
+        wires=[None, jnp.bfloat16] + [None] * (len(up) - 2),
     )
     (piece_w,), (region_h,) = scatter_sum(
         [region_w], "dom", [0], list(range(log2(doms))), riders=[region_h],

time: 67.5 us -> 64.3 us (0.953)
  waiting for transfers between devices: 32.7 us -> 29.5 us
    ppermute x6, waiting for transfers between devices: 23.3 us -> 20.1 us  [exchange(): flat = lax.ppermute(flat, axis, pairs).astype(kind)]
  transfers between devices with their start and end apart: 12 -> 12, of which waited for: 9 -> 9; matrix products, arithmetic and copies ran while one was open for 12% -> 13% of each run, Pallas kernels for 0% -> 0%
where the time goes in v10:
time: 64.3 us; the launch traced here: 64 us
  waiting for transfers between devices  29.5 us (46%)
  starting transfers between devices  17.3 us (27%)
  matrix products  6.09 us (9%)
  other arithmetic  5.27 us (8%)
  local copies, waits for them, and re-layouts  4.69 us (7%)
  between operations  1.14 us (2%)
    ppermute x6, waiting for transfers between devices, exchange(): flat = lax.ppermute(flat, axis, pairs).astype(kind)  20.1 us
    ppermute x5, waiting for transfers between devices, gather_ordered(): got = lax.ppermute(value, axis, pairs)  9.37 us
    ppermute x6, starting transfers between devices, exchange(): flat = lax.ppermute(flat, axis, pairs).astype(kind)  7.03 us
    ppermute x5, starting transfers between devices, gather_ordered(): got = lax.ppermute(value, axis, pairs)  6.81 us
    ppermute x1, starting transfers between devices, shifted(): lax.ppermute(value, axis, [(source, source + steps) for source in range(i...  3.49 us
    dot_general x1, matrix products, on_device(): z = jnp.dot(inputs, w_stack, preferred_element_type=jnp.float32)  1.9 us
    reduce_sum x1, other arithmetic, on_device(): links = jnp.where(chosen[:, :, None, :, None], masks, 0).sum(axis=1)  1.88 us
    dot_general x1, matrix products, on_device(): lax.dot_general(counts, sgrad, (((0,), (0,)), ((), ())), preferred_elemen...  1.88 us
  transfers between devices with their start and end apart: 12, of which 9 were waited for; matrix products, arithmetic and copies ran while one was open for 13% of the time, Pallas kernels for 0%

profile of v10, /device:TPU:0, one launch (start us, length us, event | category | flops | bytes accessed | tf_op | source)
XLA Modules:
  0.0 64.0 jit_solution(6258369013128677306)
XLA Ops:
  0.6 0.0 copy-start.4
  0.6 0.0 copy-start.1
  0.7 0.0 copy-start
  0.7 0.0 copy-start.3
  0.7 3.1 %collective-permute-start.1 = (bf16[8,512]{1,0:T(8,128)(2,1)}, bf16[8,512]{1,0:T(8,128)(2,1)S(1)}, u32[]{:S(2)}, u32[]{:S(2)}) collective-permute-start(bf16[8,512]{1,0:T(8,128)(2,1)} %param.8), channel_id=1, source_target_pairs={{0,16},{4,20},{8,24},{12,28},{16,0},{20,4},{24,8},{28,12},{1,17},{... | collective-permute-start | bytes 24584 | tf_op jit(solution)/shard_map/ppermute | solution.py:99
  3.7 0.9 %slice.48 = bf16[128,512]{1,0:T(8,128)(2,1)S(1)} slice(bf16[512,512]{1,0:T(8,128)(2,1)} %param.7), slice={[384:512], [0:512]} | slice | bytes 262144 | tf_op jit(solution)/shard_map/slice | solution.py:127
  4.6 3.5 %collective-permute-start = (bf16[128,512]{1,0:T(8,128)(2,1)S(1)}, bf16[128,512]{1,0:T(8,128)(2,1)S(1)}, u32[]{:S(2)}, u32[]{:S(2)}) collective-permute-start(bf16[128,512]{1,0:T(8,128)(2,1)S(1)} %slice.48), channel_id=1, source_target_pairs={{0,1},{1,2},{2,3},{4,5},{5,6},{6,7},{8,9},{9,10},{10,11},{12,13},{... | collective-permute-start | bytes 393224 | tf_op jit(solution)/shard_map/ppermute | solution.py:10
  8.1 0.7 %eq.81 = s32[4,4]{1,0:T(4,128)S(1)} reshape(s32[16]{0:T(128)} %param.10) | data formatting | bytes 128 | tf_op jit(solution)/shard_map/eq | solution.py:131
  8.9 0.1 iota_compare_fusion.4
  9.0 1.9 %select_reduce_fusion = s32[4,128,5,128]{3,1,2,0:T(8,128)S(1)} fusion(s32[4,4,128,128]{3,2,1,0:T(8,128)} %bitcast.130, pred[4,4,5]{2,1,0:T(4,128)(4,1)S(1)} %iota_compare_fusion.4), kind=kLoop, calls=%fused_computation | loop fusion | flops 2293760 | bytes 2359376 | tf_op jit(solution)/shard_map/reduce_sum | solution.py:133
  10.9 0.0 collective-permute-done.1
  10.9 0.0 copy-done.4
  10.9 1.6 %collective-permute-start.2 = (bf16[2,8,512]{2,1,0:T(8,128)(2,1)S(1)}, bf16[2,8,512]{2,1,0:T(8,128)(2,1)S(1)}, u32[]{:S(2)}, u32[]{:S(2)}) collective-permute-start(bf16[2,8,512]{2,1,0:T(8,128)(2,1)S(1)} %pad_maximum_fusion.12), channel_id=1, source_target_pairs={{0,8},{4,12},{8,0},{12,4},{16,24},{20,28},{24,16},{28,20},{1,9},{5... | collective-permute-start | bytes 49160 | tf_op jit(solution)/shard_map/ppermute | solution.py:99
  12.5 0.0 copy-done.3
  12.5 0.0 copy-done
  12.5 0.3 reduce_sum.26
  12.9 1.8 %collective-permute-done.2 = bf16[2,8,512]{2,1,0:T(8,128)(2,1)S(1)} collective-permute-done((bf16[2,8,512]{2,1,0:T(8,128)(2,1)S(1)}, bf16[2,8,512]{2,1,0:T(8,128)(2,1)S(1)}, u32[]{:S(2)}, u32[]{:S(2)}) %collective-permute-start.2) | collective-permute-done | bytes 16416 | tf_op jit(solution)/shard_map/ppermute | solution.py:99
  14.7 0.1 collective-permute-start.3
  14.8 0.0 copy-done.1
  14.8 0.2 copy.36
  15.0 0.1 convert_element_type.52
  15.2 0.9 %copy.33 = bf16[4,128,5,128]{1,0,3,2:T(4,128)(2,1)S(1)} copy(bf16[4,128,5,128]{3,1,2,0:T(8,128)(2,1)S(1)} %convert_element_type.52) | data formatting | bytes 1310720 | tf_op jit(solution)/shard_map/convert_element_type | solution.py:135
  16.1 0.0 collective-permute-done.3
  16.2 0.9 %fusion.17 = f32[512,512]{0,1:T(8,128)S(1)} fusion(bf16[64,512]{1,0:T(8,128)(2,1)S(1)} %bitcast.145, s32[512]{0:T(512)S(1)} %bitcast.152, s32[512]{0:T(512)S(1)} %bitcast.154, s32[512]{0:T(512)S(1)} %bitcast.150, s32[512]{0:T(512)S(1)} %bitcast.148), kind=kOutput, calls=%fused_computation.47 | convolution fusion | flops 33947648 | bytes 1122304 | tf_op jit(solution)/shard_map/dot_general | solution.py:143
  17.1 0.0 collective-permute-done
  17.1 0.0 copy-start.5
  17.1 0.0 copy-start.6
  17.2 0.7 %fusion.2 = bf16[512,512]{0,1:T(8,128)(2,1)S(1)} fusion(f32[512,512]{0,1:T(8,128)S(1)} %fusion.17, bf16[512,512]{0,1:T(8,128)(2,1)S(1)} %copy.36, bf16[80,8,4,128]{3,2,1,0:T(4,128)(2,1)S(1)} %bitcast.138, bf16[512,512]{1,0:T(8,128)(2,1)S(1)} %copy-done.1, bf16[128,512]{1,0:T(8,128)(2,1)S(1)} %collective-permute-done, f32[512]{0:T(512)S(1)} %add_bitcast_fusion), kind=kOutput, calls=%fused_computation.5 | convolution fusion | flops 338165760 | bytes 3409920 | tf_op jit(solution)/shard_map/dot_general | solution.py:135
  17.8 0.5 copy-done.5
  18.4 0.1 copy-done.6
  18.5 1.9 %multiply_convert_fusion = (bf16[512,512]{1,0:T(8,128)(2,1)S(1)}, bf16[512,512]{1,0:T(8,128)(2,1)}) fusion(bf16[512,512]{1,0:T(8,128)(2,1)S(1)} %copy-done.6, bf16[1024,512]{1,0:T(8,128)(2,1)S(1)} %copy-done.5, bf16[512,512]{0,1:T(8,128)(2,1)S(1)} %fusion.2, bf16[512,512]{0,1:T(8,128)(2,1)S(1)} %copy.36), kind=kOutput, calls=%fused_computation.10 | convolution fusion | flops 542113792 | bytes 3670016 | tf_op jit(solution)/shard_map/dot_general | solution.py:146
  20.4 0.0 copy-start.2
  20.4 0.7 %fusion.5 = f32[1024,512]{1,0:T(8,128)S(1)} fusion(bf16[512,512]{1,0:T(8,128)(2,1)S(1)} %get-tuple-element.3, bf16[512,512]{0,1:T(8,128)(2,1)S(1)} %fusion.2, bf16[512,512]{0,1:T(8,128)(2,1)S(1)} %copy.36), kind=kOutput, calls=%fused_computation.13 | convolution fusion | flops 538968064 | bytes 3670016 | tf_op jit(solution)/shard_map/dot_general | solution.py:150
  21.1 0.1 constant_dynamic-slice_fusion.5
  21.2 0.0 copy-done.2
  21.2 0.5 collective-permute-start.4
  21.8 1.9 %fusion.4 = f32[64,512]{1,0:T(8,128)S(1)} fusion(bf16[512,512]{1,0:T(8,128)(2,1)} %copy-done.2, bf16[1024,512]{1,0:T(8,128)(2,1)} %param.12, f32[512]{0:T(512)S(1)} %add_bitcast_fusion, s32[512]{0:T(512)S(1)} %bitcast.153, s32[512]{0:T(512)S(1)} %bitcast.155, s32[512]{0:T(512)S(1)} %bitcast.151, s32[512]{0:T(512)S(1)} %bitcast.149), kind=kOutput, calls=%fused_computation.7 | convolution fusion | flops 302907392 | bytes 1189888 | tf_op jit(solution)/shard_map/dot_general | solution.py:157
  23.7 0.5 collective-permute-done.4
  24.2 1.4 %bitcast_add_fusion = f32[4,2,2,32,512]{4,3,2,1,0:T(8,128)S(1)} fusion(f32[4,2,2,32,512]{4,3,2,1,0:T(8,128)} %bitcast.20, f32[4,2,2,2,32,512]{5,4,3,2,1,0:T(8,128)S(1)} %bitcast.129, s32[]{:T(128)S(6)} %select_n.243), kind=kLoop, calls=%fused_computation.9 | loop fusion | flops 262144 | bytes 3145732 | tf_op jit(solution)/shard_map/add | solution.py:72
  25.7 0.1 fusion.12
  25.8 1.6 %collective-permute-start.5 = (bf16[288,512]{1,0:T(8,128)(2,1)S(1)}, bf16[288,512]{1,0:T(8,128)(2,1)S(1)}, u32[]{:S(2)}, u32[]{:S(2)}) collective-permute-start(bf16[288,512]{1,0:T(8,128)(2,1)S(1)} %pad_maximum_fusion.3), channel_id=1, source_target_pairs={{0,8},{4,20},{8,0},{12,28},{16,24},{20,4},{24,16},{28,12},{1,9},{5... | collective-permute-start | bytes 884744 | tf_op jit(solution)/shard_map/ppermute | solution.py:29
  27.4 5.2 %collective-permute-done.5 = bf16[288,512]{1,0:T(8,128)(2,1)S(1)} collective-permute-done((bf16[288,512]{1,0:T(8,128)(2,1)S(1)}, bf16[288,512]{1,0:T(8,128)(2,1)S(1)}, u32[]{:S(2)}, u32[]{:S(2)}) %collective-permute-start.5) | collective-permute-done | bytes 294944 | tf_op jit(solution)/shard_map/ppermute | solution.py:29
  32.7 0.1 slice.64
  32.7 0.2 fusion.13
  32.9 0.1 dynamic-slice_select_fusion.1
  33.0 0.6 collective-permute-start.6
  33.6 6.2 %collective-permute-done.6 = f32[144,512]{1,0:T(8,128)S(1)} collective-permute-done((f32[144,512]{1,0:T(8,128)S(1)}, f32[144,512]{1,0:T(8,128)S(1)}, u32[]{:S(2)}, u32[]{:S(2)}) %collective-permute-start.6) | collective-permute-done | bytes 294944 | tf_op jit(solution)/shard_map/ppermute | solution.py:29
  39.9 1.6 %collective-permute-start.7 = (f32[80,512]{1,0:T(8,128)S(1)}, f32[80,512]{1,0:T(8,128)S(1)}, u32[]{:S(2)}, u32[]{:S(2)}) collective-permute-start(f32[80,512]{1,0:T(8,128)S(1)} %pad_maximum_fusion.7), channel_id=1, source_target_pairs={{0,1},{1,0},{2,3},{3,2},{4,5},{5,4},{6,7},{7,6},{8,9},{9,8},{10,11... | collective-permute-start | bytes 491528 | tf_op jit(solution)/shard_map/ppermute | solution.py:29
  41.6 3.7 %collective-permute-done.7 = f32[80,512]{1,0:T(8,128)S(1)} collective-permute-done((f32[80,512]{1,0:T(8,128)S(1)}, f32[80,512]{1,0:T(8,128)S(1)}, u32[]{:S(2)}, u32[]{:S(2)}) %collective-permute-start.7) | collective-permute-done | bytes 163872 | tf_op jit(solution)/shard_map/ppermute | solution.py:29
  45.4 2.7 %collective-permute-start.8 = (f32[48,512]{1,0:T(8,128)S(1)}, f32[48,512]{1,0:T(8,128)S(1)}, u32[]{:S(2)}, u32[]{:S(2)}) collective-permute-start(f32[48,512]{1,0:T(8,128)S(1)} %pad_maximum_fusion.9), channel_id=1, source_target_pairs={{0,2},{1,3},{2,0},{3,1},{4,6},{5,7},{6,4},{7,5},{8,10},{9,11},{10,... | collective-permute-start | bytes 294920 | tf_op jit(solution)/shard_map/ppermute | solution.py:29
  48.1 2.9 %collective-permute-done.8 = f32[48,512]{1,0:T(8,128)S(1)} collective-permute-done((f32[48,512]{1,0:T(8,128)S(1)}, f32[48,512]{1,0:T(8,128)S(1)}, u32[]{:S(2)}, u32[]{:S(2)}) %collective-permute-start.8) | collective-permute-done | bytes 98336 | tf_op jit(solution)/shard_map/ppermute | solution.py:29
  51.0 0.6 collective-permute-start.9
  51.6 4.1 %collective-permute-done.9 = f32[32,512]{1,0:T(8,128)S(1)} collective-permute-done((f32[32,512]{1,0:T(8,128)S(1)}, f32[32,512]{1,0:T(8,128)S(1)}, u32[]{:S(2)}, u32[]{:S(2)}) %collective-permute-start.9) | collective-permute-done | bytes 65568 | tf_op jit(solution)/shard_map/ppermute | solution.py:99
  55.7 1.6 %collective-permute-start.10 = (f32[2,32,512]{2,1,0:T(8,128)S(1)}, f32[2,32,512]{2,1,0:T(8,128)S(1)}, u32[]{:S(2)}, u32[]{:S(2)}) collective-permute-start(f32[2,32,512]{2,1,0:T(8,128)S(1)} %pad_maximum_fusion.8), channel_id=1, source_target_pairs={{0,8},{4,20},{8,0},{12,28},{16,24},{20,4},{24,16},{28,12},{1,9},{5... | collective-permute-start | bytes 393224 | tf_op jit(solution)/shard_map/ppermute | solution.py:99
  57.3 3.4 %collective-permute-done.10 = f32[2,32,512]{2,1,0:T(8,128)S(1)} collective-permute-done((f32[2,32,512]{2,1,0:T(8,128)S(1)}, f32[2,32,512]{2,1,0:T(8,128)S(1)}, u32[]{:S(2)}, u32[]{:S(2)}) %collective-permute-start.10) | collective-permute-done | bytes 131104 | tf_op jit(solution)/shard_map/ppermute | solution.py:99
  60.8 0.1 collective-permute-start.11
  60.9 1.5 %collective-permute-done.11 = f32[136,512]{1,0:T(8,128)S(1)} collective-permute-done((f32[136,512]{1,0:T(8,128)S(1)}, f32[136,512]{1,0:T(8,128)S(1)}, u32[]{:S(2)}, u32[]{:S(2)}) %collective-permute-start.11) | collective-permute-done | bytes 278560 | tf_op jit(solution)/shard_map/ppermute | solution.py:29
  62.5 0.1 select_bitcast_fusion.1
  62.6 0.8 %copy.40 = f32[2,2,2,32,512]{4,3,2,1,0:T(8,128)} copy(f32[2,2,2,32,512]{4,3,0,1,2:T(8,128)S(1)} %maximum_bitcast_fusion) | data formatting | bytes 1048576 | tf_op jit(solution)/shard_map/transpose | solution.py:110
  63.4 0.6 slice_add_fusion.2
  (40 shorter events, 0.7 us)
Async XLA Ops:
  0.6 10.2 %copy-start.4 = (bf16[8,512]{1,0:T(8,128)(2,1)S(1)}, bf16[8,512]{1,0:T(8,128)(2,1)}, u32[]{:S(2)}) copy-start(bf16[8,512]{1,0:T(8,128)(2,1)} %param.8) | copy-start | bytes 24580
  0.6 14.2 %copy-start.1 = (bf16[512,512]{1,0:T(8,128)(2,1)S(1)}, bf16[512,512]{1,0:T(8,128)(2,1)}, u32[]{:S(2)}) copy-start(bf16[512,512]{1,0:T(8,128)(2,1)} %param.7) | copy-start | bytes 1572868
  0.7 11.8 %copy-start = (s32[16,128,128]{2,1,0:T(8,128)S(1)}, s32[16,128,128]{2,1,0:T(8,128)}, u32[]{:S(2)}) copy-start(s32[16,128,128]{2,1,0:T(8,128)} %param.11) | copy-start | bytes 3145732
  0.7 11.8 %copy-start.3 = (s32[512,4]{0,1:T(4,128)S(1)}, s32[512,4]{0,1:T(4,128)}, u32[]{:S(2)}) copy-start(s32[512,4]{0,1:T(4,128)} %param.9) | copy-start | bytes 24580
  0.7 10.2 %collective-permute-start.1 = (bf16[8,512]{1,0:T(8,128)(2,1)}, bf16[8,512]{1,0:T(8,128)(2,1)S(1)}, u32[]{:S(2)}, u32[]{:S(2)}) collective-permute-start(bf16[8,512]{1,0:T(8,128)(2,1)} %param.8), channel_id=1, source_target_pairs={{0,16},{4,20},{8,24},{12,28},{16,0},{20,4},{24,8},{28,12},{1,17},{... | collective-permute-start | bytes 24584 | tf_op jit(solution)/shard_map/ppermute | solution.py:99
  4.6 12.5 %collective-permute-start = (bf16[128,512]{1,0:T(8,128)(2,1)S(1)}, bf16[128,512]{1,0:T(8,128)(2,1)S(1)}, u32[]{:S(2)}, u32[]{:S(2)}) collective-permute-start(bf16[128,512]{1,0:T(8,128)(2,1)S(1)} %slice.48), channel_id=1, source_target_pairs={{0,1},{1,2},{2,3},{4,5},{5,6},{6,7},{8,9},{9,10},{10,11},{12,13},{... | collective-permute-start | bytes 393224 | tf_op jit(solution)/shard_map/ppermute | solution.py:10
  10.9 3.8 %collective-permute-start.2 = (bf16[2,8,512]{2,1,0:T(8,128)(2,1)S(1)}, bf16[2,8,512]{2,1,0:T(8,128)(2,1)S(1)}, u32[]{:S(2)}, u32[]{:S(2)}) collective-permute-start(bf16[2,8,512]{2,1,0:T(8,128)(2,1)S(1)} %pad_maximum_fusion.12), channel_id=1, source_target_pairs={{0,8},{4,12},{8,0},{12,4},{16,24},{20,28},{24,16},{28,20},{1,9},{5... | collective-permute-start | bytes 49160 | tf_op jit(solution)/shard_map/ppermute | solution.py:99
  14.7 1.4 %collective-permute-start.3 = (bf16[2,2,8,512]{3,2,0,1:T(8,128)(2,1)S(1)}, bf16[2,2,8,512]{3,2,0,1:T(8,128)(2,1)S(1)}, u32[]{:S(2)}, u32[]{:S(2)}) collective-permute-start(bf16[2,2,8,512]{3,2,0,1:T(8,128)(2,1)S(1)} %pad_maximum_fusion.11), channel_id=1, source_target_pairs={{0,4},{4,0},{8,12},{12,8},{16,20},{20,16},{24,28},{28,24},{1,5},{5... | collective-permute-start | bytes 98312 | tf_op jit(solution)/shard_map/ppermute | solution.py:99
  17.1 1.2 %copy-start.5 = (bf16[1024,512]{1,0:T(8,128)(2,1)S(1)}, bf16[1024,512]{1,0:T(8,128)(2,1)}, u32[]{:S(2)}) copy-start(bf16[1024,512]{1,0:T(8,128)(2,1)} %param.12) | copy-start | bytes 3145732
  17.1 1.3 %copy-start.6 = (bf16[512,512]{1,0:T(8,128)(2,1)S(1)}, bf16[512,512]{1,0:T(8,128)(2,1)}, u32[]{:S(2)}) copy-start(bf16[512,512]{1,0:T(8,128)(2,1)} %param.13) | copy-start | bytes 1572868
  20.4 0.8 %copy-start.2 = (bf16[512,512]{1,0:T(8,128)(2,1)}, bf16[512,512]{1,0:T(8,128)(2,1)S(1)}, u32[]{:S(2)}) copy-start(bf16[512,512]{1,0:T(8,128)(2,1)S(1)} %get-tuple-element.3) | copy-start | bytes 1572868
  21.2 3.0 %collective-permute-start.4 = (f32[512,512]{1,0:T(8,128)S(1)}, f32[512,512]{1,0:T(8,128)}, u32[]{:S(2)}, u32[]{:S(2)}) collective-permute-start(f32[512,512]{1,0:T(8,128)S(1)} %bitcast.132), channel_id=1, source_target_pairs={{0,4},{4,0},{8,12},{12,8},{16,20},{20,16},{24,28},{28,24},{1,5},{5... | collective-permute-start | bytes 3145736 | tf_op jit(solution)/shard_map/ppermute | solution.py:29
  25.8 6.8 %collective-permute-start.5 = (bf16[288,512]{1,0:T(8,128)(2,1)S(1)}, bf16[288,512]{1,0:T(8,128)(2,1)S(1)}, u32[]{:S(2)}, u32[]{:S(2)}) collective-permute-start(bf16[288,512]{1,0:T(8,128)(2,1)S(1)} %pad_maximum_fusion.3), channel_id=1, source_target_pairs={{0,8},{4,20},{8,0},{12,28},{16,24},{20,4},{24,16},{28,12},{1,9},{5... | collective-permute-start | bytes 884744 | tf_op jit(solution)/shard_map/ppermute | solution.py:29
  33.0 6.8 %collective-permute-start.6 = (f32[144,512]{1,0:T(8,128)S(1)}, f32[144,512]{1,0:T(8,128)S(1)}, u32[]{:S(2)}, u32[]{:S(2)}) collective-permute-start(f32[144,512]{1,0:T(8,128)S(1)} %pad_maximum_fusion.4), channel_id=1, source_target_pairs={{0,16},{4,12},{8,24},{12,4},{16,0},{20,28},{24,8},{28,20},{1,17},{... | collective-permute-start | bytes 884744 | tf_op jit(solution)/shard_map/ppermute | solution.py:29
  39.9 5.4 %collective-permute-start.7 = (f32[80,512]{1,0:T(8,128)S(1)}, f32[80,512]{1,0:T(8,128)S(1)}, u32[]{:S(2)}, u32[]{:S(2)}) collective-permute-start(f32[80,512]{1,0:T(8,128)S(1)} %pad_maximum_fusion.7), channel_id=1, source_target_pairs={{0,1},{1,0},{2,3},{3,2},{4,5},{5,4},{6,7},{7,6},{8,9},{9,8},{10,11... | collective-permute-start | bytes 491528 | tf_op jit(solution)/shard_map/ppermute | solution.py:29
  45.4 5.6 %collective-permute-start.8 = (f32[48,512]{1,0:T(8,128)S(1)}, f32[48,512]{1,0:T(8,128)S(1)}, u32[]{:S(2)}, u32[]{:S(2)}) collective-permute-start(f32[48,512]{1,0:T(8,128)S(1)} %pad_maximum_fusion.9), channel_id=1, source_target_pairs={{0,2},{1,3},{2,0},{3,1},{4,6},{5,7},{6,4},{7,5},{8,10},{9,11},{10,... | collective-permute-start | bytes 294920 | tf_op jit(solution)/shard_map/ppermute | solution.py:29
  51.0 4.6 %collective-permute-start.9 = (f32[32,512]{1,0:T(8,128)S(1)}, f32[32,512]{1,0:T(8,128)S(1)}, u32[]{:S(2)}, u32[]{:S(2)}) collective-permute-start(f32[32,512]{1,0:T(8,128)S(1)} %slice_add_fusion), channel_id=1, source_target_pairs={{0,16},{4,12},{8,24},{12,4},{16,0},{20,28},{24,8},{28,20},{1,17},{... | collective-permute-start | bytes 196616 | tf_op jit(solution)/shard_map/ppermute | solution.py:99
  55.7 5.0 %collective-permute-start.10 = (f32[2,32,512]{2,1,0:T(8,128)S(1)}, f32[2,32,512]{2,1,0:T(8,128)S(1)}, u32[]{:S(2)}, u32[]{:S(2)}) collective-permute-start(f32[2,32,512]{2,1,0:T(8,128)S(1)} %pad_maximum_fusion.8), channel_id=1, source_target_pairs={{0,8},{4,20},{8,0},{12,28},{16,24},{20,4},{24,16},{28,12},{1,9},{5... | collective-permute-start | bytes 393224 | tf_op jit(solution)/shard_map/ppermute | solution.py:99
  60.8 1.6 %collective-permute-start.11 = (f32[136,512]{1,0:T(8,128)S(1)}, f32[136,512]{1,0:T(8,128)S(1)}, u32[]{:S(2)}, u32[]{:S(2)}) collective-permute-start(f32[136,512]{1,0:T(8,128)S(1)} %pad_maximum_fusion.5), channel_id=1, source_target_pairs={{0,4},{4,0},{8,12},{12,8},{16,20},{20,16},{24,28},{28,24},{1,5},{5... | collective-permute-start | bytes 835592 | tf_op jit(solution)/shard_map/ppermute | solution.py:29
